TPU v7x, 32 devices: a whole 2x2x4 slice. The times are simulated.
32 devices in a mesh: grp: 4 (over y, x), patch: 8 (over z, core).
Axes of the slice: x: 2, y: 2, z: 4, core: 2. Of those that a mesh axis runs over, the one named last changes fastest.
Arguments:
- state: float32 [9, 60, 65536], P(None, 'grp', 'patch'), may hold values from -6 to 6
- courant_x: float32 [60, 65536], P('grp', 'patch'), may hold values from -0.45 to 0.45
- courant_y: float32 [60, 65536], P('grp', 'patch'), may hold values from -0.45 to 0.45
- surface: bfloat16 [16, 65536], P('grp', 'patch'), may hold values from -6 to 6
- w_in: bfloat16 [556, 256], replicated, may hold values from -0.25 to 0.25
- b_hidden: float32 [4, 256], replicated, may hold values from -3 to 3
- w_mid: bfloat16 [3, 256, 256], replicated, may hold values from -0.375 to 0.375
- w_out: bfloat16 [256, 540], replicated, may hold values from -0.375 to 0.375
- owner_map: int32 [512, 1], replicated, may hold values from 0 to 7; in each aligned block of 16 rows (0 to 15, 16 to 31, ...) at most 4 rows name the same one
- neighbours: int32 [8, 4], replicated, may hold values from 0 to 7, as said below
Outputs:
- new_state: float32 [9, 60, 65536], P(None, 'grp', 'patch')
- owner_heating: float32 [128, 1024], P('grp', 'patch')
Inputs may be any that keep to these rules, and one draw needn't show every extreme that they name: owner_map[b, 0] is the owner of block b (row b % 64 of patch b // 64); within each aligned run of 16 blocks no owner is named more than 4 times, and in some run one owner exactly 4 times. The patches tile a periodic arrangement of 2 by 4: neighbours[p, 0] and neighbours[p, 1] precede and follow p along the first direction, neighbours[p, 2] and neighbours[p, 3] along the second; neighbours[neighbours[p, 0], 1] = p, neighbours[neighbours[p, 2], 3] = p, and neighbours[neighbours[p, 0], 2] = neighbours[neighbours[p, 2], 0].
All inputs are finite; a program needn't handle non-finite values.
Results may differ from a plain program's by a relative error of at most 0.0059.
The roundings to bfloat16 on the way count: a program that leaves them out, or rounds other values in their place, can miss the bound.
Values may be sent and summed in bfloat16 or wider, within the bound.
No kernel may reach another device: no remote copies, remote signals or barrier semaphores. Data moves between devices by JAX's collectives and lax.ppermute only.
A program may use at most 640 MiB of HBM per device.

v0:
```python
import functools

import jax
import jax.numpy as jnp
from jax import lax
from jax.experimental import pallas as pl
from jax.experimental.pallas import tpu as pltpu
from jax.sharding import PartitionSpec as P

VARS = 9
LEV = 60
SURF = 16
SUBSTEPS = 3
PY = 128
PX = 64


KAPPA = 0.24
PHYS_DT = 0.05
HEAT_WEIGHT = 0.125


def stencil_kernel(*refs, with_tend):
    if with_tend:
        st_ref, cx_ref, cy_ref, halo_ref, tend_ref, out_ref, edge_ref = refs
    else:
        st_ref, cx_ref, cy_ref, halo_ref, out_ref, edge_ref = refs
    rows = st_ref.shape[2] // PY
    halo = halo_ref[0].astype(jnp.float32)
    north = halo[:, 0:PY]
    south = halo[:, PY : 2 * PY]
    sides = halo[:, 2 * PY : 3 * PY]
    lane = lax.broadcasted_iota(jnp.int32, north.shape, 1)
    cols = jnp.zeros_like(north)
    for x in range(rows):
        here = slice(x * PY, (x + 1) * PY)
        cur = st_ref[0, :, here]
        up = north if x == 0 else st_ref[0, :, (x - 1) * PY : x * PY]
        down = south if x == rows - 1 else st_ref[0, :, (x + 1) * PY : (x + 2) * PY]
        west = jnp.where(lane == 0, pltpu.roll(sides, (PY - x) % PY, 1), pltpu.roll(cur, 1, 1))
        east = jnp.where(
            lane == PY - 1, pltpu.roll(sides, (PY - 1 - rows - x) % PY, 1), pltpu.roll(cur, PY - 1, 1)
        )
        along_x = cx_ref[:, here]
        along_y = cy_ref[:, here]
        val = (
            cur
            - 0.5 * along_x * (down - up)
            - 0.5 * along_y * (east - west)
            + KAPPA * (up + down + west + east - 4.0 * cur)
        )
        if with_tend:
            val = val + PHYS_DT * tend_ref[x, 0].astype(jnp.float32)
        out_ref[0, :, here] = val
        if x == 0:
            edge_ref[0, :, 0:PY] = val
        if x == rows - 1:
            edge_ref[0, :, PY : 2 * PY] = val
        cols = jnp.where(lane == x, pltpu.roll(val, x % PY, 1), cols)
        cols = jnp.where(lane == rows + x, pltpu.roll(val, (rows + x - PY + 1) % PY, 1), cols)
    edge_ref[0, :, 2 * PY : 3 * PY] = cols


def stencil(tracer, along_x, along_y, halo, tend):
    n_vars, levels, width = tracer.shape
    with_tend = tend is not None
    in_specs = [
        pl.BlockSpec((1, levels, width), lambda v: (v, 0, 0)),
        pl.BlockSpec((levels, width), lambda v: (0, 0)),
        pl.BlockSpec((levels, width), lambda v: (0, 0)),
        pl.BlockSpec((1, levels, 3 * PY), lambda v: (v, 0, 0)),
    ]
    args = [tracer, along_x, along_y, halo]
    if with_tend:
        in_specs.append(pl.BlockSpec((tend.shape[0], 1, levels, PY), lambda v: (0, v, 0, 0)))
        args.append(tend)
    return pl.pallas_call(
        functools.partial(stencil_kernel, with_tend=with_tend),
        grid=(n_vars,),
        in_specs=in_specs,
        out_specs=[
            pl.BlockSpec((1, levels, width), lambda v: (v, 0, 0)),
            pl.BlockSpec((1, levels, 3 * PY), lambda v: (v, 0, 0)),
        ],
        out_shape=[
            jax.ShapeDtypeStruct(tracer.shape, jnp.float32),
            jax.ShapeDtypeStruct((n_vars, levels, 3 * PY), jnp.float32),
        ],
        cost_estimate=pl.CostEstimate(
            flops=20 * tracer.size, transcendentals=0, bytes_accessed=4 * (2 * tracer.size + 2 * along_x.size)
        ),
    )(*args)


def first_edges(tracer):
    width = tracer.shape[-1]
    return jnp.concatenate(
        [tracer[..., 0:PY], tracer[..., width - PY :], tracer[..., 0::PY], tracer[..., PY - 1 :: PY]],
        axis=-1,
    )


def exchange_halo(edges, beside_all, patches):
    payload = edges.astype(jnp.bfloat16)
    sent = jnp.broadcast_to(payload[None], (patches,) + payload.shape)
    got = lax.all_to_all(sent, "patch", split_axis=0, concat_axis=0, tiled=True)
    rows = PX
    north = jnp.take(got, beside_all[0], axis=0)[..., PY : 2 * PY]
    south = jnp.take(got, beside_all[1], axis=0)[..., 0:PY]
    west = jnp.take(got, beside_all[2], axis=0)[..., 2 * PY + rows : 3 * PY]
    east = jnp.take(got, beside_all[3], axis=0)[..., 2 * PY : 2 * PY + rows]
    return jnp.concatenate([north, south, west, east], axis=-1)


def activate(pre_act):
    return jax.nn.silu(pre_act).astype(jnp.bfloat16)


def hidden_layers(hidden, b_hidden, w_mid):
    for layer_index in range(w_mid.shape[0]):
        pre_act = (
            jnp.einsum(
                "...h,hj->...j", hidden, w_mid[layer_index], preferred_element_type=jnp.float32
            )
            + b_hidden[layer_index + 1]
        )
        hidden = activate(pre_act)
    return hidden


def on_device(
    state, courant_x, courant_y, surface, w_in, b_hidden, w_mid, w_out, owner_map, neighbours
):
    groups = lax.axis_size("grp")
    patches = lax.axis_size("patch")
    group_here = lax.axis_index("grp")
    patch_here = lax.axis_index("patch")
    level_share = LEV // groups
    surf_share = SURF // groups
    feat_share = VARS * level_share + surf_share
    quarter_rows = PX // groups
    capacity = max(2, 2 * quarter_rows // patches)
    slot_count = patches * capacity
    tracer = state.reshape(VARS, level_share, PX, PY)
    beside_all = jnp.take(neighbours, patch_here, axis=0)
    features = jnp.concatenate(
        [
            tracer.astype(jnp.bfloat16).reshape(VARS * level_share, PX, PY),
            surface.reshape(surf_share, PX, PY),
        ],
        axis=0,
    )
    by_quarter = features.reshape(feat_share, groups, quarter_rows, PY).transpose(1, 2, 0, 3)
    owners_all = owner_map.reshape(patches, groups, quarter_rows)
    owners_here = jnp.take(owners_all, patch_here, axis=0)
    matches = (owners_here[..., None] == jnp.arange(patches, dtype=jnp.int32)).astype(jnp.int32)
    slot_rank = jnp.sum((jnp.cumsum(matches, axis=1) - matches) * matches, axis=2)
    slot_index = owners_here * capacity + slot_rank
    selector = (
        slot_index[:, None, :] == jnp.arange(slot_count, dtype=jnp.int32)[None, :, None]
    ).astype(jnp.bfloat16)
    selector_here = jnp.take(selector, group_here, axis=0)
    state_part = (
        w_in[: VARS * LEV]
        .reshape(VARS, groups, level_share, -1)
        .transpose(1, 0, 2, 3)
        .reshape(groups, VARS * level_share, -1)
    )
    w_local = jnp.concatenate(
        [state_part, w_in[VARS * LEV :].reshape(groups, surf_share, -1)], axis=1
    )
    w_split = w_out.reshape(-1, VARS, groups, level_share)
    regrouped = lax.all_to_all(by_quarter, "grp", split_axis=0, concat_axis=0, tiled=True)
    pre_act = (
        jnp.einsum("gbfc,gfh->bch", regrouped, w_local, preferred_element_type=jnp.float32)
        + b_hidden[0]
    )
    hidden = hidden_layers(activate(pre_act), b_hidden, w_mid)
    tendency = jnp.einsum(
        "bch,hvgl->bvglc", hidden, w_split, preferred_element_type=jnp.float32
    ).astype(jnp.bfloat16)
    heating = HEAT_WEIGHT * jnp.sum(tendency[:, 0].astype(jnp.float32), axis=(1, 2))
    packed = jnp.dot(
        selector_here.astype(jnp.float32), heating, precision=lax.Precision.HIGHEST
    ).reshape(patches, capacity, PY)
    owner_heating = lax.all_to_all(
        packed, "patch", split_axis=0, concat_axis=0, tiled=True
    ).reshape(slot_count, PY)
    arrived = lax.all_to_all(tendency, "grp", split_axis=2, concat_axis=0, tiled=True)
    tendency_here = arrived.reshape(PX, VARS, level_share, PY)
    advected = state
    edges = first_edges(state)
    for section_index in range(SUBSTEPS):
        halo = exchange_halo(edges, beside_all, patches)
        last = section_index == SUBSTEPS - 1
        advected, edges = stencil(
            advected, courant_x, courant_y, halo, tendency_here if last else None
        )
    new_state = advected
    return (new_state, owner_heating)


def solution(mesh):
    placed = (
        P(None, "grp", "patch"),
        P("grp", "patch"),
        P("grp", "patch"),
        P("grp", "patch"),
        P(),
        P(),
        P(),
        P(),
        P(),
        P(),
    )
    return jax.shard_map(
        on_device,
        mesh=mesh,
        in_specs=placed,
        out_specs=(P(None, "grp", "patch"), P("grp", "patch")),
        check_vma=False,
    )
```

profile of v0, /device:TPU:0, one launch (start us, length us, event | category | flops | bytes accessed | tf_op | source)
XLA Modules:
  0.0 268.3 jit_solution(3025336093339002502)
XLA Ops:
  0.6 2.6 convert.10
  3.3 1.2 slice.105
  4.4 1.2 slice.104
  5.7 1.0 broadcast_in_dim.61
  6.7 6.4 %all-to-all-start = ((bf16[8,9,15,384]{3,2,1,0:T(8,128)(2,1)}), bf16[8,9,15,384]{3,2,1,0:T(8,128)(2,1)S(1)}, u32[]{:S(2)}, u32[]{:S(2)}) async-start(bf16[8,9,15,384]{3,2,1,0:T(8,128)(2,1)} %broadcast_in_dim.61), calls=%async_computation | async-start | bytes 1769472 | tf_op jit(solution)/shard_map/all_to_all | solution.py:106
  13.1 3.1 %convert_element_type.48 = bf16[135,4,16,128]{3,2,1,0:T(8,128)(2,1)} reshape(bf16[9,15,8192]{2,1,0:T(8,128)(2,1)S(1)} %convert.10) | data formatting | bytes 4423680 | tf_op jit(solution)/shard_map/convert_element_type | solution.py:148
  16.2 1.8 maximum_bitcast_fusion
  18.0 1.8 copy.19
  19.8 16.3 %all-to-all-done = bf16[8,9,15,384]{3,2,1,0:T(8,128)(2,1)S(1)} async-done(((bf16[8,9,15,384]{3,2,1,0:T(8,128)(2,1)}), bf16[8,9,15,384]{3,2,1,0:T(8,128)(2,1)S(1)}, u32[]{:S(2)}, u32[]{:S(2)}) %all-to-all-start) | async-done | bytes 829472 | tf_op jit(solution)/shard_map/all_to_all | solution.py:106
  36.1 3.7 %all-to-all-start.3 = ((bf16[4,16,139,128]{3,1,2,0:T(8,128)(2,1)}), bf16[4,16,139,128]{3,1,2,0:T(8,128)(2,1)S(1)}, u32[]{:S(2)}, u32[]{:S(2)}) async-start(bf16[4,16,139,128]{3,1,2,0:T(8,128)(2,1)} %copy.19), calls=%async_computation.3 | async-start | bytes 4554752 | tf_op jit(solution)/shard_map/all_to_all | solution.py:173
  50.2 1.1 reshape.88
  52.2 1.0 reshape.386
  54.2 12.3 %all-to-all-done.3 = bf16[4,16,139,128]{3,1,2,0:T(8,128)(2,1)S(1)} async-done(((bf16[4,16,139,128]{3,1,2,0:T(8,128)(2,1)}), bf16[4,16,139,128]{3,1,2,0:T(8,128)(2,1)S(1)}, u32[]{:S(2)}, u32[]{:S(2)}) %all-to-all-start.3) | async-done | bytes 2277408 | tf_op jit(solution)/shard_map/all_to_all | solution.py:173
  66.5 4.1 %multiply_convert_fusion.2 = bf16[16,128,256]{2,1,0:T(8,128)(2,1)} fusion(f32[256]{0:T(256)S(1)} %bitcast.99, bf16[4,16,139,128]{3,1,2,0:T(8,128)(2,1)S(1)} %all-to-all-done.3, f32[256]{0:T(256)S(1)} %bitcast.100, bf16[4,4,256]{2,1,0:T(4,128)(2,1)S(1)} %reshape.90, bf16[4,135,256]{2,1,0:T(8,128)(2,1)} %copy.21, bf16[3,256,256]{2,1,0:T(8,128)(2,1)} %param.18), kind=kOutput, calls=%fused_computation.7 | convolution fusion | flops 858304512 | bytes 3745792 | tf_op jit(solution)/shard_map/...h,hj->...j/dot_general | solution.py:122
  70.6 2.9 %multiply_convert_fusion.1 = bf16[16,128,256]{2,1,0:T(8,128)(2,1)} fusion(bf16[16,128,256]{2,1,0:T(8,128)(2,1)} %multiply_convert_fusion.2, f32[256]{0:T(256)S(1)} %bitcast.98, bf16[3,256,256]{2,1,0:T(8,128)(2,1)S(1)} %copy-done.6), kind=kOutput, calls=%fused_computation.6 | convolution fusion | flops 271581184 | bytes 2229248 | tf_op jit(solution)/shard_map/...h,hj->...j/dot_general | solution.py:122
  73.5 2.5 convert_bitcast_fusion
  76.0 0.7 fusion.25
  76.8 3.3 %all-to-all-start.5 = ((f32[8,4,128]{2,1,0:T(4,128)}), f32[8,4,128]{2,1,0:T(4,128)S(1)}, u32[]{:S(2)}, u32[]{:S(2)}) async-start(f32[8,4,128]{2,1,0:T(4,128)} %bitcast.40), calls=%async_computation.5 | async-start | bytes 32768 | tf_op jit(solution)/shard_map/all_to_all | solution.py:186
  80.8 40.8 %shard_map.113 = (f32[9,15,8192]{2,1,0:T(8,128)}, f32[9,15,384]{2,1,0:T(8,128)}) custom-call(f32[9,15,8192]{2,1,0:T(8,128)} %refs_0_.1, f32[15,8192]{1,0:T(8,128)} %refs_1_.5, f32[15,8192]{1,0:T(8,128)} %refs_2_.5, bf16[9,15,384]{2,1,0:T(8,128)(2,1)} %pad_maximum_fusion.1.refs_3_), custom_call_target="tpu_custom_call" | custom-call | flops 22118400 | bytes 9830400 | tf_op jit(solution)/shard_map/pallas_call | solution.py:77
  121.6 1.0 convert_element_type.46
  122.6 1.0 broadcast_in_dim.64
  123.6 5.0 %all-to-all-start.1 = ((bf16[8,9,15,384]{3,2,1,0:T(8,128)(2,1)}), bf16[8,9,15,384]{3,2,1,0:T(8,128)(2,1)S(1)}, u32[]{:S(2)}, u32[]{:S(2)}) async-start(bf16[8,9,15,384]{3,2,1,0:T(8,128)(2,1)} %broadcast_in_dim.64), calls=%async_computation.1 | async-start | bytes 1769472 | tf_op jit(solution)/shard_map/all_to_all | solution.py:106
  128.6 4.0 %copy.23 = bf16[16,9,4,15,128]{4,0,3,1,2:T(8,128)(2,1)} copy(bf16[16,9,4,15,128]{4,3,2,1,0:T(8,128)(2,1)S(1)} %convert_bitcast_fusion) | data formatting | bytes 4423680 | tf_op jit(solution)/shard_map/convert_element_type | solution.py:181
  132.6 19.1 %all-to-all-done.1 = bf16[8,9,15,384]{3,2,1,0:T(8,128)(2,1)S(1)} async-done(((bf16[8,9,15,384]{3,2,1,0:T(8,128)(2,1)}), bf16[8,9,15,384]{3,2,1,0:T(8,128)(2,1)S(1)}, u32[]{:S(2)}, u32[]{:S(2)}) %all-to-all-start.1) | async-done | bytes 829472 | tf_op jit(solution)/shard_map/all_to_all | solution.py:106
  151.7 3.6 %all-to-all-start.4 = ((bf16[16,9,4,15,128]{4,0,3,1,2:T(8,128)(2,1)}), bf16[16,9,4,15,128]{4,0,3,1,2:T(8,128)(2,1)S(1)}, u32[]{:S(2)}, u32[]{:S(2)}) async-start(bf16[16,9,4,15,128]{4,0,3,1,2:T(8,128)(2,1)} %copy.23), calls=%async_computation.4 | async-start | bytes 4423680 | tf_op jit(solution)/shard_map/all_to_all | solution.py:189
  156.2 40.8 %shard_map.114 = (f32[9,15,8192]{2,1,0:T(8,128)}, f32[9,15,384]{2,1,0:T(8,128)}) custom-call(f32[9,15,8192]{2,1,0:T(8,128)} %get-tuple-element.8.refs_0_, f32[15,8192]{1,0:T(8,128)} %refs_1_.5, f32[15,8192]{1,0:T(8,128)} %refs_2_.5, bf16[9,15,384]{2,1,0:T(8,128)(2,1)} %pad_maximum_fusion.2.refs_3_), custom_call_target="tpu_custom_call" | custom-call | flops 22118400 | bytes 9830400 | tf_op jit(solution)/shard_map/pallas_call | solution.py:77
  197.0 0.9 convert_element_type.47
  198.0 1.0 broadcast_in_dim.65
  199.0 3.6 %all-to-all-start.2 = ((bf16[8,9,15,384]{3,2,1,0:T(8,128)(2,1)}), bf16[8,9,15,384]{3,2,1,0:T(8,128)(2,1)S(1)}, u32[]{:S(2)}, u32[]{:S(2)}) async-start(bf16[8,9,15,384]{3,2,1,0:T(8,128)(2,1)} %broadcast_in_dim.65), calls=%async_computation.2 | async-start | bytes 1769472 | tf_op jit(solution)/shard_map/all_to_all | solution.py:106
  202.6 2.0 copy.24
  204.6 20.9 %all-to-all-done.2 = bf16[8,9,15,384]{3,2,1,0:T(8,128)(2,1)S(1)} async-done(((bf16[8,9,15,384]{3,2,1,0:T(8,128)(2,1)}), bf16[8,9,15,384]{3,2,1,0:T(8,128)(2,1)S(1)}, u32[]{:S(2)}, u32[]{:S(2)}) %all-to-all-start.2) | async-done | bytes 829472 | tf_op jit(solution)/shard_map/all_to_all | solution.py:106
  226.5 41.2 %shard_map.115 = (f32[9,15,8192]{2,1,0:T(8,128)}, f32[9,15,384]{2,1,0:T(8,128)}) custom-call(f32[9,15,8192]{2,1,0:T(8,128)} %get-tuple-element.10.refs_0_, f32[15,8192]{1,0:T(8,128)} %refs_1_.5, f32[15,8192]{1,0:T(8,128)} %refs_2_.5, bf16[9,15,384]{2,1,0:T(8,128)(2,1)} %pad_maximum_fusion.3.refs_3_, bf16[64,9,15,128]{3,2,1,0:T(8,128)(2,1)} %bitcast.90), custom_call_target="tpu_custom_call" | custom-call | flops 22118400 | bytes 9830400 | tf_op jit(solution)/shard_map/pallas_call | solution.py:77
  (56 shorter events, 8.0 us)
Async XLA Ops:
  6.7 29.4 %all-to-all-start = ((bf16[8,9,15,384]{3,2,1,0:T(8,128)(2,1)}), bf16[8,9,15,384]{3,2,1,0:T(8,128)(2,1)S(1)}, u32[]{:S(2)}, u32[]{:S(2)}) async-start(bf16[8,9,15,384]{3,2,1,0:T(8,128)(2,1)} %broadcast_in_dim.61), calls=%async_computation | async-start | bytes 1769472 | tf_op jit(solution)/shard_map/all_to_all | solution.py:106
  13.0 3.1 %copy-start.1 = (bf16[4,8192]{1,0:T(4,128)(2,1)S(1)}, bf16[4,8192]{1,0:T(4,128)(2,1)}, u32[]{:S(2)}) copy-start(bf16[4,8192]{1,0:T(4,128)(2,1)} %param.15) | copy-start | bytes 196612
  19.8 20.1 %copy-start.3 = (s32[8,4]{0,1:T(4,128)S(1)}, s32[8,4]{0,1:T(4,128)}, u32[]{:S(2)}) copy-start(s32[8,4]{0,1:T(4,128)} %param.21) | copy-start | bytes 388
  19.8 28.3 %copy-start = (bf16[556,256]{1,0:T(8,128)(2,1)S(1)}, bf16[556,256]{1,0:T(8,128)(2,1)}, u32[]{:S(2)}) copy-start(bf16[556,256]{1,0:T(8,128)(2,1)} %param.16) | copy-start | bytes 854020
  19.8 29.6 %copy-start.4 = (s32[512,1]{0,1:T(1,128)S(1)}, s32[512,1]{0,1:T(1,128)}, u32[]{:S(2)}) copy-start(s32[512,1]{0,1:T(1,128)} %param.20) | copy-start | bytes 6148
  36.1 30.4 %all-to-all-start.3 = ((bf16[4,16,139,128]{3,1,2,0:T(8,128)(2,1)}), bf16[4,16,139,128]{3,1,2,0:T(8,128)(2,1)S(1)}, u32[]{:S(2)}, u32[]{:S(2)}) async-start(bf16[4,16,139,128]{3,1,2,0:T(8,128)(2,1)} %copy.19), calls=%async_computation.3 | async-start | bytes 4554752 | tf_op jit(solution)/shard_map/all_to_all | solution.py:173
  39.8 14.2 %copy-start.2 = (f32[4,256]{1,0:T(4,128)S(1)}, f32[4,256]{1,0:T(4,128)}, u32[]{:S(2)}) copy-start(f32[4,256]{1,0:T(4,128)} %param.17) | copy-start | bytes 12292
  66.5 4.1 %copy-start.6 = (bf16[3,256,256]{2,1,0:T(8,128)(2,1)S(1)}, bf16[3,256,256]{2,1,0:T(8,128)(2,1)}, u32[]{:S(2)}) copy-start(bf16[3,256,256]{2,1,0:T(8,128)(2,1)} %param.18) | copy-start | bytes 1179652
  73.5 2.5 copy-start.5
  76.8 45.8 %all-to-all-start.5 = ((f32[8,4,128]{2,1,0:T(4,128)}), f32[8,4,128]{2,1,0:T(4,128)S(1)}, u32[]{:S(2)}, u32[]{:S(2)}) async-start(f32[8,4,128]{2,1,0:T(4,128)} %bitcast.40), calls=%async_computation.5 | async-start | bytes 32768 | tf_op jit(solution)/shard_map/all_to_all | solution.py:186
  123.6 28.1 %all-to-all-start.1 = ((bf16[8,9,15,384]{3,2,1,0:T(8,128)(2,1)}), bf16[8,9,15,384]{3,2,1,0:T(8,128)(2,1)S(1)}, u32[]{:S(2)}, u32[]{:S(2)}) async-start(bf16[8,9,15,384]{3,2,1,0:T(8,128)(2,1)} %broadcast_in_dim.64), calls=%async_computation.1 | async-start | bytes 1769472 | tf_op jit(solution)/shard_map/all_to_all | solution.py:106
  151.7 46.3 %all-to-all-start.4 = ((bf16[16,9,4,15,128]{4,0,3,1,2:T(8,128)(2,1)}), bf16[16,9,4,15,128]{4,0,3,1,2:T(8,128)(2,1)S(1)}, u32[]{:S(2)}, u32[]{:S(2)}) async-start(bf16[16,9,4,15,128]{4,0,3,1,2:T(8,128)(2,1)} %copy.23), calls=%async_computation.4 | async-start | bytes 4423680 | tf_op jit(solution)/shard_map/all_to_all | solution.py:189
  199.0 26.5 %all-to-all-start.2 = ((bf16[8,9,15,384]{3,2,1,0:T(8,128)(2,1)}), bf16[8,9,15,384]{3,2,1,0:T(8,128)(2,1)S(1)}, u32[]{:S(2)}, u32[]{:S(2)}) async-start(bf16[8,9,15,384]{3,2,1,0:T(8,128)(2,1)} %broadcast_in_dim.65), calls=%async_computation.2 | async-start | bytes 1769472 | tf_op jit(solution)/shard_map/all_to_all | solution.py:106
where the time goes:
time: 269 us; the launch traced here: 268 us
  Pallas kernels  123 us (46%)
  waiting for transfers between devices  68.7 us (26%)
  starting transfers between devices  25.6 us (10%)
  local copies, waits for them, and re-layouts  22.6 us (8%)
  matrix products  10.2 us (4%)
  other arithmetic  9.98 us (4%)
  between operations  8.48 us (3%)
    pallas_call x3, Pallas kernels, stencil(): pl.pallas_call(functools.partial(stencil_kernel, with_tend=with_tend), gr...  123 us
    all_to_all x3, waiting for transfers between devices, exchange_halo(): got = lax.all_to_all(sent, 'patch', split_axis=0, concat_axis=0, tiled=True)  56.4 us
    all_to_all x3, starting transfers between devices, exchange_halo(): got = lax.all_to_all(sent, 'patch', split_axis=0, concat_axis=0, tiled=True)  14.9 us
    all_to_all x1, waiting for transfers between devices, on_device(): lax.all_to_all(by_quarter, 'grp', split_axis=0, concat_axis=0, tiled=True)  12.3 us
    dot_general x2, matrix products, hidden_layers(): jnp.einsum('...h,hj->...j', hidden, w_mid[layer_index], preferred_element...  6.99 us
  transfers between devices with their start and end apart: 6, of which 4 were waited for; matrix products, arithmetic and copies ran while one was open for 9% of the time, Pallas kernels for 30%

commit v1 on v0

--- a/solution.py
+++ b/solution.py
@@ -22,25 +22,21 @@
 
 def stencil_kernel(*refs, with_tend):
     if with_tend:
-        st_ref, cx_ref, cy_ref, halo_ref, tend_ref, out_ref, edge_ref = refs
+        st_ref, cx_ref, cy_ref, rows_ref, sides_ref, tend_ref, out_ref = refs
     else:
-        st_ref, cx_ref, cy_ref, halo_ref, out_ref, edge_ref = refs
+        st_ref, cx_ref, cy_ref, rows_ref, sides_ref, out_ref = refs
     rows = st_ref.shape[2] // PY
-    halo = halo_ref[0].astype(jnp.float32)
-    north = halo[:, 0:PY]
-    south = halo[:, PY : 2 * PY]
-    sides = halo[:, 2 * PY : 3 * PY]
+    north = rows_ref[0, :, 0:PY]
+    south = rows_ref[0, :, PY : 2 * PY]
     lane = lax.broadcasted_iota(jnp.int32, north.shape, 1)
-    cols = jnp.zeros_like(north)
     for x in range(rows):
         here = slice(x * PY, (x + 1) * PY)
         cur = st_ref[0, :, here]
         up = north if x == 0 else st_ref[0, :, (x - 1) * PY : x * PY]
         down = south if x == rows - 1 else st_ref[0, :, (x + 1) * PY : (x + 2) * PY]
-        west = jnp.where(lane == 0, pltpu.roll(sides, (PY - x) % PY, 1), pltpu.roll(cur, 1, 1))
-        east = jnp.where(
-            lane == PY - 1, pltpu.roll(sides, (PY - 1 - rows - x) % PY, 1), pltpu.roll(cur, PY - 1, 1)
-        )
+        side = sides_ref[0, :, here]
+        west = jnp.where(lane == 0, side, pltpu.roll(cur, 1, 1))
+        east = jnp.where(lane == PY - 1, side, pltpu.roll(cur, PY - 1, 1))
         along_x = cx_ref[:, here]
         along_y = cy_ref[:, here]
         val = (
@@ -52,25 +48,19 @@
         if with_tend:
             val = val + PHYS_DT * tend_ref[x, 0].astype(jnp.float32)
         out_ref[0, :, here] = val
-        if x == 0:
-            edge_ref[0, :, 0:PY] = val
-        if x == rows - 1:
-            edge_ref[0, :, PY : 2 * PY] = val
-        cols = jnp.where(lane == x, pltpu.roll(val, x % PY, 1), cols)
-        cols = jnp.where(lane == rows + x, pltpu.roll(val, (rows + x - PY + 1) % PY, 1), cols)
-    edge_ref[0, :, 2 * PY : 3 * PY] = cols
-
-
-def stencil(tracer, along_x, along_y, halo, tend):
+
+
+def stencil(tracer, along_x, along_y, halo_rows, halo_sides, tend):
     n_vars, levels, width = tracer.shape
     with_tend = tend is not None
     in_specs = [
         pl.BlockSpec((1, levels, width), lambda v: (v, 0, 0)),
         pl.BlockSpec((levels, width), lambda v: (0, 0)),
         pl.BlockSpec((levels, width), lambda v: (0, 0)),
-        pl.BlockSpec((1, levels, 3 * PY), lambda v: (v, 0, 0)),
+        pl.BlockSpec((1, levels, 2 * PY), lambda v: (v, 0, 0)),
+        pl.BlockSpec((1, levels, width), lambda v: (v, 0, 0)),
     ]
-    args = [tracer, along_x, along_y, halo]
+    args = [tracer, along_x, along_y, halo_rows, halo_sides]
     if with_tend:
         in_specs.append(pl.BlockSpec((tend.shape[0], 1, levels, PY), lambda v: (0, v, 0, 0)))
         args.append(tend)
@@ -78,38 +68,37 @@
         functools.partial(stencil_kernel, with_tend=with_tend),
         grid=(n_vars,),
         in_specs=in_specs,
-        out_specs=[
-            pl.BlockSpec((1, levels, width), lambda v: (v, 0, 0)),
-            pl.BlockSpec((1, levels, 3 * PY), lambda v: (v, 0, 0)),
-        ],
-        out_shape=[
-            jax.ShapeDtypeStruct(tracer.shape, jnp.float32),
-            jax.ShapeDtypeStruct((n_vars, levels, 3 * PY), jnp.float32),
-        ],
+        out_specs=pl.BlockSpec((1, levels, width), lambda v: (v, 0, 0)),
+        out_shape=jax.ShapeDtypeStruct(tracer.shape, jnp.float32),
         cost_estimate=pl.CostEstimate(
-            flops=20 * tracer.size, transcendentals=0, bytes_accessed=4 * (2 * tracer.size + 2 * along_x.size)
+            flops=20 * tracer.size, transcendentals=0, bytes_accessed=4 * (3 * tracer.size + 2 * along_x.size)
         ),
     )(*args)
 
 
-def first_edges(tracer):
+def edges_of(tracer):
     width = tracer.shape[-1]
     return jnp.concatenate(
         [tracer[..., 0:PY], tracer[..., width - PY :], tracer[..., 0::PY], tracer[..., PY - 1 :: PY]],
         axis=-1,
-    )
-
-
-def exchange_halo(edges, beside_all, patches):
-    payload = edges.astype(jnp.bfloat16)
+    ).astype(jnp.bfloat16)
+
+
+def exchange_halo(tracer, beside_all, patches):
+    payload = edges_of(tracer)
     sent = jnp.broadcast_to(payload[None], (patches,) + payload.shape)
-    got = lax.all_to_all(sent, "patch", split_axis=0, concat_axis=0, tiled=True)
+    got = lax.all_to_all(sent, "patch", split_axis=0, concat_axis=0, tiled=True).astype(jnp.float32)
     rows = PX
     north = jnp.take(got, beside_all[0], axis=0)[..., PY : 2 * PY]
     south = jnp.take(got, beside_all[1], axis=0)[..., 0:PY]
-    west = jnp.take(got, beside_all[2], axis=0)[..., 2 * PY + rows : 3 * PY]
+    west = jnp.take(got, beside_all[2], axis=0)[..., 2 * PY + rows : 2 * PY + 2 * rows]
     east = jnp.take(got, beside_all[3], axis=0)[..., 2 * PY : 2 * PY + rows]
-    return jnp.concatenate([north, south, west, east], axis=-1)
+    width = tracer.shape[-1]
+    lane = lax.broadcasted_iota(jnp.int32, tracer.shape, 2) % PY
+    spread_w = jnp.broadcast_to(west[..., None], west.shape + (PY,)).reshape(tracer.shape)
+    spread_e = jnp.broadcast_to(east[..., None], east.shape + (PY,)).reshape(tracer.shape)
+    sides = jnp.where(lane == 0, spread_w, jnp.where(lane == PY - 1, spread_e, 0.0))
+    return jnp.concatenate([north, south], axis=-1), sides
 
 
 def activate(pre_act):
@@ -189,12 +178,11 @@
     arrived = lax.all_to_all(tendency, "grp", split_axis=2, concat_axis=0, tiled=True)
     tendency_here = arrived.reshape(PX, VARS, level_share, PY)
     advected = state
-    edges = first_edges(state)
     for section_index in range(SUBSTEPS):
-        halo = exchange_halo(edges, beside_all, patches)
+        halo_rows, halo_sides = exchange_halo(advected, beside_all, patches)
         last = section_index == SUBSTEPS - 1
-        advected, edges = stencil(
-            advected, courant_x, courant_y, halo, tendency_here if last else None
+        advected = stencil(
+            advected, courant_x, courant_y, halo_rows, halo_sides, tendency_here if last else None
         )
     new_state = advected
     return (new_state, owner_heating)

time: 269 us -> 231 us (0.86)
  Pallas kernels: 123 us -> 31.8 us
  local copies, waits for them, and re-layouts: 22.6 us -> 83.6 us
  waiting for transfers between devices: 68.7 us -> 33.7 us
  other arithmetic: 9.98 us -> 35.3 us
    pallas_call x3, Pallas kernels: 123 us -> 31.8 us  [stencil(): pl.pallas_call(functools.partial(stencil_kernel, with_tend=with_tend), gr...]
    reshape x0 -> x6, local copies, waits for them, and re-layouts: none -> 33.6 us  [the longest x3 16.9 us: exchange_halo(): jnp.broadcast_to(east[..., None], east.shape + (PY,)).reshape(tracer.shape)]
    all_to_all x3, waiting for transfers between devices: 56.4 us -> 33.7 us  [exchange_halo(): lax.all_to_all(sent, 'patch', split_axis=0, concat_axis=0, tiled=True)]
    select_n x3 -> x6, other arithmetic: 0.21 us -> 20.4 us  [the longest x3 20.2 us: exchange_halo(): jnp.where(lane == 0, spread_w, jnp.where(lane == PY - 1, spread_e, 0.0))]
    broadcast_in_dim x0 -> x6, local copies, waits for them, and re-layouts: none -> 19.1 us  [the longest x3 9.6 us: exchange_halo(): jnp.broadcast_to(east[..., None], east.shape + (PY,)).reshape(tracer.shape)]
    all_to_all x1, waiting for transfers between devices: 12.3 us -> 0.01 us  [on_device(): lax.all_to_all(by_quarter, 'grp', split_axis=0, concat_axis=0, tiled=True)]
    slice x6 -> x12, local copies, waits for them, and re-layouts: 2.57 us -> 11.5 us  [the longest x3 5.22 us: edges_of(): tracer[..., PY - 1::PY]]
    another operation x1 -> x3, other arithmetic: 2.62 us -> 9.27 us
  transfers between devices with their start and end apart: 6 -> 6, of which waited for: 4 -> 3; matrix products, arithmetic and copies ran while one was open for 9% -> 41% of each run, Pallas kernels for 30% -> 9%
where the time goes in v1:
time: 231 us; the launch traced here: 229 us
  local copies, waits for them, and re-layouts  83.6 us (36%)
  other arithmetic  35.3 us (15%)
  waiting for transfers between devices  33.7 us (15%)
  Pallas kernels  31.8 us (14%)
  starting transfers between devices  27.1 us (12%)
  matrix products  8.7 us (4%)
  between operations  8.67 us (4%)
    all_to_all x3, waiting for transfers between devices, exchange_halo(): lax.all_to_all(sent, 'patch', split_axis=0, concat_axis=0, tiled=True)  33.7 us
    pallas_call x3, Pallas kernels, stencil(): pl.pallas_call(functools.partial(stencil_kernel, with_tend=with_tend), gr...  31.8 us
    select_n x3, other arithmetic, exchange_halo(): jnp.where(lane == 0, spread_w, jnp.where(lane == PY - 1, spread_e, 0.0))  20.2 us
    reshape x3, local copies, waits for them, and re-layouts, exchange_halo(): jnp.broadcast_to(east[..., None], east.shape + (PY,)).reshape(tracer.shape)  16.9 us
    reshape x3, local copies, waits for them, and re-layouts, exchange_halo(): jnp.broadcast_to(west[..., None], west.shape + (PY,)).reshape(tracer.shape)  16.7 us
    all_to_all x3, starting transfers between devices, exchange_halo(): lax.all_to_all(sent, 'patch', split_axis=0, concat_axis=0, tiled=True)  15.1 us
    broadcast_in_dim x3, local copies, waits for them, and re-layouts, exchange_halo(): jnp.broadcast_to(east[..., None], east.shape + (PY,)).reshape(tracer.shape)  9.6 us
    broadcast_in_dim x3, local copies, waits for them, and re-layouts, exchange_halo(): jnp.broadcast_to(west[..., None], west.shape + (PY,)).reshape(tracer.shape)  9.52 us
  transfers between devices with their start and end apart: 6, of which 3 were waited for; matrix products, arithmetic and copies ran while one was open for 41% of the time, Pallas kernels for 9%

profile of v1, /device:TPU:0, one launch (start us, length us, event | category | flops | bytes accessed | tf_op | source)
XLA Modules:
  0.0 228.9 jit_solution(5264110565208857523)
XLA Ops:
  6.7 6.4 %all-to-all-start = ((bf16[8,9,15,384]{3,2,1,0:T(8,128)(2,1)}), bf16[8,9,15,384]{3,2,1,0:T(8,128)(2,1)S(1)}, u32[]{:S(2)}, u32[]{:S(2)}) async-start(bf16[8,9,15,384]{3,2,1,0:T(8,128)(2,1)} %broadcast_in_dim.63), calls=%async_computation | async-start | bytes 1769472 | tf_op jit(solution)/shard_map/all_to_all | solution.py:90
  21.3 3.1 %convert_element_type.62 = bf16[135,4,16,128]{3,2,1,0:T(8,128)(2,1)} reshape(bf16[9,15,8192]{2,1,0:T(8,128)(2,1)S(1)} %convert.30) | data formatting | bytes 4423680 | tf_op jit(solution)/shard_map/convert_element_type | solution.py:137
  36.1 4.5 %all-to-all-start.3 = ((bf16[4,16,139,128]{3,1,2,0:T(8,128)(2,1)}), bf16[4,16,139,128]{3,1,2,0:T(8,128)(2,1)}, u32[]{:S(2)}, u32[]{:S(2)}) async-start(bf16[4,16,139,128]{3,1,2,0:T(8,128)(2,1)} %copy.19), calls=%async_computation.3 | async-start | bytes 4554752 | tf_op jit(solution)/shard_map/all_to_all | solution.py:162
  40.9 3.1 %broadcast_in_dim.106 = f32[9,15,64,128]{3,2,1,0:T(8,128)} broadcast(f32[9,15,64]{2,1,0:T(8,128)S(1)} %slice.216), dimensions={0,1,2} | broadcast | bytes 4458240 | tf_op jit(solution)/shard_map/broadcast_in_dim | solution.py:98
  44.1 5.6 %reshape.168 = f32[9,15,8192]{2,1,0:T(8,128)} reshape(f32[9,15,64,128]{3,2,1,0:T(8,128)} %broadcast_in_dim.106) | data formatting | bytes 8847360 | tf_op jit(solution)/shard_map/reshape | solution.py:98
  49.6 3.2 %broadcast_in_dim.107 = f32[9,15,64,128]{3,2,1,0:T(8,128)} broadcast(f32[9,15,64]{2,1,0:T(8,128)S(1)} %slice.217), dimensions={0,1,2} | broadcast | bytes 4458240 | tf_op jit(solution)/shard_map/broadcast_in_dim | solution.py:99
  52.9 5.6 %reshape.169 = f32[9,15,8192]{2,1,0:T(8,128)} reshape(f32[9,15,64,128]{3,2,1,0:T(8,128)} %broadcast_in_dim.107) | data formatting | bytes 8847360 | tf_op jit(solution)/shard_map/reshape | solution.py:99
  59.2 6.7 %fusion.2.refs_4_ = f32[9,15,8192]{2,1,0:T(8,128)} fusion(f32[9,15,8192]{2,1,0:T(8,128)} %reshape.168, f32[9,15,8192]{2,1,0:T(8,128)} %reshape.169, s32[8192]{0:T(1024)S(1)} %get-tuple-element.73, s32[8192]{0:T(1024)S(1)} %get-tuple-element.74, pred[8192]{0:T(1024)(128)(4,1)S(1)} %fusion.31), kind=kLoop, calls=%fused_computation.4 | loop fusion | flops 5529600 | bytes 13344768 | tf_op jit(solution)/shard_map/jit(_where)/select_n | solution.py:100
  65.9 10.3 %shard_map.113.refs_0_ = f32[9,15,8192]{2,1,0:T(8,128)} custom-call(f32[9,15,8192]{2,1,0:T(8,128)} %refs_0_.1, f32[15,8192]{1,0:T(8,128)} %refs_1_.5, f32[15,8192]{1,0:T(8,128)} %refs_2_.5, f32[9,15,256]{2,1,0:T(8,128)} %pad_maximum_fusion.refs_3_, f32[9,15,8192]{2,1,0:T(8,128)} %fusion.2.refs_4_), custom_call_target="tpu_custom_call" | custom-call | flops 22118400 | bytes 14254080 | tf_op jit(solution)/shard_map/pallas_call | solution.py:67
  82.3 3.7 %all-to-all-start.1 = ((bf16[8,9,15,384]{3,2,1,0:T(8,128)(2,1)}), bf16[8,9,15,384]{3,2,1,0:T(8,128)(2,1)S(1)}, u32[]{:S(2)}, u32[]{:S(2)}) async-start(bf16[8,9,15,384]{3,2,1,0:T(8,128)(2,1)} %broadcast_in_dim.109), calls=%async_computation.1 | async-start | bytes 1769472 | tf_op jit(solution)/shard_map/all_to_all | solution.py:90
  86.1 3.7 %multiply_convert_fusion.2 = bf16[16,128,256]{2,1,0:T(8,128)(2,1)S(1)} fusion(f32[256]{0:T(256)S(1)} %bitcast.111, bf16[4,16,139,128]{3,1,2,0:T(8,128)(2,1)} %all-to-all-done.3, f32[256]{0:T(256)S(1)} %bitcast.112, bf16[4,4,256]{2,1,0:T(4,128)(2,1)S(1)} %reshape.176, bf16[4,135,256]{2,1,0:T(8,128)(2,1)S(1)} %copy-done.1, bf16[3,256,256]{2,1,0:T(8,128)(2,1)S(1)} %copy-done.5), kind=kOutput, calls=%fused_computation.15 | convolution fusion | flops 858304512 | bytes 3745792 | tf_op jit(solution)/shard_map/...h,hj->...j/dot_general | solution.py:111
  94.0 3.9 %copy.23 = bf16[16,9,4,15,128]{4,0,3,1,2:T(8,128)(2,1)} copy(bf16[16,9,4,15,128]{4,3,2,1,0:T(8,128)(2,1)S(1)} %convert_bitcast_fusion) | data formatting | bytes 4423680 | tf_op jit(solution)/shard_map/convert_element_type | solution.py:170
  98.8 10.1 %all-to-all-done.1 = bf16[8,9,15,384]{3,2,1,0:T(8,128)(2,1)S(1)} async-done(((bf16[8,9,15,384]{3,2,1,0:T(8,128)(2,1)}), bf16[8,9,15,384]{3,2,1,0:T(8,128)(2,1)S(1)}, u32[]{:S(2)}, u32[]{:S(2)}) %all-to-all-start.1) | async-done | bytes 829472 | tf_op jit(solution)/shard_map/all_to_all | solution.py:90
  108.9 3.3 %all-to-all-start.5 = ((f32[8,4,128]{2,1,0:T(4,128)}), f32[8,4,128]{2,1,0:T(4,128)S(1)}, u32[]{:S(2)}, u32[]{:S(2)}) async-start(f32[8,4,128]{2,1,0:T(4,128)} %bitcast.40), calls=%async_computation.5 | async-start | bytes 32768 | tf_op jit(solution)/shard_map/all_to_all | solution.py:175
  113.2 3.2 %broadcast_in_dim.110 = f32[9,15,64,128]{3,2,1,0:T(8,128)} broadcast(f32[9,15,64]{2,1,0:T(8,128)S(1)} %slice.222), dimensions={0,1,2} | broadcast | bytes 4458240 | tf_op jit(solution)/shard_map/broadcast_in_dim | solution.py:98
  116.5 5.6 %reshape.170 = f32[9,15,8192]{2,1,0:T(8,128)} reshape(f32[9,15,64,128]{3,2,1,0:T(8,128)} %broadcast_in_dim.110) | data formatting | bytes 8847360 | tf_op jit(solution)/shard_map/reshape | solution.py:98
  122.0 3.2 %broadcast_in_dim.111 = f32[9,15,64,128]{3,2,1,0:T(8,128)} broadcast(f32[9,15,64]{2,1,0:T(8,128)S(1)} %slice.223), dimensions={0,1,2} | broadcast | bytes 4458240 | tf_op jit(solution)/shard_map/broadcast_in_dim | solution.py:99
  125.2 5.7 %reshape.171 = f32[9,15,8192]{2,1,0:T(8,128)} reshape(f32[9,15,64,128]{3,2,1,0:T(8,128)} %broadcast_in_dim.111) | data formatting | bytes 8847360 | tf_op jit(solution)/shard_map/reshape | solution.py:99
  130.9 4.1 %all-to-all-start.4 = ((bf16[16,9,4,15,128]{4,0,3,1,2:T(8,128)(2,1)}), bf16[16,9,4,15,128]{4,0,3,1,2:T(8,128)(2,1)S(1)}, u32[]{:S(2)}, u32[]{:S(2)}) async-start(bf16[16,9,4,15,128]{4,0,3,1,2:T(8,128)(2,1)} %copy.23), calls=%async_computation.4 | async-start | bytes 4423680 | tf_op jit(solution)/shard_map/all_to_all | solution.py:178
  135.0 6.7 %fusion.1.refs_4_ = f32[9,15,8192]{2,1,0:T(8,128)} fusion(f32[9,15,8192]{2,1,0:T(8,128)} %reshape.170, f32[9,15,8192]{2,1,0:T(8,128)} %reshape.171, s32[8192]{0:T(1024)S(1)} %get-tuple-element.73, s32[8192]{0:T(1024)S(1)} %get-tuple-element.74, pred[8192]{0:T(1024)(128)(4,1)S(1)} %fusion.31), kind=kLoop, calls=%fused_computation.3 | loop fusion | flops 5529600 | bytes 13344768 | tf_op jit(solution)/shard_map/jit(_where)/select_n | solution.py:100
  141.8 10.3 %shard_map.114.refs_0_ = f32[9,15,8192]{2,1,0:T(8,128)} custom-call(f32[9,15,8192]{2,1,0:T(8,128)} %shard_map.113.refs_0_, f32[15,8192]{1,0:T(8,128)} %refs_1_.5, f32[15,8192]{1,0:T(8,128)} %refs_2_.5, f32[9,15,256]{2,1,0:T(8,128)} %pad_maximum_fusion.1.refs_3_, f32[9,15,8192]{2,1,0:T(8,128)} %fusion.1.refs_4_), custom_call_target="tpu_custom_call" | custom-call | flops 22118400 | bytes 14254080 | tf_op jit(solution)/shard_map/pallas_call | solution.py:67
  152.1 4.0 %convert.32 = bf16[9,15,8192]{2,1,0:T(8,128)(2,1)} convert(f32[9,15,8192]{2,1,0:T(8,128)} %shard_map.114.refs_0_) | non-fusion elementwise | flops 1105920 | bytes 6635520 | tf_op jit(solution)/shard_map/convert.7
  156.1 2.9 %slice.157 = bf16[9,15,64]{2,1,0:T(8,128)(2,1)S(1)} slice(bf16[9,15,8192]{2,1,0:T(8,128)(2,1)} %convert.32), slice={[0:9:1], [0:15:1], [127:8192:128]} | slice | bytes 34560 | tf_op jit(solution)/shard_map/slice | solution.py:82
  159.0 2.9 %slice.156 = bf16[9,15,64]{2,1,0:T(8,128)(2,1)S(1)} slice(bf16[9,15,8192]{2,1,0:T(8,128)(2,1)} %convert.32), slice={[0:9:1], [0:15:1], [0:8192:128]} | slice | bytes 34560 | tf_op jit(solution)/shard_map/slice | solution.py:82
  163.8 5.0 %all-to-all-start.2 = ((bf16[8,9,15,384]{3,2,1,0:T(8,128)(2,1)}), bf16[8,9,15,384]{3,2,1,0:T(8,128)(2,1)S(1)}, u32[]{:S(2)}, u32[]{:S(2)}) async-start(bf16[8,9,15,384]{3,2,1,0:T(8,128)(2,1)} %broadcast_in_dim.112), calls=%async_computation.2 | async-start | bytes 1769472 | tf_op jit(solution)/shard_map/all_to_all | solution.py:90
  170.8 21.0 %all-to-all-done.2 = bf16[8,9,15,384]{3,2,1,0:T(8,128)(2,1)S(1)} async-done(((bf16[8,9,15,384]{3,2,1,0:T(8,128)(2,1)}), bf16[8,9,15,384]{3,2,1,0:T(8,128)(2,1)S(1)}, u32[]{:S(2)}, u32[]{:S(2)}) %all-to-all-start.2) | async-done | bytes 829472 | tf_op jit(solution)/shard_map/all_to_all | solution.py:90
  192.2 3.1 %broadcast_in_dim.113 = f32[9,15,64,128]{3,2,1,0:T(8,128)} broadcast(f32[9,15,64]{2,1,0:T(8,128)S(1)} %slice.228), dimensions={0,1,2} | broadcast | bytes 4458240 | tf_op jit(solution)/shard_map/broadcast_in_dim | solution.py:98
  195.4 5.6 %reshape.172 = f32[9,15,8192]{2,1,0:T(8,128)} reshape(f32[9,15,64,128]{3,2,1,0:T(8,128)} %broadcast_in_dim.113) | data formatting | bytes 8847360 | tf_op jit(solution)/shard_map/reshape | solution.py:98
  200.9 3.2 %broadcast_in_dim.114 = f32[9,15,64,128]{3,2,1,0:T(8,128)} broadcast(f32[9,15,64]{2,1,0:T(8,128)S(1)} %slice.229), dimensions={0,1,2} | broadcast | bytes 4458240 | tf_op jit(solution)/shard_map/broadcast_in_dim | solution.py:99
  204.1 5.6 %reshape.173 = f32[9,15,8192]{2,1,0:T(8,128)} reshape(f32[9,15,64,128]{3,2,1,0:T(8,128)} %broadcast_in_dim.114) | data formatting | bytes 8847360 | tf_op jit(solution)/shard_map/reshape | solution.py:99
  210.4 6.7 %fusion.refs_4_ = f32[9,15,8192]{2,1,0:T(8,128)} fusion(f32[9,15,8192]{2,1,0:T(8,128)} %reshape.172, f32[9,15,8192]{2,1,0:T(8,128)} %reshape.173, s32[8192]{0:T(1024)S(1)} %get-tuple-element.73, s32[8192]{0:T(1024)S(1)} %get-tuple-element.74, pred[8192]{0:T(1024)(128)(4,1)S(1)} %fusion.31), kind=kLoop, calls=%fused_computation.2 | loop fusion | flops 5529600 | bytes 13344768 | tf_op jit(solution)/shard_map/jit(_where)/select_n | solution.py:100
  217.1 11.2 %shard_map.115 = f32[9,15,8192]{2,1,0:T(8,128)} custom-call(f32[9,15,8192]{2,1,0:T(8,128)} %shard_map.114.refs_0_, f32[15,8192]{1,0:T(8,128)} %refs_1_.5, f32[15,8192]{1,0:T(8,128)} %refs_2_.5, f32[9,15,256]{2,1,0:T(8,128)} %pad_maximum_fusion.2.refs_3_, f32[9,15,8192]{2,1,0:T(8,128)} %fusion.refs_4_, bf16[64,9,15,128]{3,2,1,0:T(8,128)(2,1)} %bitcast.102), custom_call_target="tpu_custom_call" | custom-call | flops 22118400 | bytes 14254080 | tf_op jit(solution)/shard_map/pallas_call | solution.py:67
  (83 shorter events, 36.8 us)
Async XLA Ops:
  3.3 9.8 %copy-start.3 = (s32[8,4]{0,1:T(4,128)S(1)}, s32[8,4]{0,1:T(4,128)}, u32[]{:S(2)}) copy-start(s32[8,4]{0,1:T(4,128)} %param.21) | copy-start | bytes 388
  6.7 29.4 %all-to-all-start = ((bf16[8,9,15,384]{3,2,1,0:T(8,128)(2,1)}), bf16[8,9,15,384]{3,2,1,0:T(8,128)(2,1)S(1)}, u32[]{:S(2)}, u32[]{:S(2)}) async-start(bf16[8,9,15,384]{3,2,1,0:T(8,128)(2,1)} %broadcast_in_dim.63), calls=%async_computation | async-start | bytes 1769472 | tf_op jit(solution)/shard_map/all_to_all | solution.py:90
  21.3 3.1 %copy-start = (bf16[556,256]{1,0:T(8,128)(2,1)S(1)}, bf16[556,256]{1,0:T(8,128)(2,1)}, u32[]{:S(2)}) copy-start(bf16[556,256]{1,0:T(8,128)(2,1)} %param.16) | copy-start | bytes 854020
  28.9 2.0 slice-start
  28.9 3.4 %copy-start.4 = (s32[512,1]{0,1:T(1,128)S(1)}, s32[512,1]{0,1:T(1,128)}, u32[]{:S(2)}) copy-start(s32[512,1]{0,1:T(1,128)} %param.20) | copy-start | bytes 6148
  28.9 4.6 %copy-start.2 = (f32[4,256]{1,0:T(4,128)S(1)}, f32[4,256]{1,0:T(4,128)}, u32[]{:S(2)}) copy-start(f32[4,256]{1,0:T(4,128)} %param.17) | copy-start | bytes 12292
  36.1 45.2 %all-to-all-start.3 = ((bf16[4,16,139,128]{3,1,2,0:T(8,128)(2,1)}), bf16[4,16,139,128]{3,1,2,0:T(8,128)(2,1)}, u32[]{:S(2)}, u32[]{:S(2)}) async-start(bf16[4,16,139,128]{3,1,2,0:T(8,128)(2,1)} %copy.19), calls=%async_computation.3 | async-start | bytes 4554752 | tf_op jit(solution)/shard_map/all_to_all | solution.py:162
  78.8 7.2 %copy-start.1 = (bf16[4,135,256]{2,1,0:T(8,128)(2,1)S(1)}, bf16[4,135,256]{2,1,0:T(8,128)(2,1)}, u32[]{:S(2)}) copy-start(bf16[4,135,256]{2,1,0:T(8,128)(2,1)} %copy.21) | copy-start | bytes 829444
  78.9 7.2 %copy-start.5 = (bf16[3,256,256]{2,1,0:T(8,128)(2,1)S(1)}, bf16[3,256,256]{2,1,0:T(8,128)(2,1)}, u32[]{:S(2)}) copy-start(bf16[3,256,256]{2,1,0:T(8,128)(2,1)} %param.18) | copy-start | bytes 1179652
  82.3 26.5 %all-to-all-start.1 = ((bf16[8,9,15,384]{3,2,1,0:T(8,128)(2,1)}), bf16[8,9,15,384]{3,2,1,0:T(8,128)(2,1)S(1)}, u32[]{:S(2)}, u32[]{:S(2)}) async-start(bf16[8,9,15,384]{3,2,1,0:T(8,128)(2,1)} %broadcast_in_dim.109), calls=%async_computation.1 | async-start | bytes 1769472 | tf_op jit(solution)/shard_map/all_to_all | solution.py:90
  108.9 22.0 %all-to-all-start.5 = ((f32[8,4,128]{2,1,0:T(4,128)}), f32[8,4,128]{2,1,0:T(4,128)S(1)}, u32[]{:S(2)}, u32[]{:S(2)}) async-start(f32[8,4,128]{2,1,0:T(4,128)} %bitcast.40), calls=%async_computation.5 | async-start | bytes 32768 | tf_op jit(solution)/shard_map/all_to_all | solution.py:175
  130.9 31.9 %all-to-all-start.4 = ((bf16[16,9,4,15,128]{4,0,3,1,2:T(8,128)(2,1)}), bf16[16,9,4,15,128]{4,0,3,1,2:T(8,128)(2,1)S(1)}, u32[]{:S(2)}, u32[]{:S(2)}) async-start(bf16[16,9,4,15,128]{4,0,3,1,2:T(8,128)(2,1)} %copy.23), calls=%async_computation.4 | async-start | bytes 4423680 | tf_op jit(solution)/shard_map/all_to_all | solution.py:178
  163.8 28.1 %all-to-all-start.2 = ((bf16[8,9,15,384]{3,2,1,0:T(8,128)(2,1)}), bf16[8,9,15,384]{3,2,1,0:T(8,128)(2,1)S(1)}, u32[]{:S(2)}, u32[]{:S(2)}) async-start(bf16[8,9,15,384]{3,2,1,0:T(8,128)(2,1)} %broadcast_in_dim.112), calls=%async_computation.2 | async-start | bytes 1769472 | tf_op jit(solution)/shard_map/all_to_all | solution.py:90

commit v2 on v1

--- a/solution.py
+++ b/solution.py
@@ -22,19 +22,20 @@
 
 def stencil_kernel(*refs, with_tend):
     if with_tend:
-        st_ref, cx_ref, cy_ref, rows_ref, sides_ref, tend_ref, out_ref = refs
+        st_ref, cx_ref, cy_ref, rows_ref, tend_ref, out_ref = refs
     else:
-        st_ref, cx_ref, cy_ref, rows_ref, sides_ref, out_ref = refs
+        st_ref, cx_ref, cy_ref, rows_ref, out_ref = refs
     rows = st_ref.shape[2] // PY
     north = rows_ref[0, :, 0:PY]
     south = rows_ref[0, :, PY : 2 * PY]
+    sides = rows_ref[0, :, 2 * PY : 3 * PY]
     lane = lax.broadcasted_iota(jnp.int32, north.shape, 1)
     for x in range(rows):
         here = slice(x * PY, (x + 1) * PY)
         cur = st_ref[0, :, here]
         up = north if x == 0 else st_ref[0, :, (x - 1) * PY : x * PY]
         down = south if x == rows - 1 else st_ref[0, :, (x + 1) * PY : (x + 2) * PY]
-        side = sides_ref[0, :, here]
+        side = pltpu.roll(sides, (PY - 2 * x) % PY, 1)
         west = jnp.where(lane == 0, side, pltpu.roll(cur, 1, 1))
         east = jnp.where(lane == PY - 1, side, pltpu.roll(cur, PY - 1, 1))
         along_x = cx_ref[:, here]
@@ -50,17 +51,16 @@
         out_ref[0, :, here] = val
 
 
-def stencil(tracer, along_x, along_y, halo_rows, halo_sides, tend):
+def stencil(tracer, along_x, along_y, halo, tend):
     n_vars, levels, width = tracer.shape
     with_tend = tend is not None
     in_specs = [
         pl.BlockSpec((1, levels, width), lambda v: (v, 0, 0)),
         pl.BlockSpec((levels, width), lambda v: (0, 0)),
         pl.BlockSpec((levels, width), lambda v: (0, 0)),
-        pl.BlockSpec((1, levels, 2 * PY), lambda v: (v, 0, 0)),
-        pl.BlockSpec((1, levels, width), lambda v: (v, 0, 0)),
+        pl.BlockSpec((1, levels, 3 * PY), lambda v: (v, 0, 0)),
     ]
-    args = [tracer, along_x, along_y, halo_rows, halo_sides]
+    args = [tracer, along_x, along_y, halo]
     if with_tend:
         in_specs.append(pl.BlockSpec((tend.shape[0], 1, levels, PY), lambda v: (0, v, 0, 0)))
         args.append(tend)
@@ -71,7 +71,7 @@
         out_specs=pl.BlockSpec((1, levels, width), lambda v: (v, 0, 0)),
         out_shape=jax.ShapeDtypeStruct(tracer.shape, jnp.float32),
         cost_estimate=pl.CostEstimate(
-            flops=20 * tracer.size, transcendentals=0, bytes_accessed=4 * (3 * tracer.size + 2 * along_x.size)
+            flops=20 * tracer.size, transcendentals=0, bytes_accessed=4 * (2 * tracer.size + 2 * along_x.size)
         ),
     )(*args)
 
@@ -87,18 +87,14 @@
 def exchange_halo(tracer, beside_all, patches):
     payload = edges_of(tracer)
     sent = jnp.broadcast_to(payload[None], (patches,) + payload.shape)
-    got = lax.all_to_all(sent, "patch", split_axis=0, concat_axis=0, tiled=True).astype(jnp.float32)
+    got = lax.all_to_all(sent, "patch", split_axis=0, concat_axis=0, tiled=True)
     rows = PX
     north = jnp.take(got, beside_all[0], axis=0)[..., PY : 2 * PY]
     south = jnp.take(got, beside_all[1], axis=0)[..., 0:PY]
     west = jnp.take(got, beside_all[2], axis=0)[..., 2 * PY + rows : 2 * PY + 2 * rows]
     east = jnp.take(got, beside_all[3], axis=0)[..., 2 * PY : 2 * PY + rows]
-    width = tracer.shape[-1]
-    lane = lax.broadcasted_iota(jnp.int32, tracer.shape, 2) % PY
-    spread_w = jnp.broadcast_to(west[..., None], west.shape + (PY,)).reshape(tracer.shape)
-    spread_e = jnp.broadcast_to(east[..., None], east.shape + (PY,)).reshape(tracer.shape)
-    sides = jnp.where(lane == 0, spread_w, jnp.where(lane == PY - 1, spread_e, 0.0))
-    return jnp.concatenate([north, south], axis=-1), sides
+    sides = jnp.stack([west, jnp.roll(east, -1, axis=-1)], axis=-1).reshape(west.shape[:-1] + (2 * rows,))
+    return jnp.concatenate([north, south, sides], axis=-1).astype(jnp.float32)
 
 
 def activate(pre_act):
@@ -179,10 +175,10 @@
     tendency_here = arrived.reshape(PX, VARS, level_share, PY)
     advected = state
     for section_index in range(SUBSTEPS):
-        halo_rows, halo_sides = exchange_halo(advected, beside_all, patches)
+        halo = exchange_halo(advected, beside_all, patches)
         last = section_index == SUBSTEPS - 1
         advected = stencil(
-            advected, courant_x, courant_y, halo_rows, halo_sides, tendency_here if last else None
+            advected, courant_x, courant_y, halo, tendency_here if last else None
         )
     new_state = advected
     return (new_state, owner_heating)

time: 231 us -> 184 us (0.80)
  local copies, waits for them, and re-layouts: 83.6 us -> 30.9 us
  waiting for transfers between devices: 33.7 us -> 63.9 us
  other arithmetic: 35.3 us -> 15.2 us
    reshape x6 -> x3, local copies, waits for them, and re-layouts: 33.6 us -> 0.52 us  [exchange_halo(): jnp.stack([west, jnp.roll(east, -1, axis=-1)], axis=-1)]
    select_n x6 -> x3, other arithmetic: 20.4 us -> 0.2 us  [exchange_halo(): north = jnp.take(got, beside_all[0], axis=0)[..., PY:2 * PY]]
    broadcast_in_dim x6 -> x0, local copies, waits for them, and re-layouts: 19.1 us -> none  [the longest x3 9.6 us: exchange_halo(): jnp.broadcast_to(east[..., None], east.shape + (PY,)).reshape(tracer.shape)]
    all_to_all x3, waiting for transfers between devices: 33.7 us -> 46.6 us  [exchange_halo(): got = lax.all_to_all(sent, 'patch', split_axis=0, concat_axis=0, tiled=True)]
    all_to_all x1, waiting for transfers between devices: 0.01 us -> 7.85 us  [on_device(): lax.all_to_all(by_quarter, 'grp', split_axis=0, concat_axis=0, tiled=True)]
    all_to_all x1, waiting for transfers between devices: 0.01 us -> 5.49 us  [on_device(): lax.all_to_all(packed, 'patch', split_axis=0, concat_axis=0, tiled=True)]
    all_to_all x1, waiting for transfers between devices: 0.01 us -> 3.91 us  [on_device(): lax.all_to_all(tendency, 'grp', split_axis=2, concat_axis=0, tiled=True)]
    pallas_call x3, Pallas kernels: 31.8 us -> 29.5 us  [stencil(): pl.pallas_call(functools.partial(stencil_kernel, with_tend=with_tend), gr...]
  transfers between devices with their start and end apart: 6 -> 6, of which waited for: 3 -> 6; matrix products, arithmetic and copies ran while one was open for 41% -> 20% of each run, Pallas kernels for 9% -> 11%
where the time goes in v2:
time: 184 us; the launch traced here: 182 us
  waiting for transfers between devices  63.9 us (35%)
  local copies, waits for them, and re-layouts  30.9 us (17%)
  Pallas kernels  29.5 us (16%)
  starting transfers between devices  25.3 us (14%)
  other arithmetic  15.2 us (8%)
  between operations  8.73 us (5%)
  matrix products  8.6 us (5%)
    all_to_all x3, waiting for transfers between devices, exchange_halo(): got = lax.all_to_all(sent, 'patch', split_axis=0, concat_axis=0, tiled=True)  46.6 us
    pallas_call x3, Pallas kernels, stencil(): pl.pallas_call(functools.partial(stencil_kernel, with_tend=with_tend), gr...  29.5 us
    all_to_all x3, starting transfers between devices, exchange_halo(): got = lax.all_to_all(sent, 'patch', split_axis=0, concat_axis=0, tiled=True)  13.5 us
    another operation x3, other arithmetic  9.33 us
    all_to_all x1, waiting for transfers between devices, on_device(): lax.all_to_all(by_quarter, 'grp', split_axis=0, concat_axis=0, tiled=True)  7.85 us
    all_to_all x1, waiting for transfers between devices, on_device(): lax.all_to_all(packed, 'patch', split_axis=0, concat_axis=0, tiled=True)  5.49 us
    dot_general x2, matrix products, hidden_layers(): jnp.einsum('...h,hj->...j', hidden, w_mid[layer_index], preferred_element...  5.41 us
    slice x3, local copies, waits for them, and re-layouts, edges_of(): tracer[..., PY - 1::PY]  5.22 us
  transfers between devices with their start and end apart: 6, of which 6 were waited for; matrix products, arithmetic and copies ran while one was open for 20% of the time, Pallas kernels for 11%

profile of v2, /device:TPU:0, one launch (start us, length us, event | category | flops | bytes accessed | tf_op | source)
XLA Modules:
  0.0 182.1 jit_solution(11050796716285405711)
XLA Ops:
  0.6 2.6 %convert.30 = bf16[9,15,8192]{2,1,0:T(8,128)(2,1)S(1)} convert(f32[9,15,8192]{2,1,0:T(8,128)} %refs_0_.1) | non-fusion elementwise | flops 1105920 | bytes 6635520 | tf_op jit(solution)/shard_map/convert.23
  3.3 1.2 slice.157
  4.4 1.2 slice.156
  6.7 6.4 %all-to-all-start = ((bf16[8,9,15,384]{3,2,1,0:T(8,128)(2,1)}), bf16[8,9,15,384]{3,2,1,0:T(8,128)(2,1)S(1)}, u32[]{:S(2)}, u32[]{:S(2)}) async-start(bf16[8,9,15,384]{3,2,1,0:T(8,128)(2,1)} %broadcast_in_dim.61), calls=%async_computation | async-start | bytes 1769472 | tf_op jit(solution)/shard_map/all_to_all | solution.py:90
  21.5 3.1 %convert_element_type.62 = bf16[135,4,16,128]{3,2,1,0:T(8,128)(2,1)} reshape(bf16[9,15,8192]{2,1,0:T(8,128)(2,1)S(1)} %convert.30) | data formatting | bytes 4423680 | tf_op jit(solution)/shard_map/convert_element_type | solution.py:133
  25.9 1.8 %maximum_bitcast_fusion = bf16[4,16,139,128]{3,1,0,2:T(8,128)(2,1)S(1)} fusion(bf16[4,4,16,128]{3,2,1,0:T(8,128)(2,1)S(1)} %bitcast.112, bf16[135,4,16,128]{3,2,1,0:T(8,128)(2,1)} %convert_element_type.62), kind=kLoop, calls=%fused_computation.3 | loop fusion | flops 1138688 | bytes 4554752 | tf_op jit(solution)/shard_map/transpose | solution.py:138
  27.7 1.8 copy.34
  29.5 6.7 %all-to-all-done = bf16[8,9,15,384]{3,2,1,0:T(8,128)(2,1)S(1)} async-done(((bf16[8,9,15,384]{3,2,1,0:T(8,128)(2,1)}), bf16[8,9,15,384]{3,2,1,0:T(8,128)(2,1)S(1)}, u32[]{:S(2)}, u32[]{:S(2)}) %all-to-all-start) | async-done | bytes 829472 | tf_op jit(solution)/shard_map/all_to_all | solution.py:90
  36.1 4.7 %all-to-all-start.3 = ((bf16[4,16,139,128]{3,1,2,0:T(8,128)(2,1)}), bf16[4,16,139,128]{3,1,2,0:T(8,128)(2,1)}, u32[]{:S(2)}, u32[]{:S(2)}) async-start(bf16[4,16,139,128]{3,1,2,0:T(8,128)(2,1)} %copy.34), calls=%async_computation.3 | async-start | bytes 4554752 | tf_op jit(solution)/shard_map/all_to_all | solution.py:158
  44.9 9.7 %shard_map.113.refs_0_ = f32[9,15,8192]{2,1,0:T(8,128)} custom-call(f32[9,15,8192]{2,1,0:T(8,128)} %refs_0_.1, f32[15,8192]{1,0:T(8,128)} %refs_1_.5, f32[15,8192]{1,0:T(8,128)} %refs_2_.5, f32[9,15,384]{2,1,0:T(8,128)} %maximum_convert_fusion.refs_3_), custom_call_target="tpu_custom_call" | custom-call | flops 22118400 | bytes 9830400 | tf_op jit(solution)/shard_map/pallas_call | solution.py:67
  54.6 2.7 %convert.31 = bf16[9,15,8192]{2,1,0:T(8,128)(2,1)S(1)} convert(f32[9,15,8192]{2,1,0:T(8,128)} %shard_map.113.refs_0_) | non-fusion elementwise | flops 1105920 | bytes 6635520 | tf_op jit(solution)/shard_map/convert.15
  57.3 1.2 slice.169
  58.4 1.2 slice.170
  59.6 7.9 %all-to-all-done.3 = bf16[4,16,139,128]{3,1,2,0:T(8,128)(2,1)} async-done(((bf16[4,16,139,128]{3,1,2,0:T(8,128)(2,1)}), bf16[4,16,139,128]{3,1,2,0:T(8,128)(2,1)}, u32[]{:S(2)}, u32[]{:S(2)}) %all-to-all-start.3) | async-done | bytes 2277408 | tf_op jit(solution)/shard_map/all_to_all | solution.py:158
  67.5 3.7 %multiply_convert_fusion.2 = bf16[16,128,256]{2,1,0:T(8,128)(2,1)S(1)} fusion(f32[256]{0:T(256)S(1)} %bitcast.117, bf16[4,16,139,128]{3,1,2,0:T(8,128)(2,1)} %all-to-all-done.3, f32[256]{0:T(256)S(1)} %bitcast.118, bf16[4,4,256]{2,1,0:T(4,128)(2,1)S(1)} %reshape.158, bf16[4,135,256]{2,1,0:T(8,128)(2,1)S(1)} %copy-done.2, bf16[3,256,256]{2,1,0:T(8,128)(2,1)S(1)} %copy-done.10), kind=kOutput, calls=%fused_computation.7 | convolution fusion | flops 858304512 | bytes 3745792 | tf_op jit(solution)/shard_map/...h,hj->...j/dot_general | solution.py:107
  71.2 1.7 multiply_convert_fusion.1
  72.9 2.4 %convert_bitcast_fusion = bf16[16,9,4,15,128]{4,3,2,1,0:T(8,128)(2,1)S(1)} fusion(bf16[256,9,4,15,1]{0,3,2,1,4:T(8,128)(2,1)S(1)} %reshape.454, bf16[16,128,256]{2,1,0:T(8,128)(2,1)} %multiply_convert_fusion.1, f32[256]{0:T(256)S(1)} %bitcast.115, bf16[3,256,256]{2,1,0:T(8,128)(2,1)S(1)} %copy-done.10), kind=kOutput, calls=%fused_computation.2 | convolution fusion | flops 838918144 | bytes 3687424 | tf_op jit(solution)/shard_map/bch,hvgl->bvglc/dot_general | solution.py:164
  76.2 3.3 %all-to-all-start.5 = ((f32[8,4,128]{2,1,0:T(4,128)}), f32[8,4,128]{2,1,0:T(4,128)S(1)}, u32[]{:S(2)}, u32[]{:S(2)}) async-start(f32[8,4,128]{2,1,0:T(4,128)} %bitcast.49), calls=%async_computation.5 | async-start | bytes 32768 | tf_op jit(solution)/shard_map/all_to_all | solution.py:171
  79.6 5.5 %all-to-all-done.5 = f32[8,4,128]{2,1,0:T(4,128)S(1)} async-done(((f32[8,4,128]{2,1,0:T(4,128)}), f32[8,4,128]{2,1,0:T(4,128)S(1)}, u32[]{:S(2)}, u32[]{:S(2)}) %all-to-all-start.5) | async-done | bytes 16416 | tf_op jit(solution)/shard_map/all_to_all | solution.py:171
  86.1 3.5 %all-to-all-start.1 = ((bf16[8,9,15,384]{3,2,1,0:T(8,128)(2,1)}), bf16[8,9,15,384]{3,2,1,0:T(8,128)(2,1)S(1)}, u32[]{:S(2)}, u32[]{:S(2)}) async-start(bf16[8,9,15,384]{3,2,1,0:T(8,128)(2,1)} %broadcast_in_dim.64), calls=%async_computation.1 | async-start | bytes 1769472 | tf_op jit(solution)/shard_map/all_to_all | solution.py:90
  89.7 4.0 %copy.38 = bf16[16,9,4,15,128]{4,0,3,1,2:T(8,128)(2,1)} copy(bf16[16,9,4,15,128]{4,3,2,1,0:T(8,128)(2,1)S(1)} %convert_bitcast_fusion) | data formatting | bytes 4423680 | tf_op jit(solution)/shard_map/convert_element_type | solution.py:166
  93.6 19.0 %all-to-all-done.1 = bf16[8,9,15,384]{3,2,1,0:T(8,128)(2,1)S(1)} async-done(((bf16[8,9,15,384]{3,2,1,0:T(8,128)(2,1)}), bf16[8,9,15,384]{3,2,1,0:T(8,128)(2,1)S(1)}, u32[]{:S(2)}, u32[]{:S(2)}) %all-to-all-start.1) | async-done | bytes 829472 | tf_op jit(solution)/shard_map/all_to_all | solution.py:90
  112.7 3.8 %all-to-all-start.4 = ((bf16[16,9,4,15,128]{4,0,3,1,2:T(8,128)(2,1)}), bf16[16,9,4,15,128]{4,0,3,1,2:T(8,128)(2,1)S(1)}, u32[]{:S(2)}, u32[]{:S(2)}) async-start(bf16[16,9,4,15,128]{4,0,3,1,2:T(8,128)(2,1)} %copy.38), calls=%async_computation.4 | async-start | bytes 4423680 | tf_op jit(solution)/shard_map/all_to_all | solution.py:174
  118.0 9.7 %shard_map.114.refs_0_ = f32[9,15,8192]{2,1,0:T(8,128)} custom-call(f32[9,15,8192]{2,1,0:T(8,128)} %shard_map.113.refs_0_, f32[15,8192]{1,0:T(8,128)} %refs_1_.5, f32[15,8192]{1,0:T(8,128)} %refs_2_.5, f32[9,15,384]{2,1,0:T(8,128)} %maximum_convert_fusion.1.refs_3_), custom_call_target="tpu_custom_call" | custom-call | flops 22118400 | bytes 9830400 | tf_op jit(solution)/shard_map/pallas_call | solution.py:67
  127.7 4.0 %convert.32 = bf16[9,15,8192]{2,1,0:T(8,128)(2,1)} convert(f32[9,15,8192]{2,1,0:T(8,128)} %shard_map.114.refs_0_) | non-fusion elementwise | flops 1105920 | bytes 6635520 | tf_op jit(solution)/shard_map/convert.7
  131.7 2.9 %slice.178 = bf16[9,15,64]{2,1,0:T(8,128)(2,1)S(1)} slice(bf16[9,15,8192]{2,1,0:T(8,128)(2,1)} %convert.32), slice={[0:9:1], [0:15:1], [0:8192:128]} | slice | bytes 34560 | tf_op jit(solution)/shard_map/slice | solution.py:82
  134.6 2.9 %slice.179 = bf16[9,15,64]{2,1,0:T(8,128)(2,1)S(1)} slice(bf16[9,15,8192]{2,1,0:T(8,128)(2,1)} %convert.32), slice={[0:9:1], [0:15:1], [127:8192:128]} | slice | bytes 34560 | tf_op jit(solution)/shard_map/slice | solution.py:82
  138.4 3.9 %all-to-all-done.4 = bf16[16,9,4,15,128]{4,0,3,1,2:T(8,128)(2,1)S(1)} async-done(((bf16[16,9,4,15,128]{4,0,3,1,2:T(8,128)(2,1)}), bf16[16,9,4,15,128]{4,0,3,1,2:T(8,128)(2,1)S(1)}, u32[]{:S(2)}, u32[]{:S(2)}) %all-to-all-start.4) | async-done | bytes 2211872 | tf_op jit(solution)/shard_map/all_to_all | solution.py:174
  143.3 3.6 %all-to-all-start.2 = ((bf16[8,9,15,384]{3,2,1,0:T(8,128)(2,1)}), bf16[8,9,15,384]{3,2,1,0:T(8,128)(2,1)S(1)}, u32[]{:S(2)}, u32[]{:S(2)}) async-start(bf16[8,9,15,384]{3,2,1,0:T(8,128)(2,1)} %broadcast_in_dim.65), calls=%async_computation.2 | async-start | bytes 1769472 | tf_op jit(solution)/shard_map/all_to_all | solution.py:90
  146.9 2.1 %copy.39 = bf16[4,16,9,1,15,128]{5,4,2,1,0,3:T(8,128)(2,1)} copy(bf16[4,16,9,1,15,128]{5,1,4,2,0,3:T(8,128)(2,1)S(1)} %bitcast.106) | data formatting | bytes 4423680 | tf_op jit(solution)/shard_map/all_to_all | solution.py:174
  148.9 20.9 %all-to-all-done.2 = bf16[8,9,15,384]{3,2,1,0:T(8,128)(2,1)S(1)} async-done(((bf16[8,9,15,384]{3,2,1,0:T(8,128)(2,1)}), bf16[8,9,15,384]{3,2,1,0:T(8,128)(2,1)S(1)}, u32[]{:S(2)}, u32[]{:S(2)}) %all-to-all-start.2) | async-done | bytes 829472 | tf_op jit(solution)/shard_map/all_to_all | solution.py:90
  171.4 10.1 %shard_map.115 = f32[9,15,8192]{2,1,0:T(8,128)} custom-call(f32[9,15,8192]{2,1,0:T(8,128)} %shard_map.114.refs_0_, f32[15,8192]{1,0:T(8,128)} %refs_1_.5, f32[15,8192]{1,0:T(8,128)} %refs_2_.5, f32[9,15,384]{2,1,0:T(8,128)} %maximum_convert_fusion.2.refs_3_, bf16[64,9,15,128]{3,2,1,0:T(8,128)(2,1)} %bitcast.105), custom_call_target="tpu_custom_call" | custom-call | flops 22118400 | bytes 9830400 | tf_op jit(solution)/shard_map/pallas_call | solution.py:67
  (87 shorter events, 14.5 us)
Async XLA Ops:
  3.3 9.8 %copy-start.5 = (s32[8,4]{0,1:T(4,128)S(1)}, s32[8,4]{0,1:T(4,128)}, u32[]{:S(2)}) copy-start(s32[8,4]{0,1:T(4,128)} %param.21) | copy-start | bytes 388
  3.3 18.2 %copy-start = (bf16[556,256]{1,0:T(8,128)(2,1)S(1)}, bf16[556,256]{1,0:T(8,128)(2,1)}, u32[]{:S(2)}) copy-start(bf16[556,256]{1,0:T(8,128)(2,1)} %param.16) | copy-start | bytes 854020
  6.7 29.4 %all-to-all-start = ((bf16[8,9,15,384]{3,2,1,0:T(8,128)(2,1)}), bf16[8,9,15,384]{3,2,1,0:T(8,128)(2,1)S(1)}, u32[]{:S(2)}, u32[]{:S(2)}) async-start(bf16[8,9,15,384]{3,2,1,0:T(8,128)(2,1)} %broadcast_in_dim.61), calls=%async_computation | async-start | bytes 1769472 | tf_op jit(solution)/shard_map/all_to_all | solution.py:90
  21.4 3.6 %copy-start.6 = (s32[512,1]{0,1:T(1,128)S(1)}, s32[512,1]{0,1:T(1,128)}, u32[]{:S(2)}) copy-start(s32[512,1]{0,1:T(1,128)} %param.20) | copy-start | bytes 6148
  21.5 4.4 %copy-start.3 = (bf16[4,8192]{1,0:T(4,128)(2,1)S(1)}, bf16[4,8192]{1,0:T(4,128)(2,1)}, u32[]{:S(2)}) copy-start(bf16[4,8192]{1,0:T(4,128)(2,1)} %param.15) | copy-start | bytes 196612
  29.5 11.5 %slice-start = ((bf16[556,256]{1,0:T(8,128)(2,1)}), bf16[540,256]{1,0:T(8,128)(2,1)S(1)}, s32[]{:S(2)}) async-start(bf16[556,256]{1,0:T(8,128)(2,1)} %param.16), calls=%async_computation.6 | async-start | bytes 557056 | tf_op jit(solution)/shard_map/slice | solution.py:149
  29.5 12.5 %copy-start.1 = (bf16[256,540]{0,1:T(8,128)(2,1)S(1)}, bf16[256,540]{0,1:T(8,128)(2,1)}, u32[]{:S(2)}) copy-start(bf16[256,540]{0,1:T(8,128)(2,1)} %param.19) | copy-start | bytes 829444
  36.1 31.3 %all-to-all-start.3 = ((bf16[4,16,139,128]{3,1,2,0:T(8,128)(2,1)}), bf16[4,16,139,128]{3,1,2,0:T(8,128)(2,1)}, u32[]{:S(2)}, u32[]{:S(2)}) async-start(bf16[4,16,139,128]{3,1,2,0:T(8,128)(2,1)} %copy.34), calls=%async_computation.3 | async-start | bytes 4554752 | tf_op jit(solution)/shard_map/all_to_all | solution.py:158
  40.8 2.1 %copy-start.4 = (f32[4,256]{1,0:T(4,128)S(1)}, f32[4,256]{1,0:T(4,128)}, u32[]{:S(2)}) copy-start(f32[4,256]{1,0:T(4,128)} %param.17) | copy-start | bytes 12292
  54.6 12.9 %copy-start.2 = (bf16[4,135,256]{2,1,0:T(8,128)(2,1)S(1)}, bf16[4,135,256]{2,1,0:T(8,128)(2,1)}, u32[]{:S(2)}) copy-start(bf16[4,135,256]{2,1,0:T(8,128)(2,1)} %copy.36) | copy-start | bytes 829444
  54.6 12.9 %copy-start.7 = (f32[1,256]{1,0:T(1,128)S(1)}, f32[1,256]{1,0:T(1,128)}, u32[]{:S(2)}) copy-start(f32[1,256]{1,0:T(1,128)} %get-tuple-element.66) | copy-start | bytes 3076
  54.6 12.9 %copy-start.8 = (f32[1,256]{1,0:T(1,128)S(1)}, f32[1,256]{1,0:T(1,128)}, u32[]{:S(2)}) copy-start(f32[1,256]{1,0:T(1,128)} %get-tuple-element.67) | copy-start | bytes 3076
  54.6 12.9 %copy-start.10 = (bf16[3,256,256]{2,1,0:T(8,128)(2,1)S(1)}, bf16[3,256,256]{2,1,0:T(8,128)(2,1)}, u32[]{:S(2)}) copy-start(bf16[3,256,256]{2,1,0:T(8,128)(2,1)} %param.18) | copy-start | bytes 1179652
  72.9 2.5 %copy-start.9 = (s32[1,16]{1,0:T(1,128)S(1)}, s32[1,16]{1,0:T(1,128)}, u32[]{:S(2)}) copy-start(s32[1,16]{1,0:T(1,128)} %constant_dynamic-slice_fusion) | copy-start | bytes 196
  76.2 8.9 %all-to-all-start.5 = ((f32[8,4,128]{2,1,0:T(4,128)}), f32[8,4,128]{2,1,0:T(4,128)S(1)}, u32[]{:S(2)}, u32[]{:S(2)}) async-start(f32[8,4,128]{2,1,0:T(4,128)} %bitcast.49), calls=%async_computation.5 | async-start | bytes 32768 | tf_op jit(solution)/shard_map/all_to_all | solution.py:171
  86.1 26.5 %all-to-all-start.1 = ((bf16[8,9,15,384]{3,2,1,0:T(8,128)(2,1)}), bf16[8,9,15,384]{3,2,1,0:T(8,128)(2,1)S(1)}, u32[]{:S(2)}, u32[]{:S(2)}) async-start(bf16[8,9,15,384]{3,2,1,0:T(8,128)(2,1)} %broadcast_in_dim.64), calls=%async_computation.1 | async-start | bytes 1769472 | tf_op jit(solution)/shard_map/all_to_all | solution.py:90
  112.7 29.7 %all-to-all-start.4 = ((bf16[16,9,4,15,128]{4,0,3,1,2:T(8,128)(2,1)}), bf16[16,9,4,15,128]{4,0,3,1,2:T(8,128)(2,1)S(1)}, u32[]{:S(2)}, u32[]{:S(2)}) async-start(bf16[16,9,4,15,128]{4,0,3,1,2:T(8,128)(2,1)} %copy.38), calls=%async_computation.4 | async-start | bytes 4423680 | tf_op jit(solution)/shard_map/all_to_all | solution.py:174
  143.3 26.5 %all-to-all-start.2 = ((bf16[8,9,15,384]{3,2,1,0:T(8,128)(2,1)}), bf16[8,9,15,384]{3,2,1,0:T(8,128)(2,1)S(1)}, u32[]{:S(2)}, u32[]{:S(2)}) async-start(bf16[8,9,15,384]{3,2,1,0:T(8,128)(2,1)} %broadcast_in_dim.65), calls=%async_computation.2 | async-start | bytes 1769472 | tf_op jit(solution)/shard_map/all_to_all | solution.py:90

commit v3 on v2

--- a/solution.py
+++ b/solution.py
@@ -86,8 +86,7 @@
 
 def exchange_halo(tracer, beside_all, patches):
     payload = edges_of(tracer)
-    sent = jnp.broadcast_to(payload[None], (patches,) + payload.shape)
-    got = lax.all_to_all(sent, "patch", split_axis=0, concat_axis=0, tiled=True)
+    got = lax.all_gather(payload, "patch", axis=0, tiled=False)
     rows = PX
     north = jnp.take(got, beside_all[0], axis=0)[..., PY : 2 * PY]
     south = jnp.take(got, beside_all[1], axis=0)[..., 0:PY]

time: 184 us -> 159 us (0.86)
  waiting for transfers between devices: 63.9 us -> 1.53 us
  blocking collectives: 0 us -> 48.9 us
  starting transfers between devices: 25.3 us -> 14.7 us
  local copies, waits for them, and re-layouts: 30.9 us -> 26.6 us
  other arithmetic: 15.2 us -> 19 us
    all_gather x0 -> x3, blocking collectives: none -> 48.9 us  [exchange_halo(): got = lax.all_gather(payload, 'patch', axis=0, tiled=False)]
    all_to_all x3 -> x0, waiting for transfers between devices: 46.6 us -> none  [exchange_halo(): got = lax.all_to_all(sent, 'patch', split_axis=0, concat_axis=0, tiled=True)]
    all_to_all x3 -> x0, starting transfers between devices: 13.5 us -> none  [exchange_halo(): got = lax.all_to_all(sent, 'patch', split_axis=0, concat_axis=0, tiled=True)]
    all_to_all x1, waiting for transfers between devices: 7.85 us -> 0.01 us  [on_device(): lax.all_to_all(by_quarter, 'grp', split_axis=0, concat_axis=0, tiled=True)]
    all_to_all x1, waiting for transfers between devices: 5.49 us -> 1.52 us  [on_device(): lax.all_to_all(packed, 'patch', split_axis=0, concat_axis=0, tiled=True)]
    all_to_all x1, waiting for transfers between devices: 3.91 us -> 0.01 us  [on_device(): lax.all_to_all(tendency, 'grp', split_axis=2, concat_axis=0, tiled=True)]
    broadcast_in_dim x3 -> x0, local copies, waits for them, and re-layouts: 2.99 us -> none  [exchange_halo(): sent = jnp.broadcast_to(payload[None], (patches,) + payload.shape)]
    all_to_all x1, starting transfers between devices: 3.34 us -> 5.32 us  [on_device(): lax.all_to_all(packed, 'patch', split_axis=0, concat_axis=0, tiled=True)]
  transfers between devices with their start and end apart: 6 -> 3, of which waited for: 6 -> 1; matrix products, arithmetic and copies ran while one was open for 20% -> 21% of each run, Pallas kernels for 11% -> 12%
where the time goes in v3:
time: 159 us; the launch traced here: 157 us
  blocking collectives  48.9 us (31%)
  Pallas kernels  29.4 us (18%)
  local copies, waits for them, and re-layouts  26.6 us (17%)
  other arithmetic  19 us (12%)
  starting transfers between devices  14.7 us (9%)
  between operations  8.76 us (6%)
  matrix products  8.59 us (5%)
    all_gather x3, blocking collectives, exchange_halo(): got = lax.all_gather(payload, 'patch', axis=0, tiled=False)  48.9 us
    pallas_call x3, Pallas kernels, stencil(): pl.pallas_call(functools.partial(stencil_kernel, with_tend=with_tend), gr...  29.4 us
    another operation x3, other arithmetic  9.31 us
    slice x3, local copies, waits for them, and re-layouts, edges_of(): tracer[..., PY - 1::PY]  5.84 us
    dot_general x2, matrix products, hidden_layers(): jnp.einsum('...h,hj->...j', hidden, w_mid[layer_index], preferred_element...  5.39 us
    all_to_all x1, starting transfers between devices, on_device(): lax.all_to_all(by_quarter, 'grp', split_axis=0, concat_axis=0, tiled=True)  5.32 us
    all_to_all x1, starting transfers between devices, on_device(): lax.all_to_all(packed, 'patch', split_axis=0, concat_axis=0, tiled=True)  5.32 us
    slice x3, local copies, waits for them, and re-layouts, edges_of(): tracer[..., 0::PY]  5.2 us
  transfers between devices with their start and end apart: 3, of which 1 were waited for; matrix products, arithmetic and copies ran while one was open for 21% of the time, Pallas kernels for 12%

profile of v3, /device:TPU:0, one launch (start us, length us, event | category | flops | bytes accessed | tf_op | source)
XLA Modules:
  0.0 157.5 jit_solution(2671778766023247707)
XLA Ops:
  0.6 0.9 copy.45
  1.5 2.6 %convert.42 = bf16[9,15,8192]{2,1,0:T(8,128)(2,1)S(1)} convert(f32[9,15,8192]{2,1,0:T(8,128)} %refs_0_.1) | non-fusion elementwise | flops 1105920 | bytes 6635520 | tf_op jit(solution)/shard_map/convert.35
  4.1 3.1 %convert_element_type.71 = bf16[135,4,16,128]{3,2,1,0:T(8,128)(2,1)} reshape(bf16[9,15,8192]{2,1,0:T(8,128)(2,1)S(1)} %convert.42) | data formatting | bytes 4423680 | tf_op jit(solution)/shard_map/convert_element_type | solution.py:132
  7.2 3.4 %copy_bitcast_fusion = bf16[4,16,139,128]{3,1,2,0:T(8,128)(2,1)} fusion(bf16[4,4,16,128]{3,2,1,0:T(8,128)(2,1)S(1)} %bitcast.130, bf16[135,4,16,128]{3,2,1,0:T(8,128)(2,1)} %convert_element_type.71), kind=kLoop, calls=%fused_computation.4 | loop fusion | flops 1138688 | bytes 4554752 | tf_op jit(solution)/shard_map/transpose | solution.py:137
  10.6 5.3 %all-to-all-start = ((bf16[4,16,139,128]{3,1,2,0:T(8,128)(2,1)}), bf16[4,16,139,128]{3,1,2,0:T(8,128)(2,1)}, u32[]{:S(2)}, u32[]{:S(2)}) async-start(bf16[4,16,139,128]{3,1,2,0:T(8,128)(2,1)} %copy_bitcast_fusion), calls=%async_computation | async-start | bytes 4554752 | tf_op jit(solution)/shard_map/all_to_all | solution.py:157
  24.4 1.2 slice.157
  25.6 1.2 slice.156
  26.9 16.8 %all_gather.12 = bf16[8,9,15,384]{3,2,1,0:T(8,128)(2,1)S(1)} all-gather(bf16[1,9,15,384]{3,2,1,0:T(8,128)(2,1)S(1)} %pad_maximum_fusion.1), channel_id=1, replica_groups=mesh['grp'=4,'patch'=8] {'patch'}, dimensions={0}, use_global_device_ids=true | all-gather | bytes 933120 | tf_op jit(solution)/shard_map/all_gather | solution.py:89
  45.2 9.7 %shard_map.113.refs_0_ = f32[9,15,8192]{2,1,0:T(8,128)} custom-call(f32[9,15,8192]{2,1,0:T(8,128)} %refs_0_.1, f32[15,8192]{1,0:T(8,128)} %refs_1_.5, f32[15,8192]{1,0:T(8,128)} %refs_2_.5, f32[9,15,384]{2,1,0:T(8,128)} %maximum_convert_fusion.refs_3_), custom_call_target="tpu_custom_call" | custom-call | flops 22118400 | bytes 9830400 | tf_op jit(solution)/shard_map/pallas_call | solution.py:67
  54.8 2.7 %convert.43 = bf16[9,15,8192]{2,1,0:T(8,128)(2,1)S(1)} convert(f32[9,15,8192]{2,1,0:T(8,128)} %shard_map.113.refs_0_) | non-fusion elementwise | flops 1105920 | bytes 6635520 | tf_op jit(solution)/shard_map/convert.23
  57.5 1.2 slice.169
  58.7 1.8 %slice.170 = bf16[9,15,64]{2,1,0:T(8,128)(2,1)} slice(bf16[9,15,8192]{2,1,0:T(8,128)(2,1)S(1)} %convert.43), slice={[0:9:1], [0:15:1], [127:8192:128]} | slice | bytes 34560 | tf_op jit(solution)/shard_map/slice | solution.py:82
  62.9 1.0 select_reduce_fusion
  63.9 0.9 pad_maximum_fusion.2
  64.8 16.6 %all_gather.13 = bf16[8,9,15,384]{3,2,1,0:T(8,128)(2,1)S(1)} all-gather(bf16[1,9,15,384]{3,2,1,0:T(8,128)(2,1)S(1)} %pad_maximum_fusion.2), channel_id=1, replica_groups=mesh['grp'=4,'patch'=8] {'patch'}, dimensions={0}, use_global_device_ids=true | all-gather | bytes 933120 | tf_op jit(solution)/shard_map/all_gather | solution.py:89
  81.5 0.9 fusion.41
  82.4 3.7 %multiply_convert_fusion.2 = bf16[16,128,256]{2,1,0:T(8,128)(2,1)S(1)} fusion(f32[256]{0:T(256)S(1)} %bitcast.141, bf16[4,16,139,128]{3,1,2,0:T(8,128)(2,1)} %all-to-all-done, f32[256]{0:T(256)S(1)} %bitcast.142, bf16[4,4,256]{2,1,0:T(4,128)(2,1)S(1)} %reshape.248, bf16[4,135,256]{2,1,0:T(8,128)(2,1)S(1)} %copy.38, bf16[3,256,256]{2,1,0:T(8,128)(2,1)S(1)} %copy-done.4), kind=kOutput, calls=%fused_computation.8 | convolution fusion | flops 858304512 | bytes 3745792 | tf_op jit(solution)/shard_map/...h,hj->...j/dot_general | solution.py:106
  86.1 1.7 %multiply_convert_fusion.1 = bf16[16,128,256]{2,1,0:T(8,128)(2,1)} fusion(bf16[16,128,256]{2,1,0:T(8,128)(2,1)S(1)} %multiply_convert_fusion.2, f32[256]{0:T(256)S(1)} %bitcast.140, bf16[3,256,256]{2,1,0:T(8,128)(2,1)S(1)} %copy-done.4), kind=kOutput, calls=%fused_computation.7 | convolution fusion | flops 271581184 | bytes 2229248 | tf_op jit(solution)/shard_map/...h,hj->...j/dot_general | solution.py:106
  87.8 2.5 %convert_bitcast_fusion = bf16[16,9,4,15,128]{4,3,2,1,0:T(8,128)(2,1)S(1)} fusion(bf16[256,9,4,15,1]{0,3,2,1,4:T(8,128)(2,1)S(1)} %reshape.544, bf16[16,128,256]{2,1,0:T(8,128)(2,1)} %multiply_convert_fusion.1, f32[256]{0:T(256)S(1)} %bitcast.139, bf16[3,256,256]{2,1,0:T(8,128)(2,1)} %param.18), kind=kOutput, calls=%fused_computation.2 | convolution fusion | flops 838918144 | bytes 3668992 | tf_op jit(solution)/shard_map/bch,hvgl->bvglc/dot_general | solution.py:163
  90.3 0.7 fusion.25
  91.0 5.3 %all-to-all-start.2 = ((f32[8,4,128]{2,1,0:T(4,128)}), f32[8,4,128]{2,1,0:T(4,128)S(1)}, u32[]{:S(2)}, u32[]{:S(2)}) async-start(f32[8,4,128]{2,1,0:T(4,128)} %bitcast.61), calls=%async_computation.2 | async-start | bytes 32768 | tf_op jit(solution)/shard_map/all_to_all | solution.py:170
  96.5 4.0 %copy.40 = bf16[16,9,4,15,128]{4,0,3,1,2:T(8,128)(2,1)} copy(bf16[16,9,4,15,128]{4,3,2,1,0:T(8,128)(2,1)S(1)} %convert_bitcast_fusion) | data formatting | bytes 4423680 | tf_op jit(solution)/shard_map/convert_element_type | solution.py:165
  100.5 1.5 all-to-all-done.2
  102.0 4.0 %all-to-all-start.1 = ((bf16[16,9,4,15,128]{4,0,3,1,2:T(8,128)(2,1)}), bf16[16,9,4,15,128]{4,0,3,1,2:T(8,128)(2,1)S(1)}, u32[]{:S(2)}, u32[]{:S(2)}) async-start(bf16[16,9,4,15,128]{4,0,3,1,2:T(8,128)(2,1)} %copy.40), calls=%async_computation.1 | async-start | bytes 4423680 | tf_op jit(solution)/shard_map/all_to_all | solution.py:173
  107.3 9.7 %shard_map.114.refs_0_ = f32[9,15,8192]{2,1,0:T(8,128)} custom-call(f32[9,15,8192]{2,1,0:T(8,128)} %shard_map.113.refs_0_, f32[15,8192]{1,0:T(8,128)} %refs_1_.5, f32[15,8192]{1,0:T(8,128)} %refs_2_.5, f32[9,15,384]{2,1,0:T(8,128)} %maximum_convert_fusion.1.refs_3_), custom_call_target="tpu_custom_call" | custom-call | flops 22118400 | bytes 9830400 | tf_op jit(solution)/shard_map/pallas_call | solution.py:67
  117.0 4.0 %convert.44 = bf16[9,15,8192]{2,1,0:T(8,128)(2,1)} convert(f32[9,15,8192]{2,1,0:T(8,128)} %shard_map.114.refs_0_) | non-fusion elementwise | flops 1105920 | bytes 6635520 | tf_op jit(solution)/shard_map/convert.11
  121.0 2.9 %slice.178 = bf16[9,15,64]{2,1,0:T(8,128)(2,1)S(1)} slice(bf16[9,15,8192]{2,1,0:T(8,128)(2,1)} %convert.44), slice={[0:9:1], [0:15:1], [0:8192:128]} | slice | bytes 34560 | tf_op jit(solution)/shard_map/slice | solution.py:82
  123.9 2.9 %slice.179 = bf16[9,15,64]{2,1,0:T(8,128)(2,1)S(1)} slice(bf16[9,15,8192]{2,1,0:T(8,128)(2,1)} %convert.44), slice={[0:9:1], [0:15:1], [127:8192:128]} | slice | bytes 34560 | tf_op jit(solution)/shard_map/slice | solution.py:82
  126.8 0.8 slice_bitcast_fusion.2
  127.7 15.5 %all_gather.14 = bf16[8,9,15,384]{3,2,1,0:T(8,128)(2,1)S(1)} all-gather(bf16[1,9,15,384]{3,2,1,0:T(8,128)(2,1)S(1)} %pad_maximum_fusion.3), channel_id=1, replica_groups=mesh['grp'=4,'patch'=8] {'patch'}, dimensions={0}, use_global_device_ids=true | all-gather | bytes 933120 | tf_op jit(solution)/shard_map/all_gather | solution.py:89
  144.7 2.0 %copy.41 = bf16[4,16,9,1,15,128]{5,4,2,1,0,3:T(8,128)(2,1)} copy(bf16[4,16,9,1,15,128]{5,1,4,2,0,3:T(8,128)(2,1)S(1)} %bitcast.124) | data formatting | bytes 4423680 | tf_op jit(solution)/shard_map/all_to_all | solution.py:173
  146.7 10.1 %shard_map.115 = f32[9,15,8192]{2,1,0:T(8,128)} custom-call(f32[9,15,8192]{2,1,0:T(8,128)} %shard_map.114.refs_0_, f32[15,8192]{1,0:T(8,128)} %refs_1_.5, f32[15,8192]{1,0:T(8,128)} %refs_2_.5, f32[9,15,384]{2,1,0:T(8,128)} %maximum_convert_fusion.2.refs_3_, bf16[64,9,15,128]{3,2,1,0:T(8,128)(2,1)} %bitcast.123), custom_call_target="tpu_custom_call" | custom-call | flops 22118400 | bytes 9830400 | tf_op jit(solution)/shard_map/pallas_call | solution.py:67
  (68 shorter events, 8.4 us)
Async XLA Ops:
  10.6 5.3 %copy-start.2 = (s32[8,4]{0,1:T(4,128)S(1)}, s32[8,4]{0,1:T(4,128)}, u32[]{:S(2)}) copy-start(s32[8,4]{0,1:T(4,128)} %param.21) | copy-start | bytes 388
  10.6 13.8 %copy-start = (bf16[556,256]{1,0:T(8,128)(2,1)S(1)}, bf16[556,256]{1,0:T(8,128)(2,1)}, u32[]{:S(2)}) copy-start(bf16[556,256]{1,0:T(8,128)(2,1)} %param.16) | copy-start | bytes 854020
  10.6 71.8 %all-to-all-start = ((bf16[4,16,139,128]{3,1,2,0:T(8,128)(2,1)}), bf16[4,16,139,128]{3,1,2,0:T(8,128)(2,1)}, u32[]{:S(2)}, u32[]{:S(2)}) async-start(bf16[4,16,139,128]{3,1,2,0:T(8,128)(2,1)} %copy_bitcast_fusion), calls=%async_computation | async-start | bytes 4554752 | tf_op jit(solution)/shard_map/all_to_all | solution.py:157
  54.8 6.1 %copy-start.3 = (s32[512,1]{0,1:T(1,128)S(1)}, s32[512,1]{0,1:T(1,128)}, u32[]{:S(2)}) copy-start(s32[512,1]{0,1:T(1,128)} %param.20) | copy-start | bytes 6148
  54.8 7.6 %slice-start = ((bf16[556,256]{1,0:T(8,128)(2,1)}), bf16[540,256]{1,0:T(8,128)(2,1)S(1)}, s32[]{:S(2)}) async-start(bf16[556,256]{1,0:T(8,128)(2,1)} %param.16), calls=%async_computation.3 | async-start | bytes 557056 | tf_op jit(solution)/shard_map/slice | solution.py:148
  57.5 5.3 %copy-start.1 = (bf16[256,540]{0,1:T(8,128)(2,1)S(1)}, bf16[256,540]{0,1:T(8,128)(2,1)}, u32[]{:S(2)}) copy-start(bf16[256,540]{0,1:T(8,128)(2,1)} %param.19) | copy-start | bytes 829444
  63.9 18.5 %copy-start.4 = (bf16[3,256,256]{2,1,0:T(8,128)(2,1)S(1)}, bf16[3,256,256]{2,1,0:T(8,128)(2,1)}, u32[]{:S(2)}) copy-start(bf16[3,256,256]{2,1,0:T(8,128)(2,1)} %param.18) | copy-start | bytes 1179652
  91.0 11.0 %all-to-all-start.2 = ((f32[8,4,128]{2,1,0:T(4,128)}), f32[8,4,128]{2,1,0:T(4,128)S(1)}, u32[]{:S(2)}, u32[]{:S(2)}) async-start(f32[8,4,128]{2,1,0:T(4,128)} %bitcast.61), calls=%async_computation.2 | async-start | bytes 32768 | tf_op jit(solution)/shard_map/all_to_all | solution.py:170
  102.0 42.7 %all-to-all-start.1 = ((bf16[16,9,4,15,128]{4,0,3,1,2:T(8,128)(2,1)}), bf16[16,9,4,15,128]{4,0,3,1,2:T(8,128)(2,1)S(1)}, u32[]{:S(2)}, u32[]{:S(2)}) async-start(bf16[16,9,4,15,128]{4,0,3,1,2:T(8,128)(2,1)} %copy.40), calls=%async_computation.1 | async-start | bytes 4423680 | tf_op jit(solution)/shard_map/all_to_all | solution.py:173

commit v4 on v3

--- a/solution.py
+++ b/solution.py
@@ -22,14 +22,17 @@
 
 def stencil_kernel(*refs, with_tend):
     if with_tend:
-        st_ref, cx_ref, cy_ref, rows_ref, tend_ref, out_ref = refs
+        st_ref, cx_ref, cy_ref, rows_ref, tend_ref, out_ref, erow_ref, ecol_ref, stack_ref = refs
     else:
-        st_ref, cx_ref, cy_ref, rows_ref, out_ref = refs
+        st_ref, cx_ref, cy_ref, rows_ref, out_ref, erow_ref, ecol_ref, stack_ref = refs
     rows = st_ref.shape[2] // PY
+    slot = stack_ref.shape[0] // rows
+    levels = st_ref.shape[1]
     north = rows_ref[0, :, 0:PY]
     south = rows_ref[0, :, PY : 2 * PY]
     sides = rows_ref[0, :, 2 * PY : 3 * PY]
     lane = lax.broadcasted_iota(jnp.int32, north.shape, 1)
+    stack_ref[...] = jnp.zeros(stack_ref.shape, stack_ref.dtype)
     for x in range(rows):
         here = slice(x * PY, (x + 1) * PY)
         cur = st_ref[0, :, here]
@@ -49,10 +52,26 @@
         if with_tend:
             val = val + PHYS_DT * tend_ref[x, 0].astype(jnp.float32)
         out_ref[0, :, here] = val
+        packed = val.astype(jnp.bfloat16)
+        stack_ref[x * slot : x * slot + levels, :] = packed
+        if x == 0:
+            erow_ref[0, :, 0:PY] = packed
+        if x == rows - 1:
+            erow_ref[0, :, PY : 2 * PY] = packed
+    pick_row = lax.broadcasted_iota(jnp.int32, (8, PY), 0)
+    pick_lane = lax.broadcasted_iota(jnp.int32, (8, PY), 1)
+    picker = (
+        ((pick_row == 0) & (pick_lane == 0)) | ((pick_row == 1) & (pick_lane == PY - 1))
+    ).astype(jnp.bfloat16)
+    ecol_ref[0] = lax.dot_general(
+        picker, stack_ref[...], (((1,), (1,)), ((), ())), preferred_element_type=jnp.float32
+    )
 
 
 def stencil(tracer, along_x, along_y, halo, tend):
     n_vars, levels, width = tracer.shape
+    rows = width // PY
+    slot = 16
     with_tend = tend is not None
     in_specs = [
         pl.BlockSpec((1, levels, width), lambda v: (v, 0, 0)),
@@ -68,30 +87,46 @@
         functools.partial(stencil_kernel, with_tend=with_tend),
         grid=(n_vars,),
         in_specs=in_specs,
-        out_specs=pl.BlockSpec((1, levels, width), lambda v: (v, 0, 0)),
-        out_shape=jax.ShapeDtypeStruct(tracer.shape, jnp.float32),
+        out_specs=[
+            pl.BlockSpec((1, levels, width), lambda v: (v, 0, 0)),
+            pl.BlockSpec((1, levels, 2 * PY), lambda v: (v, 0, 0)),
+            pl.BlockSpec((1, 8, rows * slot), lambda v: (v, 0, 0)),
+        ],
+        out_shape=[
+            jax.ShapeDtypeStruct(tracer.shape, jnp.float32),
+            jax.ShapeDtypeStruct((n_vars, levels, 2 * PY), jnp.bfloat16),
+            jax.ShapeDtypeStruct((n_vars, 8, rows * slot), jnp.float32),
+        ],
+        scratch_shapes=[pltpu.VMEM((rows * slot, PY), jnp.bfloat16)],
         cost_estimate=pl.CostEstimate(
             flops=20 * tracer.size, transcendentals=0, bytes_accessed=4 * (2 * tracer.size + 2 * along_x.size)
         ),
     )(*args)
 
 
-def edges_of(tracer):
-    width = tracer.shape[-1]
-    return jnp.concatenate(
-        [tracer[..., 0:PY], tracer[..., width - PY :], tracer[..., 0::PY], tracer[..., PY - 1 :: PY]],
-        axis=-1,
-    ).astype(jnp.bfloat16)
-
-
-def exchange_halo(tracer, beside_all, patches):
-    payload = edges_of(tracer)
+def first_edges(tracer):
+    n_vars, levels, width = tracer.shape
+    rows = width // PY
+    edge_rows = jnp.concatenate([tracer[..., 0:PY], tracer[..., width - PY :]], axis=-1)
+    edge_cols = jnp.stack([tracer[..., 0::PY], tracer[..., PY - 1 :: PY]], axis=1)
+    edge_cols = jnp.swapaxes(edge_cols, 2, 3)
+    edge_cols = jnp.pad(edge_cols, ((0, 0), (0, 0), (0, 0), (0, 16 - levels)))
+    return edge_rows.astype(jnp.bfloat16), edge_cols.reshape(n_vars, 2, rows * 16)
+
+
+def exchange_halo(edge_rows, edge_cols, beside_all, patches):
+    n_vars, levels, _ = edge_rows.shape
+    rows = PX
+    row_flat = edge_rows.astype(jnp.bfloat16).reshape(-1)
+    col_flat = edge_cols[:, 0:2].astype(jnp.bfloat16).reshape(-1)
+    payload = jnp.concatenate([row_flat, col_flat])
     got = lax.all_gather(payload, "patch", axis=0, tiled=False)
-    rows = PX
-    north = jnp.take(got, beside_all[0], axis=0)[..., PY : 2 * PY]
-    south = jnp.take(got, beside_all[1], axis=0)[..., 0:PY]
-    west = jnp.take(got, beside_all[2], axis=0)[..., 2 * PY + rows : 2 * PY + 2 * rows]
-    east = jnp.take(got, beside_all[3], axis=0)[..., 2 * PY : 2 * PY + rows]
+    rows_all = got[:, : row_flat.size].reshape((patches,) + edge_rows.shape)
+    cols_all = got[:, row_flat.size :].reshape(patches, n_vars, 2, rows, 16)
+    north = jnp.take(rows_all, beside_all[0], axis=0)[..., PY : 2 * PY]
+    south = jnp.take(rows_all, beside_all[1], axis=0)[..., 0:PY]
+    west = jnp.swapaxes(jnp.take(cols_all, beside_all[2], axis=0)[:, 1, :, 0:levels], 1, 2)
+    east = jnp.swapaxes(jnp.take(cols_all, beside_all[3], axis=0)[:, 0, :, 0:levels], 1, 2)
     sides = jnp.stack([west, jnp.roll(east, -1, axis=-1)], axis=-1).reshape(west.shape[:-1] + (2 * rows,))
     return jnp.concatenate([north, south, sides], axis=-1).astype(jnp.float32)
 
@@ -173,10 +208,11 @@
     arrived = lax.all_to_all(tendency, "grp", split_axis=2, concat_axis=0, tiled=True)
     tendency_here = arrived.reshape(PX, VARS, level_share, PY)
     advected = state
+    edge_rows, edge_cols = first_edges(state)
     for section_index in range(SUBSTEPS):
-        halo = exchange_halo(advected, beside_all, patches)
+        halo = exchange_halo(edge_rows, edge_cols, beside_all, patches)
         last = section_index == SUBSTEPS - 1
-        advected = stencil(
+        advected, edge_rows, edge_cols = stencil(
             advected, courant_x, courant_y, halo, tendency_here if last else None
         )
     new_state = advected

time: 159 us -> 171 us (1.075)
  blocking collectives: 48.9 us -> 62.3 us
  other arithmetic: 19 us -> 9.61 us
  local copies, waits for them, and re-layouts: 26.6 us -> 32.7 us
  matrix products: 8.59 us -> 10.8 us
    all_gather x3, blocking collectives: 48.9 us -> 62.3 us  [exchange_halo(): got = lax.all_gather(payload, 'patch', axis=0, tiled=False)]
    reshape x0 -> x5, local copies, waits for them, and re-layouts: none -> 9.05 us  [the longest x3 7.18 us: exchange_halo(): cols_all = got[:, row_flat.size:].reshape(patches, n_vars, 2, rows, 16)]
    slice x13 -> x16, local copies, waits for them, and re-layouts: 11.7 us -> 3.14 us  [the longest x2 2.31 us: first_edges(): edge_cols = jnp.stack([tracer[..., 0::PY], tracer[..., PY - 1::PY]], axis=1)]
    another operation x3 -> x1, other arithmetic: 9.31 us -> 2.62 us
    unnamed x13 -> x26, local copies, waits for them, and re-layouts: 1.99 us -> 4.89 us
    dot_general x2, matrix products: 5.39 us -> 7.6 us  [hidden_layers(): jnp.einsum('...h,hj->...j', hidden, w_mid[layer_index], preferred_element...]
    transpose x0 -> x4, local copies, waits for them, and re-layouts: none -> 1.85 us  [the longest x1 1.82 us: on_device(): features.reshape(feat_share, groups, quarter_rows, PY).transpose(1, 2, 0, 3)]
    all_to_all x1, starting transfers between devices: 5.32 us -> 3.56 us  [on_device(): lax.all_to_all(packed, 'patch', split_axis=0, concat_axis=0, tiled=True)]
  transfers between devices with their start and end apart: 3 -> 3, of which waited for: 1 -> 1; matrix products, arithmetic and copies ran while one was open for 21% -> 17% of each run, Pallas kernels for 12% -> 12%
where the time goes in v4:
time: 171 us; the launch traced here: 169 us
  blocking collectives  62.3 us (36%)
  local copies, waits for them, and re-layouts  32.7 us (19%)
  Pallas kernels  30.6 us (18%)
  starting transfers between devices  13 us (8%)
  matrix products  10.8 us (6%)
  other arithmetic  9.61 us (6%)
  between operations  9.02 us (5%)
    all_gather x3, blocking collectives, exchange_halo(): got = lax.all_gather(payload, 'patch', axis=0, tiled=False)  62.3 us
    pallas_call x3, Pallas kernels, stencil(): pl.pallas_call(functools.partial(stencil_kernel, with_tend=with_tend), gr...  30.6 us
    dot_general x2, matrix products, hidden_layers(): jnp.einsum('...h,hj->...j', hidden, w_mid[layer_index], preferred_element...  7.6 us
    reshape x3, local copies, waits for them, and re-layouts, exchange_halo(): cols_all = got[:, row_flat.size:].reshape(patches, n_vars, 2, rows, 16)  7.18 us
    all_to_all x1, starting transfers between devices, on_device(): lax.all_to_all(by_quarter, 'grp', split_axis=0, concat_axis=0, tiled=True)  5.32 us
    unnamed x26, local copies, waits for them, and re-layouts  4.89 us
    all_to_all x1, starting transfers between devices, on_device(): lax.all_to_all(tendency, 'grp', split_axis=2, concat_axis=0, tiled=True)  4.1 us
    convert_element_type x1, local copies, waits for them, and re-layouts, on_device(): tendency = jnp.einsum('bch,hvgl->bvglc', hidden, w_split, preferred_eleme...  3.95 us
  transfers between devices with their start and end apart: 3, of which 1 were waited for; matrix products, arithmetic and copies ran while one was open for 17% of the time, Pallas kernels for 12%

profile of v4, /device:TPU:0, one launch (start us, length us, event | category | flops | bytes accessed | tf_op | source)
XLA Modules:
  0.0 169.3 jit_solution(14839732337861145746)
XLA Ops:
  0.6 0.9 copy.145
  1.5 2.6 %convert.21 = bf16[9,15,8192]{2,1,0:T(8,128)(2,1)S(1)} convert(f32[9,15,8192]{2,1,0:T(8,128)} %refs_0_.1) | non-fusion elementwise | flops 1105920 | bytes 6635520 | tf_op jit(solution)/shard_map/convert.14
  4.1 3.1 %convert_element_type.63 = bf16[135,4,16,128]{3,2,1,0:T(8,128)(2,1)} reshape(bf16[9,15,8192]{2,1,0:T(8,128)(2,1)S(1)} %convert.21) | data formatting | bytes 4423680 | tf_op jit(solution)/shard_map/convert_element_type | solution.py:167
  7.2 1.8 %maximum_bitcast_fusion = bf16[4,16,139,128]{3,1,0,2:T(8,128)(2,1)S(1)} fusion(bf16[4,4,16,128]{3,2,1,0:T(8,128)(2,1)S(1)} %bitcast.169, bf16[135,4,16,128]{3,2,1,0:T(8,128)(2,1)} %convert_element_type.63), kind=kLoop, calls=%fused_computation.3 | loop fusion | flops 1138688 | bytes 4554752 | tf_op jit(solution)/shard_map/transpose | solution.py:172
  9.0 1.8 %copy.125 = bf16[4,16,139,128]{3,1,2,0:T(8,128)(2,1)} copy(bf16[4,16,139,128]{3,1,0,2:T(8,128)(2,1)S(1)} %maximum_bitcast_fusion) | data formatting | bytes 4554752 | tf_op jit(solution)/shard_map/transpose | solution.py:172
  10.8 5.3 %all-to-all-start = ((bf16[4,16,139,128]{3,1,2,0:T(8,128)(2,1)}), bf16[4,16,139,128]{3,1,2,0:T(8,128)(2,1)}, u32[]{:S(2)}, u32[]{:S(2)}) async-start(bf16[4,16,139,128]{3,1,2,0:T(8,128)(2,1)} %copy.125), calls=%async_computation | async-start | bytes 4554752 | tf_op jit(solution)/shard_map/all_to_all | solution.py:192
  24.5 1.2 slice.151
  25.7 1.2 slice.150
  27.6 22.3 %all-gather.3 = bf16[8,1,52992]{2,1,0:T(2,128)(2,1)S(1)} all-gather(bf16[1,1,52992]{2,1,0:T(2,128)(2,1)S(1)} %reshape.423), channel_id=2, replica_groups=mesh['grp'=4,'patch'=8] {'patch'}, dimensions={0}, use_global_device_ids=true | all-gather | bytes 953856 | tf_op jit(solution)/shard_map/all_gather | solution.py:123
  50.1 1.9 %reshape.105 = bf16[8,9,2,64,16]{4,3,2,1,0:T(8,128)(2,1)S(1)} reshape(bf16[8,18432]{1,0:T(8,128)(2,1)S(1)} %slice.250) | data formatting | bytes 589824 | tf_op jit(solution)/shard_map/reshape | solution.py:125
  53.8 0.7 maximum_convert_fusion.refs_3_
  54.5 10.1 %shard_map.113 = (f32[9,15,8192]{2,1,0:T(8,128)}, bf16[9,15,256]{2,1,0:T(8,128)(2,1)}, f32[9,8,1024]{2,1,0:T(8,128)}) custom-call(f32[9,15,8192]{2,1,0:T(8,128)} %refs_0_.1, f32[15,8192]{1,0:T(8,128)} %refs_1_.5, f32[15,8192]{1,0:T(8,128)} %refs_2_.5, f32[9,15,384]{2,1,0:T(8,128)} %maximum_convert_fusion.refs_3_), custom_call_target="tpu_custom_call" | custom-call | flops 22118400 | bytes 9830400 | tf_op jit(solution)/shard_map/pallas_call | solution.py:86
  64.5 1.0 fusion.27
  65.5 0.9 reshape.107
  66.6 19.8 %all-gather.4 = bf16[8,1,52992]{2,1,0:T(2,128)(2,1)S(1)} all-gather(bf16[1,1,52992]{2,1,0:T(2,128)(2,1)S(1)} %reshape.425), channel_id=3, replica_groups=mesh['grp'=4,'patch'=8] {'patch'}, dimensions={0}, use_global_device_ids=true | all-gather | bytes 953856 | tf_op jit(solution)/shard_map/all_gather | solution.py:123
  86.6 1.9 %reshape.110 = bf16[8,9,2,64,16]{4,3,2,1,0:T(8,128)(2,1)S(1)} reshape(bf16[8,18432]{1,0:T(8,128)(2,1)S(1)} %slice.259) | data formatting | bytes 589824 | tf_op jit(solution)/shard_map/reshape | solution.py:125
  92.8 10.1 %shard_map.114 = (f32[9,15,8192]{2,1,0:T(8,128)}, bf16[9,15,256]{2,1,0:T(8,128)(2,1)}, f32[9,8,1024]{2,1,0:T(8,128)}) custom-call(f32[9,15,8192]{2,1,0:T(8,128)} %get-tuple-element.11.refs_0_, f32[15,8192]{1,0:T(8,128)} %refs_1_.5, f32[15,8192]{1,0:T(8,128)} %refs_2_.5, f32[9,15,384]{2,1,0:T(8,128)} %maximum_convert_fusion.1.refs_3_), custom_call_target="tpu_custom_call" | custom-call | flops 22118400 | bytes 9830400 | tf_op jit(solution)/shard_map/pallas_call | solution.py:86
  103.0 1.0 fusion.28
  104.0 0.9 reshape.112
  105.2 4.7 %multiply_convert_fusion.2 = bf16[16,128,256]{2,1,0:T(8,128)(2,1)} fusion(f32[256]{0:T(256)S(1)} %bitcast.178, bf16[4,16,139,128]{3,1,2,0:T(8,128)(2,1)} %all-to-all-done, f32[256]{0:T(256)S(1)} %bitcast.179, bf16[4,4,256]{2,1,0:T(4,128)(2,1)S(1)} %reshape.119, bf16[4,135,256]{2,1,0:T(8,128)(2,1)S(1)} %copy.127, bf16[3,256,256]{2,1,0:T(8,128)(2,1)S(1)} %copy-done.5), kind=kOutput, calls=%fused_computation.7 | convolution fusion | flops 858304512 | bytes 3745792 | tf_op jit(solution)/shard_map/...h,hj->...j/dot_general | solution.py:141
  109.9 2.9 %multiply_convert_fusion.1 = bf16[16,128,256]{2,1,0:T(8,128)(2,1)} fusion(bf16[16,128,256]{2,1,0:T(8,128)(2,1)} %multiply_convert_fusion.2, f32[256]{0:T(256)S(1)} %bitcast.177, bf16[3,256,256]{2,1,0:T(8,128)(2,1)S(1)} %copy-done.5), kind=kOutput, calls=%fused_computation.6 | convolution fusion | flops 271581184 | bytes 2229248 | tf_op jit(solution)/shard_map/...h,hj->...j/dot_general | solution.py:141
  112.8 2.5 %convert_bitcast_fusion = bf16[16,9,4,15,128]{4,3,2,1,0:T(8,128)(2,1)S(1)} fusion(bf16[256,9,4,15,1]{0,3,2,1,4:T(8,128)(2,1)S(1)} %reshape.450, bf16[16,128,256]{2,1,0:T(8,128)(2,1)} %multiply_convert_fusion.1, f32[256]{0:T(256)S(1)} %bitcast.176, bf16[3,256,256]{2,1,0:T(8,128)(2,1)S(1)} %copy-done.5), kind=kOutput, calls=%fused_computation.2 | convolution fusion | flops 838918144 | bytes 3687424 | tf_op jit(solution)/shard_map/bch,hvgl->bvglc/dot_general | solution.py:198
  115.3 0.7 fusion.33
  116.1 3.6 %all-to-all-start.2 = ((f32[8,4,128]{2,1,0:T(4,128)}), f32[8,4,128]{2,1,0:T(4,128)S(1)}, u32[]{:S(2)}, u32[]{:S(2)}) async-start(f32[8,4,128]{2,1,0:T(4,128)} %bitcast.70), calls=%async_computation.2 | async-start | bytes 32768 | tf_op jit(solution)/shard_map/all_to_all | solution.py:205
  119.8 3.9 %copy.129 = bf16[16,9,4,15,128]{4,0,3,1,2:T(8,128)(2,1)} copy(bf16[16,9,4,15,128]{4,3,2,1,0:T(8,128)(2,1)S(1)} %convert_bitcast_fusion) | data formatting | bytes 4423680 | tf_op jit(solution)/shard_map/convert_element_type | solution.py:200
  123.7 1.3 all-to-all-done.2
  125.0 4.1 %all-to-all-start.1 = ((bf16[16,9,4,15,128]{4,0,3,1,2:T(8,128)(2,1)}), bf16[16,9,4,15,128]{4,0,3,1,2:T(8,128)(2,1)S(1)}, u32[]{:S(2)}, u32[]{:S(2)}) async-start(bf16[16,9,4,15,128]{4,0,3,1,2:T(8,128)(2,1)} %copy.129), calls=%async_computation.1 | async-start | bytes 4423680 | tf_op jit(solution)/shard_map/all_to_all | solution.py:208
  129.1 20.2 %all-gather.5 = bf16[8,1,52992]{2,1,0:T(2,128)(2,1)S(1)} all-gather(bf16[1,1,52992]{2,1,0:T(2,128)(2,1)S(1)} %reshape.427), channel_id=4, replica_groups=mesh['grp'=4,'patch'=8] {'patch'}, dimensions={0}, use_global_device_ids=true | all-gather | bytes 953856 | tf_op jit(solution)/shard_map/all_gather | solution.py:123
  149.4 3.3 %reshape.115 = bf16[8,9,2,64,16]{4,3,2,1,0:T(8,128)(2,1)} reshape(bf16[8,18432]{1,0:T(8,128)(2,1)S(1)} %slice.268) | data formatting | bytes 589824 | tf_op jit(solution)/shard_map/reshape | solution.py:125
  152.8 1.1 select_bitcast_fusion.1
  156.2 2.1 %copy.130 = bf16[4,16,9,1,15,128]{5,4,2,1,0,3:T(8,128)(2,1)} copy(bf16[4,16,9,1,15,128]{5,1,4,2,0,3:T(8,128)(2,1)S(1)} %bitcast.154) | data formatting | bytes 4423680 | tf_op jit(solution)/shard_map/all_to_all | solution.py:208
  158.3 10.4 %shard_map.115 = (f32[9,15,8192]{2,1,0:T(8,128)}, bf16[9,15,256]{2,1,0:T(8,128)(2,1)}, f32[9,8,1024]{2,1,0:T(8,128)}) custom-call(f32[9,15,8192]{2,1,0:T(8,128)} %get-tuple-element.14.refs_0_, f32[15,8192]{1,0:T(8,128)} %refs_1_.5, f32[15,8192]{1,0:T(8,128)} %refs_2_.5, f32[9,15,384]{2,1,0:T(8,128)} %maximum_convert_fusion.2.refs_3_, ...), custom_call_target="tpu_custom_call" | custom-call | flops 22118400 | bytes 9830400 | tf_op jit(solution)/shard_map/pallas_call | solution.py:86
  (111 shorter events, 11.0 us)
Async XLA Ops:
  10.8 5.3 %copy-start.3 = (s32[8,4]{0,1:T(4,128)S(1)}, s32[8,4]{0,1:T(4,128)}, u32[]{:S(2)}) copy-start(s32[8,4]{0,1:T(4,128)} %param.23) | copy-start | bytes 388
  10.8 13.7 %copy-start = (bf16[556,256]{1,0:T(8,128)(2,1)S(1)}, bf16[556,256]{1,0:T(8,128)(2,1)}, u32[]{:S(2)}) copy-start(bf16[556,256]{1,0:T(8,128)(2,1)} %param.18) | copy-start | bytes 854020
  10.8 94.3 %all-to-all-start = ((bf16[4,16,139,128]{3,1,2,0:T(8,128)(2,1)}), bf16[4,16,139,128]{3,1,2,0:T(8,128)(2,1)}, u32[]{:S(2)}, u32[]{:S(2)}) async-start(bf16[4,16,139,128]{3,1,2,0:T(8,128)(2,1)} %copy.125), calls=%async_computation | async-start | bytes 4554752 | tf_op jit(solution)/shard_map/all_to_all | solution.py:192
  86.6 2.7 %copy-start.4 = (s32[512,1]{0,1:T(1,128)S(1)}, s32[512,1]{0,1:T(1,128)}, u32[]{:S(2)}) copy-start(s32[512,1]{0,1:T(1,128)} %param.22) | copy-start | bytes 6148
  86.6 3.5 %slice-start = ((bf16[556,256]{1,0:T(8,128)(2,1)}), bf16[540,256]{1,0:T(8,128)(2,1)S(1)}, s32[]{:S(2)}) async-start(bf16[556,256]{1,0:T(8,128)(2,1)} %param.18), calls=%async_computation.3 | async-start | bytes 557056 | tf_op jit(solution)/shard_map/slice | solution.py:183
  88.6 1.8 %copy-start.1 = (bf16[256,540]{0,1:T(8,128)(2,1)S(1)}, bf16[256,540]{0,1:T(8,128)(2,1)}, u32[]{:S(2)}) copy-start(bf16[256,540]{0,1:T(8,128)(2,1)} %param.21) | copy-start | bytes 829444
  92.8 12.3 %copy-start.2 = (f32[4,256]{1,0:T(4,128)S(1)}, f32[4,256]{1,0:T(4,128)}, u32[]{:S(2)}) copy-start(f32[4,256]{1,0:T(4,128)} %param.19) | copy-start | bytes 12292
  92.8 12.4 %copy-start.5 = (bf16[3,256,256]{2,1,0:T(8,128)(2,1)S(1)}, bf16[3,256,256]{2,1,0:T(8,128)(2,1)}, u32[]{:S(2)}) copy-start(bf16[3,256,256]{2,1,0:T(8,128)(2,1)} %param.20) | copy-start | bytes 1179652
  116.1 8.9 %all-to-all-start.2 = ((f32[8,4,128]{2,1,0:T(4,128)}), f32[8,4,128]{2,1,0:T(4,128)S(1)}, u32[]{:S(2)}, u32[]{:S(2)}) async-start(f32[8,4,128]{2,1,0:T(4,128)} %bitcast.70), calls=%async_computation.2 | async-start | bytes 32768 | tf_op jit(solution)/shard_map/all_to_all | solution.py:205
  125.0 31.2 %all-to-all-start.1 = ((bf16[16,9,4,15,128]{4,0,3,1,2:T(8,128)(2,1)}), bf16[16,9,4,15,128]{4,0,3,1,2:T(8,128)(2,1)S(1)}, u32[]{:S(2)}, u32[]{:S(2)}) async-start(bf16[16,9,4,15,128]{4,0,3,1,2:T(8,128)(2,1)} %copy.129), calls=%async_computation.1 | async-start | bytes 4423680 | tf_op jit(solution)/shard_map/all_to_all | solution.py:208

commit v5 on v4

--- a/solution.py
+++ b/solution.py
@@ -22,9 +22,9 @@
 
 def stencil_kernel(*refs, with_tend):
     if with_tend:
-        st_ref, cx_ref, cy_ref, rows_ref, tend_ref, out_ref, erow_ref, ecol_ref, stack_ref = refs
+        st_ref, cx_ref, cy_ref, rows_ref, tend_ref, out_ref, pay_ref, stack_ref = refs
     else:
-        st_ref, cx_ref, cy_ref, rows_ref, out_ref, erow_ref, ecol_ref, stack_ref = refs
+        st_ref, cx_ref, cy_ref, rows_ref, out_ref, pay_ref, stack_ref = refs
     rows = st_ref.shape[2] // PY
     slot = stack_ref.shape[0] // rows
     levels = st_ref.shape[1]
@@ -55,17 +55,27 @@
         packed = val.astype(jnp.bfloat16)
         stack_ref[x * slot : x * slot + levels, :] = packed
         if x == 0:
-            erow_ref[0, :, 0:PY] = packed
+            pay_ref[0, 0:levels, 0:PY] = packed
         if x == rows - 1:
-            erow_ref[0, :, PY : 2 * PY] = packed
-    pick_row = lax.broadcasted_iota(jnp.int32, (8, PY), 0)
-    pick_lane = lax.broadcasted_iota(jnp.int32, (8, PY), 1)
-    picker = (
-        ((pick_row == 0) & (pick_lane == 0)) | ((pick_row == 1) & (pick_lane == PY - 1))
-    ).astype(jnp.bfloat16)
-    ecol_ref[0] = lax.dot_general(
-        picker, stack_ref[...], (((1,), (1,)), ((), ())), preferred_element_type=jnp.float32
-    )
+            pay_ref[0, 0:levels, PY : 2 * PY] = packed
+    pad_rows = pay_ref.shape[1] - levels
+    if pad_rows:
+        pay_ref[0, levels:, 0 : 2 * PY] = jnp.zeros((pad_rows, 2 * PY), pay_ref.dtype)
+    chunks = stack_ref.shape[0] // PY
+    pick_row = lax.broadcasted_iota(jnp.int32, (2 * chunks, PY), 0)
+    pick_lane = lax.broadcasted_iota(jnp.int32, (2 * chunks, PY), 1)
+    cols = jnp.zeros((2 * chunks, PY), jnp.float32)
+    for j in range(chunks):
+        picker = (
+            ((pick_row == 2 * j) & (pick_lane == 0)) | ((pick_row == 2 * j + 1) & (pick_lane == PY - 1))
+        ).astype(jnp.bfloat16)
+        cols = cols + lax.dot_general(
+            picker,
+            stack_ref[j * PY : (j + 1) * PY, :],
+            (((1,), (1,)), ((), ())),
+            preferred_element_type=jnp.float32,
+        )
+    pay_ref[0, :, 2 * PY : 3 * PY] = cols.astype(pay_ref.dtype)
 
 
 def stencil(tracer, along_x, along_y, halo, tend):
@@ -89,13 +99,11 @@
         in_specs=in_specs,
         out_specs=[
             pl.BlockSpec((1, levels, width), lambda v: (v, 0, 0)),
-            pl.BlockSpec((1, levels, 2 * PY), lambda v: (v, 0, 0)),
-            pl.BlockSpec((1, 8, rows * slot), lambda v: (v, 0, 0)),
+            pl.BlockSpec((1, slot, 3 * PY), lambda v: (v, 0, 0)),
         ],
         out_shape=[
             jax.ShapeDtypeStruct(tracer.shape, jnp.float32),
-            jax.ShapeDtypeStruct((n_vars, levels, 2 * PY), jnp.bfloat16),
-            jax.ShapeDtypeStruct((n_vars, 8, rows * slot), jnp.float32),
+            jax.ShapeDtypeStruct((n_vars, slot, 3 * PY), jnp.bfloat16),
         ],
         scratch_shapes=[pltpu.VMEM((rows * slot, PY), jnp.bfloat16)],
         cost_estimate=pl.CostEstimate(
@@ -107,26 +115,32 @@
 def first_edges(tracer):
     n_vars, levels, width = tracer.shape
     rows = width // PY
+    slot = 16
+    chunk_rows = PY // slot
     edge_rows = jnp.concatenate([tracer[..., 0:PY], tracer[..., width - PY :]], axis=-1)
+    edge_rows = jnp.pad(edge_rows, ((0, 0), (0, slot - levels), (0, 0)))
     edge_cols = jnp.stack([tracer[..., 0::PY], tracer[..., PY - 1 :: PY]], axis=1)
-    edge_cols = jnp.swapaxes(edge_cols, 2, 3)
-    edge_cols = jnp.pad(edge_cols, ((0, 0), (0, 0), (0, 0), (0, 16 - levels)))
-    return edge_rows.astype(jnp.bfloat16), edge_cols.reshape(n_vars, 2, rows * 16)
-
-
-def exchange_halo(edge_rows, edge_cols, beside_all, patches):
-    n_vars, levels, _ = edge_rows.shape
+    edge_cols = jnp.pad(edge_cols, ((0, 0), (0, 0), (0, slot - levels), (0, 0)))
+    edge_cols = edge_cols.reshape(n_vars, 2, slot, rows // chunk_rows, chunk_rows)
+    edge_cols = edge_cols.transpose(0, 3, 1, 4, 2).reshape(n_vars, 2 * rows // chunk_rows, PY)
+    return jnp.concatenate([edge_rows, edge_cols], axis=-1).astype(jnp.bfloat16)
+
+
+def exchange_halo(payload, beside_all, patches, levels):
+    n_vars, slot, _ = payload.shape
     rows = PX
-    row_flat = edge_rows.astype(jnp.bfloat16).reshape(-1)
-    col_flat = edge_cols[:, 0:2].astype(jnp.bfloat16).reshape(-1)
-    payload = jnp.concatenate([row_flat, col_flat])
+    chunk_rows = PY // slot
     got = lax.all_gather(payload, "patch", axis=0, tiled=False)
-    rows_all = got[:, : row_flat.size].reshape((patches,) + edge_rows.shape)
-    cols_all = got[:, row_flat.size :].reshape(patches, n_vars, 2, rows, 16)
-    north = jnp.take(rows_all, beside_all[0], axis=0)[..., PY : 2 * PY]
-    south = jnp.take(rows_all, beside_all[1], axis=0)[..., 0:PY]
-    west = jnp.swapaxes(jnp.take(cols_all, beside_all[2], axis=0)[:, 1, :, 0:levels], 1, 2)
-    east = jnp.swapaxes(jnp.take(cols_all, beside_all[3], axis=0)[:, 0, :, 0:levels], 1, 2)
+    north = jnp.take(got, beside_all[0], axis=0)[:, 0:levels, PY : 2 * PY]
+    south = jnp.take(got, beside_all[1], axis=0)[:, 0:levels, 0:PY]
+
+    def column(patch, which):
+        cols = jnp.take(got, patch, axis=0)[..., 2 * PY : 3 * PY]
+        cols = cols.reshape(n_vars, rows // chunk_rows, 2, chunk_rows, slot)[:, :, which]
+        return cols.transpose(0, 3, 1, 2).reshape(n_vars, slot, rows)[:, 0:levels]
+
+    west = column(beside_all[2], 1)
+    east = column(beside_all[3], 0)
     sides = jnp.stack([west, jnp.roll(east, -1, axis=-1)], axis=-1).reshape(west.shape[:-1] + (2 * rows,))
     return jnp.concatenate([north, south, sides], axis=-1).astype(jnp.float32)
 
@@ -208,11 +222,11 @@
     arrived = lax.all_to_all(tendency, "grp", split_axis=2, concat_axis=0, tiled=True)
     tendency_here = arrived.reshape(PX, VARS, level_share, PY)
     advected = state
-    edge_rows, edge_cols = first_edges(state)
+    payload = first_edges(state)
     for section_index in range(SUBSTEPS):
-        halo = exchange_halo(edge_rows, edge_cols, beside_all, patches)
+        halo = exchange_halo(payload, beside_all, patches, level_share)
         last = section_index == SUBSTEPS - 1
-        advected, edge_rows, edge_cols = stencil(
+        advected, payload = stencil(
             advected, courant_x, courant_y, halo, tendency_here if last else None
         )
     new_state = advected

time: 171 us -> 194 us (1.13)
  local copies, waits for them, and re-layouts: 32.7 us -> 69.8 us
  blocking collectives: 62.3 us -> 48.7 us
    another operation x3 -> x1, local copies, waits for them, and re-layouts: 0.88 us -> 14.8 us  [exchange_halo(): north = jnp.take(rows_all, beside_all[0], axis=0)[..., PY:2 * PY]]
    all_gather x3, blocking collectives: 62.3 us -> 48.7 us  [exchange_halo(): got = lax.all_gather(payload, 'patch', axis=0, tiled=False)]
    unnamed x26 -> x16, local copies, waits for them, and re-layouts: 4.89 us -> 17.2 us
    slice x2, local copies, waits for them, and re-layouts: 2.31 us -> 13.9 us  [first_edges(): edge_cols = jnp.stack([tracer[..., 0::PY], tracer[..., PY - 1::PY]], axis=1)]
    reshape x5 -> x12, local copies, waits for them, and re-layouts: 9.05 us -> 1.49 us  [the longest x6 1.32 us: column(): cols.reshape(n_vars, rows // chunk_rows, 2, chunk_rows, slot)[:, :, which]]
    slice x13 -> x17, local copies, waits for them, and re-layouts: 0.81 us -> 3.58 us  [the longest x4 2.15 us: exchange_halo(): north = jnp.take(got, beside_all[0], axis=0)[:, 0:levels, PY:2 * PY]]
    another operation x1 -> x0, other arithmetic: 2.62 us -> none
  transfers between devices with their start and end apart: 3 -> 3, of which waited for: 1 -> 1; matrix products, arithmetic and copies ran while one was open for 17% -> 19% of each run, Pallas kernels for 12% -> 11%
where the time goes in v5:
time: 194 us; the launch traced here: 191 us
  local copies, waits for them, and re-layouts  69.8 us (36%)
  blocking collectives  48.7 us (25%)
  Pallas kernels  30.6 us (16%)
  starting transfers between devices  14.9 us (8%)
  matrix products  10.2 us (5%)
  between operations  9.03 us (5%)
  other arithmetic  7.8 us (4%)
    all_gather x3, blocking collectives, exchange_halo(): got = lax.all_gather(payload, 'patch', axis=0, tiled=False)  48.7 us
    pallas_call x3, Pallas kernels, stencil(): pl.pallas_call(functools.partial(stencil_kernel, with_tend=with_tend), gr...  30.6 us
    unnamed x16, local copies, waits for them, and re-layouts  17.2 us
    another operation x1, local copies, waits for them, and re-layouts  14.8 us
    slice x2, local copies, waits for them, and re-layouts, first_edges(): edge_cols = jnp.stack([tracer[..., 0::PY], tracer[..., PY - 1::PY]], axis=1)  13.9 us
    dot_general x2, matrix products, hidden_layers(): jnp.einsum('...h,hj->...j', hidden, w_mid[layer_index], preferred_element...  6.97 us
    all_to_all x1, starting transfers between devices, on_device(): lax.all_to_all(packed, 'patch', split_axis=0, concat_axis=0, tiled=True)  5.33 us
    all_to_all x1, starting transfers between devices, on_device(): lax.all_to_all(by_quarter, 'grp', split_axis=0, concat_axis=0, tiled=True)  5.32 us
  transfers between devices with their start and end apart: 3, of which 1 were waited for; matrix products, arithmetic and copies ran while one was open for 19% of the time, Pallas kernels for 11%

profile of v5, /device:TPU:0, one launch (start us, length us, event | category | flops | bytes accessed | tf_op | source)
XLA Modules:
  0.0 191.3 jit_solution(6825410764640726854)
XLA Ops:
  0.6 0.9 copy.182
  1.5 15.2 %copy.141 = bf16[9,15,8192]{1,2,0:T(8,128)(2,1)} copy(f32[9,15,8192]{2,1,0:T(8,128)} %refs_0_.1) | data formatting | bytes 6635520 | tf_op args[0]
  16.7 14.8 %copy.167 = bf16[9,15,8192]{2,1,0:T(8,128)(2,1)S(1)} copy(bf16[9,15,8192]{1,2,0:T(8,128)(2,1)} %copy.141) | data formatting | bytes 4423680 | tf_op jit(solution)/shard_map/convert.19
  31.5 3.1 %convert_element_type.59 = bf16[135,4,16,128]{3,2,1,0:T(8,128)(2,1)} reshape(bf16[9,15,8192]{2,1,0:T(8,128)(2,1)S(1)} %copy.167) | data formatting | bytes 4423680 | tf_op jit(solution)/shard_map/convert_element_type | solution.py:181
  34.6 1.8 maximum_bitcast_fusion
  36.4 1.7 copy.168
  38.2 5.3 %all-to-all-start = ((bf16[4,16,139,128]{3,1,2,0:T(8,128)(2,1)}), bf16[4,16,139,128]{3,1,2,0:T(8,128)(2,1)S(1)}, u32[]{:S(2)}, u32[]{:S(2)}) async-start(bf16[4,16,139,128]{3,1,2,0:T(8,128)(2,1)} %copy.168), calls=%async_computation | async-start | bytes 4554752 | tf_op jit(solution)/shard_map/all_to_all | solution.py:206
  52.7 7.1 %slice.160 = bf16[9,15,64]{1,2,0:T(8,128)(2,1)S(1)} slice(bf16[9,15,8192]{1,2,0:T(8,128)(2,1)} %copy.141), slice={[0:9:1], [0:15:1], [0:8192:128]} | slice | bytes 34560 | tf_op jit(solution)/shard_map/slice | solution.py:122
  59.8 6.8 %slice.161 = bf16[9,15,64]{1,2,0:T(8,128)(2,1)S(1)} slice(bf16[9,15,8192]{1,2,0:T(8,128)(2,1)} %copy.141), slice={[0:9:1], [0:15:1], [127:8192:128]} | slice | bytes 34560 | tf_op jit(solution)/shard_map/slice | solution.py:122
  66.7 1.1 fusion.49
  68.6 16.0 %all_gather.16 = bf16[8,9,16,384]{3,2,1,0:T(8,128)(2,1)S(1)} all-gather(bf16[1,9,16,384]{3,2,1,0:T(8,128)(2,1)S(1)} %pad_maximum_fusion), channel_id=1, replica_groups=mesh['grp'=4,'patch'=8] {'patch'}, dimensions={0}, use_global_device_ids=true | all-gather | bytes 995328 | tf_op jit(solution)/shard_map/all_gather | solution.py:133
  84.6 0.7 select_bitcast_fusion.11
  85.7 1.3 reshape.157
  88.7 0.8 copy.170
  89.5 1.0 reshape.455
  90.5 0.8 slice.245
  91.3 0.8 slice.247
  94.0 10.1 %shard_map.113 = (f32[9,15,8192]{2,1,0:T(8,128)}, bf16[9,16,384]{2,1,0:T(8,128)(2,1)}) custom-call(f32[9,15,8192]{2,1,0:T(8,128)} %refs_0_.1, f32[15,8192]{1,0:T(8,128)} %refs_1_.5, f32[15,8192]{1,0:T(8,128)} %refs_2_.5, f32[9,15,384]{2,1,0:T(8,128)} %maximum_convert_fusion.refs_3_), custom_call_target="tpu_custom_call" | custom-call | flops 22118400 | bytes 9830400 | tf_op jit(solution)/shard_map/pallas_call | solution.py:96
  104.1 16.6 %all-gather = bf16[72,16,384]{2,1,0:T(8,128)(2,1)S(1)} all-gather(bf16[9,16,384]{2,1,0:T(8,128)(2,1)} %get-tuple-element.9), channel_id=2, replica_groups=mesh['grp'=4,'patch'=8] {'patch'}, dimensions={0}, use_global_device_ids=true | all-gather | bytes 995328 | tf_op jit(solution)/shard_map/all_gather | solution.py:133
  122.9 4.0 %multiply_convert_fusion.2 = bf16[16,128,256]{2,1,0:T(8,128)(2,1)} fusion(f32[256]{0:T(256)S(1)} %bitcast.189, bf16[4,16,139,128]{3,1,2,0:T(8,128)(2,1)S(1)} %all-to-all-done, f32[256]{0:T(256)S(1)} %bitcast.190, bf16[4,4,256]{2,1,0:T(4,128)(2,1)S(1)} %copy-done.2, bf16[4,135,256]{2,1,0:T(8,128)(2,1)} %copy.170, bf16[3,256,256]{2,1,0:T(8,128)(2,1)} %param.18), kind=kOutput, calls=%fused_computation.7 | convolution fusion | flops 858304512 | bytes 3745792 | tf_op jit(solution)/shard_map/...h,hj->...j/dot_general | solution.py:155
  126.9 2.9 %multiply_convert_fusion.1 = bf16[16,128,256]{2,1,0:T(8,128)(2,1)} fusion(bf16[16,128,256]{2,1,0:T(8,128)(2,1)} %multiply_convert_fusion.2, f32[256]{0:T(256)S(1)} %bitcast.188, bf16[3,256,256]{2,1,0:T(8,128)(2,1)} %param.18), kind=kOutput, calls=%fused_computation.6 | convolution fusion | flops 271581184 | bytes 2229248 | tf_op jit(solution)/shard_map/...h,hj->...j/dot_general | solution.py:155
  129.9 2.4 %convert_bitcast_fusion = bf16[16,9,4,15,128]{4,3,2,1,0:T(8,128)(2,1)S(1)} fusion(bf16[256,9,4,15,1]{0,3,2,1,4:T(8,128)(2,1)S(1)} %reshape.455, bf16[16,128,256]{2,1,0:T(8,128)(2,1)} %multiply_convert_fusion.1, f32[256]{0:T(256)S(1)} %bitcast.187, bf16[3,256,256]{2,1,0:T(8,128)(2,1)} %param.18), kind=kOutput, calls=%fused_computation.2 | convolution fusion | flops 838918144 | bytes 3668992 | tf_op jit(solution)/shard_map/bch,hvgl->bvglc/dot_general | solution.py:212
  132.4 0.7 fusion.33
  133.1 5.3 %all-to-all-start.2 = ((f32[8,4,128]{2,1,0:T(4,128)}), f32[8,4,128]{2,1,0:T(4,128)S(1)}, u32[]{:S(2)}, u32[]{:S(2)}) async-start(f32[8,4,128]{2,1,0:T(4,128)} %bitcast.81), calls=%async_computation.2 | async-start | bytes 32768 | tf_op jit(solution)/shard_map/all_to_all | solution.py:219
  138.6 0.8 slice.254
  139.8 4.0 %copy.172 = bf16[16,9,4,15,128]{4,0,3,1,2:T(8,128)(2,1)} copy(bf16[16,9,4,15,128]{4,3,2,1,0:T(8,128)(2,1)S(1)} %convert_bitcast_fusion) | data formatting | bytes 4423680 | tf_op jit(solution)/shard_map/convert_element_type | solution.py:214
  144.1 4.2 %all-to-all-start.1 = ((bf16[16,9,4,15,128]{4,0,3,1,2:T(8,128)(2,1)}), bf16[16,9,4,15,128]{4,0,3,1,2:T(8,128)(2,1)S(1)}, u32[]{:S(2)}, u32[]{:S(2)}) async-start(bf16[16,9,4,15,128]{4,0,3,1,2:T(8,128)(2,1)} %copy.172), calls=%async_computation.1 | async-start | bytes 4423680 | tf_op jit(solution)/shard_map/all_to_all | solution.py:222
  149.6 10.1 %shard_map.114 = (f32[9,15,8192]{2,1,0:T(8,128)}, bf16[9,16,384]{2,1,0:T(8,128)(2,1)}) custom-call(f32[9,15,8192]{2,1,0:T(8,128)} %get-tuple-element.8.refs_0_, f32[15,8192]{1,0:T(8,128)} %refs_1_.5, f32[15,8192]{1,0:T(8,128)} %refs_2_.5, f32[9,15,384]{2,1,0:T(8,128)} %maximum_convert_fusion.1.refs_3_), custom_call_target="tpu_custom_call" | custom-call | flops 22118400 | bytes 9830400 | tf_op jit(solution)/shard_map/pallas_call | solution.py:96
  159.7 16.1 %all-gather.1 = bf16[72,16,384]{2,1,0:T(8,128)(2,1)S(1)} all-gather(bf16[9,16,384]{2,1,0:T(8,128)(2,1)} %get-tuple-element.11), channel_id=3, replica_groups=mesh['grp'=4,'patch'=8] {'patch'}, dimensions={0}, use_global_device_ids=true | all-gather | bytes 995328 | tf_op jit(solution)/shard_map/all_gather | solution.py:133
  177.6 0.7 maximum_convert_fusion.2.refs_3_
  178.3 2.0 %copy.173 = bf16[4,16,9,1,15,128]{5,4,2,1,0,3:T(8,128)(2,1)} copy(bf16[4,16,9,1,15,128]{5,1,4,2,0,3:T(8,128)(2,1)S(1)} %bitcast.168) | data formatting | bytes 4423680 | tf_op jit(solution)/shard_map/all_to_all | solution.py:222
  180.3 10.4 %shard_map.115 = (f32[9,15,8192]{2,1,0:T(8,128)}, bf16[9,16,384]{2,1,0:T(8,128)(2,1)}) custom-call(f32[9,15,8192]{2,1,0:T(8,128)} %get-tuple-element.10.refs_0_, f32[15,8192]{1,0:T(8,128)} %refs_1_.5, f32[15,8192]{1,0:T(8,128)} %refs_2_.5, f32[9,15,384]{2,1,0:T(8,128)} %maximum_convert_fusion.2.refs_3_, bf16[64,9,15,128]{3,2,1,0:T(8,128)(2,1)} %bitcast.167), custom_call_target="tpu_custom_call" | custom-call | flops 22118400 | bytes 9830400 | tf_op jit(solution)/shard_map/pallas_call | solution.py:96
  (93 shorter events, 12.5 us)
Async XLA Ops:
  38.2 5.3 %copy-start.4 = (s32[8,4]{0,1:T(4,128)S(1)}, s32[8,4]{0,1:T(4,128)}, u32[]{:S(2)}) copy-start(s32[8,4]{0,1:T(4,128)} %param.21) | copy-start | bytes 388
  38.2 13.9 %copy-start = (bf16[556,256]{1,0:T(8,128)(2,1)S(1)}, bf16[556,256]{1,0:T(8,128)(2,1)}, u32[]{:S(2)}) copy-start(bf16[556,256]{1,0:T(8,128)(2,1)} %param.16) | copy-start | bytes 854020
  38.2 84.7 %all-to-all-start = ((bf16[4,16,139,128]{3,1,2,0:T(8,128)(2,1)}), bf16[4,16,139,128]{3,1,2,0:T(8,128)(2,1)S(1)}, u32[]{:S(2)}, u32[]{:S(2)}) async-start(bf16[4,16,139,128]{3,1,2,0:T(8,128)(2,1)} %copy.168), calls=%async_computation | async-start | bytes 4554752 | tf_op jit(solution)/shard_map/all_to_all | solution.py:206
  68.0 19.6 %copy-start.5 = (s32[512,1]{0,1:T(1,128)S(1)}, s32[512,1]{0,1:T(1,128)}, u32[]{:S(2)}) copy-start(s32[512,1]{0,1:T(1,128)} %param.20) | copy-start | bytes 6148
  68.2 20.3 %slice-start = ((bf16[556,256]{1,0:T(8,128)(2,1)}), bf16[540,256]{1,0:T(8,128)(2,1)S(1)}, s32[]{:S(2)}) async-start(bf16[556,256]{1,0:T(8,128)(2,1)} %param.16), calls=%async_computation.3 | async-start | bytes 557056 | tf_op jit(solution)/shard_map/slice | solution.py:197
  88.3 3.0 %copy-start.1 = (s32[8,4,16]{2,1,0:T(4,128)}, s32[8,4,16]{2,1,0:T(4,128)S(1)}, u32[]{:S(2)}) copy-start(s32[8,4,16]{2,1,0:T(4,128)S(1)} %reshape.160) | copy-start | bytes 6148
  104.1 18.7 %copy-start.3 = (f32[4,256]{1,0:T(4,128)S(1)}, f32[4,256]{1,0:T(4,128)}, u32[]{:S(2)}) copy-start(f32[4,256]{1,0:T(4,128)} %param.17) | copy-start | bytes 12292
  104.1 18.7 %copy-start.2 = (bf16[4,4,256]{2,1,0:T(4,128)(2,1)S(1)}, bf16[4,4,256]{2,1,0:T(4,128)(2,1)}, u32[]{:S(2)}) copy-start(bf16[4,4,256]{2,1,0:T(4,128)(2,1)} %reshape.157) | copy-start | bytes 24580
  133.1 11.0 %all-to-all-start.2 = ((f32[8,4,128]{2,1,0:T(4,128)}), f32[8,4,128]{2,1,0:T(4,128)S(1)}, u32[]{:S(2)}, u32[]{:S(2)}) async-start(f32[8,4,128]{2,1,0:T(4,128)} %bitcast.81), calls=%async_computation.2 | async-start | bytes 32768 | tf_op jit(solution)/shard_map/all_to_all | solution.py:219
  144.1 34.2 %all-to-all-start.1 = ((bf16[16,9,4,15,128]{4,0,3,1,2:T(8,128)(2,1)}), bf16[16,9,4,15,128]{4,0,3,1,2:T(8,128)(2,1)S(1)}, u32[]{:S(2)}, u32[]{:S(2)}) async-start(bf16[16,9,4,15,128]{4,0,3,1,2:T(8,128)(2,1)} %copy.172), calls=%async_computation.1 | async-start | bytes 4423680 | tf_op jit(solution)/shard_map/all_to_all | solution.py:222

commit v6 on v5

--- a/solution.py
+++ b/solution.py
@@ -58,6 +58,10 @@
             pay_ref[0, 0:levels, 0:PY] = packed
         if x == rows - 1:
             pay_ref[0, 0:levels, PY : 2 * PY] = packed
+    finish_payload(pay_ref, stack_ref, levels)
+
+
+def finish_payload(pay_ref, stack_ref, levels):
     pad_rows = pay_ref.shape[1] - levels
     if pad_rows:
         pay_ref[0, levels:, 0 : 2 * PY] = jnp.zeros((pad_rows, 2 * PY), pay_ref.dtype)
@@ -112,18 +116,34 @@
     )(*args)
 
 
+def pack_kernel(st_ref, pay_ref, stack_ref):
+    rows = st_ref.shape[2] // PY
+    slot = stack_ref.shape[0] // rows
+    levels = st_ref.shape[1]
+    stack_ref[...] = jnp.zeros(stack_ref.shape, stack_ref.dtype)
+    for x in range(rows):
+        packed = st_ref[0, :, x * PY : (x + 1) * PY].astype(jnp.bfloat16)
+        stack_ref[x * slot : x * slot + levels, :] = packed
+        if x == 0:
+            pay_ref[0, 0:levels, 0:PY] = packed
+        if x == rows - 1:
+            pay_ref[0, 0:levels, PY : 2 * PY] = packed
+    finish_payload(pay_ref, stack_ref, levels)
+
+
 def first_edges(tracer):
     n_vars, levels, width = tracer.shape
     rows = width // PY
     slot = 16
-    chunk_rows = PY // slot
-    edge_rows = jnp.concatenate([tracer[..., 0:PY], tracer[..., width - PY :]], axis=-1)
-    edge_rows = jnp.pad(edge_rows, ((0, 0), (0, slot - levels), (0, 0)))
-    edge_cols = jnp.stack([tracer[..., 0::PY], tracer[..., PY - 1 :: PY]], axis=1)
-    edge_cols = jnp.pad(edge_cols, ((0, 0), (0, 0), (0, slot - levels), (0, 0)))
-    edge_cols = edge_cols.reshape(n_vars, 2, slot, rows // chunk_rows, chunk_rows)
-    edge_cols = edge_cols.transpose(0, 3, 1, 4, 2).reshape(n_vars, 2 * rows // chunk_rows, PY)
-    return jnp.concatenate([edge_rows, edge_cols], axis=-1).astype(jnp.bfloat16)
+    return pl.pallas_call(
+        pack_kernel,
+        grid=(n_vars,),
+        in_specs=[pl.BlockSpec((1, levels, width), lambda v: (v, 0, 0))],
+        out_specs=pl.BlockSpec((1, slot, 3 * PY), lambda v: (v, 0, 0)),
+        out_shape=jax.ShapeDtypeStruct((n_vars, slot, 3 * PY), jnp.bfloat16),
+        scratch_shapes=[pltpu.VMEM((rows * slot, PY), jnp.bfloat16)],
+        cost_estimate=pl.CostEstimate(flops=0, transcendentals=0, bytes_accessed=4 * tracer.size),
+    )(tracer)
 
 
 def exchange_halo(payload, beside_all, patches, levels):

time: 194 us -> 157 us (0.81)
  local copies, waits for them, and re-layouts: 69.8 us -> 24.1 us
  Pallas kernels: 30.6 us -> 38.1 us
  other arithmetic: 7.8 us -> 10.3 us
    slice x5 -> x0, local copies, waits for them, and re-layouts: 15.4 us -> none  [the longest x2 13.9 us: first_edges(): edge_cols = jnp.stack([tracer[..., 0::PY], tracer[..., PY - 1::PY]], axis=1)]
    unnamed x16 -> x15, local copies, waits for them, and re-layouts: 17.2 us -> 1.99 us
    another operation x1 -> x0, local copies, waits for them, and re-layouts: 14.8 us -> none
    pallas_call x0 -> x1, Pallas kernels: none -> 7.51 us  [first_edges(): pl.pallas_call(pack_kernel, grid=(n_vars,), in_specs=[pl.BlockSpec((1, le...]
    convert_element_type x0 -> x1, other arithmetic: none -> 2.62 us  [on_device(): tracer.astype(jnp.bfloat16).reshape(VARS * level_share, PX, PY)]
  transfers between devices with their start and end apart: 3 -> 3, of which waited for: 1 -> 1; matrix products, arithmetic and copies ran while one was open for 19% -> 14% of each run, Pallas kernels for 11% -> 18%
where the time goes in v6:
time: 157 us; the launch traced here: 156 us
  blocking collectives  49 us (31%)
  Pallas kernels  38.1 us (24%)
  local copies, waits for them, and re-layouts  24.1 us (15%)
  starting transfers between devices  14.9 us (9%)
  other arithmetic  10.3 us (7%)
  matrix products  10.2 us (6%)
  between operations  8.63 us (5%)
    all_gather x3, blocking collectives, exchange_halo(): got = lax.all_gather(payload, 'patch', axis=0, tiled=False)  49 us
    pallas_call x3, Pallas kernels, stencil(): pl.pallas_call(functools.partial(stencil_kernel, with_tend=with_tend), gr...  30.6 us
    pallas_call x1, Pallas kernels, first_edges(): pl.pallas_call(pack_kernel, grid=(n_vars,), in_specs=[pl.BlockSpec((1, le...  7.51 us
    dot_general x2, matrix products, hidden_layers(): jnp.einsum('...h,hj->...j', hidden, w_mid[layer_index], preferred_element...  7 us
    all_to_all x1, starting transfers between devices, on_device(): lax.all_to_all(by_quarter, 'grp', split_axis=0, concat_axis=0, tiled=True)  5.32 us
    all_to_all x1, starting transfers between devices, on_device(): lax.all_to_all(packed, 'patch', split_axis=0, concat_axis=0, tiled=True)  5.31 us
    all_to_all x1, starting transfers between devices, on_device(): lax.all_to_all(tendency, 'grp', split_axis=2, concat_axis=0, tiled=True)  4.24 us
    convert_element_type x1, local copies, waits for them, and re-layouts, on_device(): tendency = jnp.einsum('bch,hvgl->bvglc', hidden, w_split, preferred_eleme...  3.98 us
  transfers between devices with their start and end apart: 3, of which 1 were waited for; matrix products, arithmetic and copies ran while one was open for 14% of the time, Pallas kernels for 18%

profile of v6, /device:TPU:0, one launch (start us, length us, event | category | flops | bytes accessed | tf_op | source)
XLA Modules:
  0.0 155.5 jit_solution(1862755401323908786)
XLA Ops:
  0.6 0.9 copy.78
  1.5 2.6 %convert_element_type.49 = bf16[9,15,8192]{2,1,0:T(8,128)(2,1)S(1)} convert(f32[9,15,8192]{2,1,0:T(8,128)} %refs_0_.1) | non-fusion elementwise | flops 1105920 | bytes 6635520 | tf_op jit(solution)/shard_map/convert_element_type | solution.py:201
  4.1 3.1 %convert_element_type.50 = bf16[135,4,16,128]{3,2,1,0:T(8,128)(2,1)} reshape(bf16[9,15,8192]{2,1,0:T(8,128)(2,1)S(1)} %convert_element_type.49) | data formatting | bytes 4423680 | tf_op jit(solution)/shard_map/convert_element_type | solution.py:201
  7.2 1.8 %maximum_bitcast_fusion = bf16[4,16,139,128]{3,1,0,2:T(8,128)(2,1)S(1)} fusion(bf16[4,4,16,128]{3,2,1,0:T(8,128)(2,1)S(1)} %bitcast.169, bf16[135,4,16,128]{3,2,1,0:T(8,128)(2,1)} %convert_element_type.50), kind=kLoop, calls=%fused_computation.3 | loop fusion | flops 1138688 | bytes 4554752 | tf_op jit(solution)/shard_map/transpose | solution.py:206
  9.0 1.8 %copy.64 = bf16[4,16,139,128]{3,1,2,0:T(8,128)(2,1)} copy(bf16[4,16,139,128]{3,1,0,2:T(8,128)(2,1)S(1)} %maximum_bitcast_fusion) | data formatting | bytes 4554752 | tf_op jit(solution)/shard_map/transpose | solution.py:206
  10.8 5.3 %all-to-all-start = ((bf16[4,16,139,128]{3,1,2,0:T(8,128)(2,1)}), bf16[4,16,139,128]{3,1,2,0:T(8,128)(2,1)S(1)}, u32[]{:S(2)}, u32[]{:S(2)}) async-start(bf16[4,16,139,128]{3,1,2,0:T(8,128)(2,1)} %copy.64), calls=%async_computation | async-start | bytes 4554752 | tf_op jit(solution)/shard_map/all_to_all | solution.py:226
  24.4 7.5 %shard_map.113 = bf16[9,16,384]{2,1,0:T(8,128)(2,1)} custom-call(f32[9,15,8192]{2,1,0:T(8,128)} %refs_0_.1), custom_call_target="tpu_custom_call" | custom-call | bytes 4423680 | tf_op jit(solution)/shard_map/pallas_call | solution.py:138
  32.6 16.3 %all-gather = bf16[72,16,384]{2,1,0:T(8,128)(2,1)S(1)} all-gather(bf16[9,16,384]{2,1,0:T(8,128)(2,1)} %shard_map.113), channel_id=2, replica_groups=mesh['grp'=4,'patch'=8] {'patch'}, dimensions={0}, use_global_device_ids=true | all-gather | bytes 995328 | tf_op jit(solution)/shard_map/all_gather | solution.py:153
  48.8 0.7 select_bitcast_fusion.11
  49.9 1.3 reshape.119
  52.9 0.7 copy.66
  53.6 1.0 reshape.418
  54.7 0.8 slice.223
  55.5 0.8 slice.225
  57.5 0.7 maximum_convert_fusion.refs_3_
  58.2 10.1 %shard_map.114 = (f32[9,15,8192]{2,1,0:T(8,128)}, bf16[9,16,384]{2,1,0:T(8,128)(2,1)}) custom-call(f32[9,15,8192]{2,1,0:T(8,128)} %refs_0_.1, f32[15,8192]{1,0:T(8,128)} %refs_1_.5, f32[15,8192]{1,0:T(8,128)} %refs_2_.5, f32[9,15,384]{2,1,0:T(8,128)} %maximum_convert_fusion.refs_3_), custom_call_target="tpu_custom_call" | custom-call | flops 22118400 | bytes 9830400 | tf_op jit(solution)/shard_map/pallas_call | solution.py:100
  68.3 16.6 %all-gather.1 = bf16[72,16,384]{2,1,0:T(8,128)(2,1)S(1)} all-gather(bf16[9,16,384]{2,1,0:T(8,128)(2,1)} %get-tuple-element.9), channel_id=3, replica_groups=mesh['grp'=4,'patch'=8] {'patch'}, dimensions={0}, use_global_device_ids=true | all-gather | bytes 995328 | tf_op jit(solution)/shard_map/all_gather | solution.py:153
  84.9 0.7 select_bitcast_fusion.7
  87.1 4.0 %multiply_convert_fusion.2 = bf16[16,128,256]{2,1,0:T(8,128)(2,1)} fusion(f32[256]{0:T(256)S(1)} %bitcast.177, bf16[4,16,139,128]{3,1,2,0:T(8,128)(2,1)S(1)} %all-to-all-done, f32[256]{0:T(256)S(1)} %bitcast.178, bf16[4,4,256]{2,1,0:T(4,128)(2,1)S(1)} %copy-done.2, bf16[4,135,256]{2,1,0:T(8,128)(2,1)} %copy.66, bf16[3,256,256]{2,1,0:T(8,128)(2,1)} %param.18), kind=kOutput, calls=%fused_computation.7 | convolution fusion | flops 858304512 | bytes 3745792 | tf_op jit(solution)/shard_map/...h,hj->...j/dot_general | solution.py:175
  91.1 3.0 %multiply_convert_fusion.1 = bf16[16,128,256]{2,1,0:T(8,128)(2,1)} fusion(bf16[16,128,256]{2,1,0:T(8,128)(2,1)} %multiply_convert_fusion.2, f32[256]{0:T(256)S(1)} %bitcast.176, bf16[3,256,256]{2,1,0:T(8,128)(2,1)} %param.18), kind=kOutput, calls=%fused_computation.6 | convolution fusion | flops 271581184 | bytes 2229248 | tf_op jit(solution)/shard_map/...h,hj->...j/dot_general | solution.py:175
  94.1 2.4 %convert_bitcast_fusion = bf16[16,9,4,15,128]{4,3,2,1,0:T(8,128)(2,1)S(1)} fusion(bf16[256,9,4,15,1]{0,3,2,1,4:T(8,128)(2,1)S(1)} %reshape.418, bf16[16,128,256]{2,1,0:T(8,128)(2,1)} %multiply_convert_fusion.1, f32[256]{0:T(256)S(1)} %bitcast.175, bf16[3,256,256]{2,1,0:T(8,128)(2,1)} %param.18), kind=kOutput, calls=%fused_computation.2 | convolution fusion | flops 838918144 | bytes 3668992 | tf_op jit(solution)/shard_map/bch,hvgl->bvglc/dot_general | solution.py:232
  96.6 0.7 fusion.25
  97.3 5.3 %all-to-all-start.2 = ((f32[8,4,128]{2,1,0:T(4,128)}), f32[8,4,128]{2,1,0:T(4,128)S(1)}, u32[]{:S(2)}, u32[]{:S(2)}) async-start(f32[8,4,128]{2,1,0:T(4,128)} %bitcast.76), calls=%async_computation.2 | async-start | bytes 32768 | tf_op jit(solution)/shard_map/all_to_all | solution.py:239
  102.7 0.8 slice.232
  104.0 4.0 %copy.68 = bf16[16,9,4,15,128]{4,0,3,1,2:T(8,128)(2,1)} copy(bf16[16,9,4,15,128]{4,3,2,1,0:T(8,128)(2,1)S(1)} %convert_bitcast_fusion) | data formatting | bytes 4423680 | tf_op jit(solution)/shard_map/convert_element_type | solution.py:234
  108.3 4.2 %all-to-all-start.1 = ((bf16[16,9,4,15,128]{4,0,3,1,2:T(8,128)(2,1)}), bf16[16,9,4,15,128]{4,0,3,1,2:T(8,128)(2,1)S(1)}, u32[]{:S(2)}, u32[]{:S(2)}) async-start(bf16[16,9,4,15,128]{4,0,3,1,2:T(8,128)(2,1)} %copy.68), calls=%async_computation.1 | async-start | bytes 4423680 | tf_op jit(solution)/shard_map/all_to_all | solution.py:242
  113.1 0.7 maximum_convert_fusion.1.refs_3_
  113.8 10.1 %shard_map.115 = (f32[9,15,8192]{2,1,0:T(8,128)}, bf16[9,16,384]{2,1,0:T(8,128)(2,1)}) custom-call(f32[9,15,8192]{2,1,0:T(8,128)} %get-tuple-element.8.refs_0_, f32[15,8192]{1,0:T(8,128)} %refs_1_.5, f32[15,8192]{1,0:T(8,128)} %refs_2_.5, f32[9,15,384]{2,1,0:T(8,128)} %maximum_convert_fusion.1.refs_3_), custom_call_target="tpu_custom_call" | custom-call | flops 22118400 | bytes 9830400 | tf_op jit(solution)/shard_map/pallas_call | solution.py:100
  123.9 16.1 %all-gather.2 = bf16[72,16,384]{2,1,0:T(8,128)(2,1)S(1)} all-gather(bf16[9,16,384]{2,1,0:T(8,128)(2,1)} %get-tuple-element.11), channel_id=4, replica_groups=mesh['grp'=4,'patch'=8] {'patch'}, dimensions={0}, use_global_device_ids=true | all-gather | bytes 995328 | tf_op jit(solution)/shard_map/all_gather | solution.py:153
  141.8 0.7 maximum_convert_fusion.2.refs_3_
  142.5 2.0 %copy.69 = bf16[4,16,9,1,15,128]{5,4,2,1,0,3:T(8,128)(2,1)} copy(bf16[4,16,9,1,15,128]{5,1,4,2,0,3:T(8,128)(2,1)S(1)} %bitcast.157) | data formatting | bytes 4423680 | tf_op jit(solution)/shard_map/all_to_all | solution.py:242
  144.5 10.4 %shard_map.116 = (f32[9,15,8192]{2,1,0:T(8,128)}, bf16[9,16,384]{2,1,0:T(8,128)(2,1)}) custom-call(f32[9,15,8192]{2,1,0:T(8,128)} %get-tuple-element.10.refs_0_, f32[15,8192]{1,0:T(8,128)} %refs_1_.5, f32[15,8192]{1,0:T(8,128)} %refs_2_.5, f32[9,15,384]{2,1,0:T(8,128)} %maximum_convert_fusion.2.refs_3_, bf16[64,9,15,128]{3,2,1,0:T(8,128)(2,1)} %bitcast.156), custom_call_target="tpu_custom_call" | custom-call | flops 22118400 | bytes 9830400 | tf_op jit(solution)/shard_map/pallas_call | solution.py:100
  (82 shorter events, 9.6 us)
Async XLA Ops:
  10.8 5.3 %copy-start.4 = (s32[8,4]{0,1:T(4,128)S(1)}, s32[8,4]{0,1:T(4,128)}, u32[]{:S(2)}) copy-start(s32[8,4]{0,1:T(4,128)} %param.21) | copy-start | bytes 388
  10.8 76.2 %all-to-all-start = ((bf16[4,16,139,128]{3,1,2,0:T(8,128)(2,1)}), bf16[4,16,139,128]{3,1,2,0:T(8,128)(2,1)S(1)}, u32[]{:S(2)}, u32[]{:S(2)}) async-start(bf16[4,16,139,128]{3,1,2,0:T(8,128)(2,1)} %copy.64), calls=%async_computation | async-start | bytes 4554752 | tf_op jit(solution)/shard_map/all_to_all | solution.py:226
  24.4 7.5 %copy-start = (bf16[556,256]{1,0:T(8,128)(2,1)S(1)}, bf16[556,256]{1,0:T(8,128)(2,1)}, u32[]{:S(2)}) copy-start(bf16[556,256]{1,0:T(8,128)(2,1)} %param.16) | copy-start | bytes 854020
  32.0 19.8 %copy-start.5 = (s32[512,1]{0,1:T(1,128)S(1)}, s32[512,1]{0,1:T(1,128)}, u32[]{:S(2)}) copy-start(s32[512,1]{0,1:T(1,128)} %param.20) | copy-start | bytes 6148
  52.5 3.0 %copy-start.1 = (s32[8,4,16]{2,1,0:T(4,128)}, s32[8,4,16]{2,1,0:T(4,128)S(1)}, u32[]{:S(2)}) copy-start(s32[8,4,16]{2,1,0:T(4,128)S(1)} %reshape.122) | copy-start | bytes 6148
  68.3 18.7 %copy-start.3 = (f32[4,256]{1,0:T(4,128)S(1)}, f32[4,256]{1,0:T(4,128)}, u32[]{:S(2)}) copy-start(f32[4,256]{1,0:T(4,128)} %param.17) | copy-start | bytes 12292
  68.3 18.7 %copy-start.2 = (bf16[4,4,256]{2,1,0:T(4,128)(2,1)S(1)}, bf16[4,4,256]{2,1,0:T(4,128)(2,1)}, u32[]{:S(2)}) copy-start(bf16[4,4,256]{2,1,0:T(4,128)(2,1)} %reshape.119) | copy-start | bytes 24580
  97.3 11.0 %all-to-all-start.2 = ((f32[8,4,128]{2,1,0:T(4,128)}), f32[8,4,128]{2,1,0:T(4,128)S(1)}, u32[]{:S(2)}, u32[]{:S(2)}) async-start(f32[8,4,128]{2,1,0:T(4,128)} %bitcast.76), calls=%async_computation.2 | async-start | bytes 32768 | tf_op jit(solution)/shard_map/all_to_all | solution.py:239
  108.3 34.2 %all-to-all-start.1 = ((bf16[16,9,4,15,128]{4,0,3,1,2:T(8,128)(2,1)}), bf16[16,9,4,15,128]{4,0,3,1,2:T(8,128)(2,1)S(1)}, u32[]{:S(2)}, u32[]{:S(2)}) async-start(bf16[16,9,4,15,128]{4,0,3,1,2:T(8,128)(2,1)} %copy.68), calls=%async_computation.1 | async-start | bytes 4423680 | tf_op jit(solution)/shard_map/all_to_all | solution.py:242

commit v7 on v6

--- a/solution.py
+++ b/solution.py
@@ -116,14 +116,19 @@
     )(*args)
 
 
-def pack_kernel(st_ref, pay_ref, stack_ref):
+def pack_kernel(st_ref, surf_ref, pay_ref, feat_ref, stack_ref, *, n_surf):
     rows = st_ref.shape[2] // PY
     slot = stack_ref.shape[0] // rows
     levels = st_ref.shape[1]
+    keep_surface = pl.program_id(0) < n_surf
     stack_ref[...] = jnp.zeros(stack_ref.shape, stack_ref.dtype)
     for x in range(rows):
-        packed = st_ref[0, :, x * PY : (x + 1) * PY].astype(jnp.bfloat16)
+        here = slice(x * PY, (x + 1) * PY)
+        packed = st_ref[0, :, here].astype(jnp.bfloat16)
         stack_ref[x * slot : x * slot + levels, :] = packed
+        feat_ref[x, 0, 0:levels, :] = packed
+        surf_row = surf_ref[0, :, here]
+        feat_ref[x, 0, levels : levels + 1, :] = jnp.where(keep_surface, surf_row, jnp.zeros_like(surf_row))
         if x == 0:
             pay_ref[0, 0:levels, 0:PY] = packed
         if x == rows - 1:
@@ -131,19 +136,30 @@
     finish_payload(pay_ref, stack_ref, levels)
 
 
-def first_edges(tracer):
+def first_edges(tracer, surface):
     n_vars, levels, width = tracer.shape
+    n_surf = surface.shape[0]
     rows = width // PY
     slot = 16
+    surf_rows = surface.reshape(n_surf, 1, width)
     return pl.pallas_call(
-        pack_kernel,
+        functools.partial(pack_kernel, n_surf=n_surf),
         grid=(n_vars,),
-        in_specs=[pl.BlockSpec((1, levels, width), lambda v: (v, 0, 0))],
-        out_specs=pl.BlockSpec((1, slot, 3 * PY), lambda v: (v, 0, 0)),
-        out_shape=jax.ShapeDtypeStruct((n_vars, slot, 3 * PY), jnp.bfloat16),
+        in_specs=[
+            pl.BlockSpec((1, levels, width), lambda v: (v, 0, 0)),
+            pl.BlockSpec((1, 1, width), lambda v: (jnp.minimum(v, n_surf - 1), 0, 0)),
+        ],
+        out_specs=[
+            pl.BlockSpec((1, slot, 3 * PY), lambda v: (v, 0, 0)),
+            pl.BlockSpec((rows, 1, slot, PY), lambda v: (0, v, 0, 0)),
+        ],
+        out_shape=[
+            jax.ShapeDtypeStruct((n_vars, slot, 3 * PY), jnp.bfloat16),
+            jax.ShapeDtypeStruct((rows, n_vars, slot, PY), jnp.bfloat16),
+        ],
         scratch_shapes=[pltpu.VMEM((rows * slot, PY), jnp.bfloat16)],
-        cost_estimate=pl.CostEstimate(flops=0, transcendentals=0, bytes_accessed=4 * tracer.size),
-    )(tracer)
+        cost_estimate=pl.CostEstimate(flops=0, transcendentals=0, bytes_accessed=5 * tracer.size),
+    )(tracer, surf_rows)
 
 
 def exchange_halo(payload, beside_all, patches, levels):
@@ -194,16 +210,10 @@
     quarter_rows = PX // groups
     capacity = max(2, 2 * quarter_rows // patches)
     slot_count = patches * capacity
-    tracer = state.reshape(VARS, level_share, PX, PY)
+    slot = 16
     beside_all = jnp.take(neighbours, patch_here, axis=0)
-    features = jnp.concatenate(
-        [
-            tracer.astype(jnp.bfloat16).reshape(VARS * level_share, PX, PY),
-            surface.reshape(surf_share, PX, PY),
-        ],
-        axis=0,
-    )
-    by_quarter = features.reshape(feat_share, groups, quarter_rows, PY).transpose(1, 2, 0, 3)
+    payload, feat = first_edges(state, surface)
+    by_quarter = feat.reshape(groups, quarter_rows, VARS * slot, PY)
     owners_all = owner_map.reshape(patches, groups, quarter_rows)
     owners_here = jnp.take(owners_all, patch_here, axis=0)
     matches = (owners_here[..., None] == jnp.arange(patches, dtype=jnp.int32)).astype(jnp.int32)
@@ -213,15 +223,10 @@
         slot_index[:, None, :] == jnp.arange(slot_count, dtype=jnp.int32)[None, :, None]
     ).astype(jnp.bfloat16)
     selector_here = jnp.take(selector, group_here, axis=0)
-    state_part = (
-        w_in[: VARS * LEV]
-        .reshape(VARS, groups, level_share, -1)
-        .transpose(1, 0, 2, 3)
-        .reshape(groups, VARS * level_share, -1)
-    )
-    w_local = jnp.concatenate(
-        [state_part, w_in[VARS * LEV :].reshape(groups, surf_share, -1)], axis=1
-    )
+    state_part = w_in[: VARS * LEV].reshape(VARS, groups, level_share, -1).transpose(1, 0, 2, 3)
+    state_part = jnp.pad(state_part, ((0, 0), (0, 0), (0, slot - level_share), (0, 0)))
+    surf_part = w_in[VARS * LEV :].reshape(groups, surf_share, -1)
+    w_local = state_part.at[:, :surf_share, level_share, :].set(surf_part).reshape(groups, VARS * slot, -1)
     w_split = w_out.reshape(-1, VARS, groups, level_share)
     regrouped = lax.all_to_all(by_quarter, "grp", split_axis=0, concat_axis=0, tiled=True)
     pre_act = (
@@ -230,19 +235,18 @@
     )
     hidden = hidden_layers(activate(pre_act), b_hidden, w_mid)
     tendency = jnp.einsum(
-        "bch,hvgl->bvglc", hidden, w_split, preferred_element_type=jnp.float32
+        "bch,hvgl->gbvlc", hidden, w_split, preferred_element_type=jnp.float32
     ).astype(jnp.bfloat16)
-    heating = HEAT_WEIGHT * jnp.sum(tendency[:, 0].astype(jnp.float32), axis=(1, 2))
+    heating = HEAT_WEIGHT * jnp.sum(tendency[:, :, 0].astype(jnp.float32), axis=(0, 2))
     packed = jnp.dot(
         selector_here.astype(jnp.float32), heating, precision=lax.Precision.HIGHEST
     ).reshape(patches, capacity, PY)
     owner_heating = lax.all_to_all(
         packed, "patch", split_axis=0, concat_axis=0, tiled=True
     ).reshape(slot_count, PY)
-    arrived = lax.all_to_all(tendency, "grp", split_axis=2, concat_axis=0, tiled=True)
+    arrived = lax.all_to_all(tendency, "grp", split_axis=0, concat_axis=0, tiled=True)
     tendency_here = arrived.reshape(PX, VARS, level_share, PY)
     advected = state
-    payload = first_edges(state)
     for section_index in range(SUBSTEPS):
         halo = exchange_halo(payload, beside_all, patches, level_share)
         last = section_index == SUBSTEPS - 1

time: 157 us -> 155 us (0.987)
  local copies, waits for them, and re-layouts: 24.1 us -> 20.1 us
    another operation x0 -> x3, other arithmetic: none -> 3.44 us
    convert_element_type x2 -> x1, local copies, waits for them, and re-layouts: 7.07 us -> 3.97 us  [on_device(): tendency = jnp.einsum('bch,hvgl->gbvlc', hidden, w_split, preferred_eleme...]
    convert_element_type x1 -> x0, other arithmetic: 2.62 us -> none  [on_device(): tracer.astype(jnp.bfloat16).reshape(VARS * level_share, PX, PY)]
    scatter x0 -> x2, local copies, waits for them, and re-layouts: none -> 2.17 us  [on_device(): state_part.at[:, :surf_share, level_share, :].set(surf_part)]
    transpose x2 -> x0, local copies, waits for them, and re-layouts: 1.94 us -> none  [the longest x1 1.79 us: on_device(): features.reshape(feat_share, groups, quarter_rows, PY).transpose(1, 2, 0, 3)]
    transpose x1 -> x0, other arithmetic: 1.82 us -> none  [on_device(): features.reshape(feat_share, groups, quarter_rows, PY).transpose(1, 2, 0, 3)]
  transfers between devices with their start and end apart: 3 -> 3, of which waited for: 1 -> 1; matrix products, arithmetic and copies ran while one was open for 14% -> 18% of each run, Pallas kernels for 18% -> 13%
where the time goes in v7:
time: 155 us; the launch traced here: 153 us
  blocking collectives  48.9 us (32%)
  Pallas kernels  38.7 us (25%)
  local copies, waits for them, and re-layouts  20.1 us (13%)
  starting transfers between devices  14.9 us (10%)
  other arithmetic  11.3 us (7%)
  matrix products  9.96 us (6%)
  between operations  8.52 us (5%)
    all_gather x3, blocking collectives, exchange_halo(): got = lax.all_gather(payload, 'patch', axis=0, tiled=False)  48.9 us
    pallas_call x3, Pallas kernels, stencil(): pl.pallas_call(functools.partial(stencil_kernel, with_tend=with_tend), gr...  30.6 us
    pallas_call x1, Pallas kernels, first_edges(): pl.pallas_call(functools.partial(pack_kernel, n_surf=n_surf), grid=(n_var...  8.17 us
    dot_general x2, matrix products, hidden_layers(): jnp.einsum('...h,hj->...j', hidden, w_mid[layer_index], preferred_element...  6.77 us
    all_to_all x1, starting transfers between devices, on_device(): lax.all_to_all(by_quarter, 'grp', split_axis=0, concat_axis=0, tiled=True)  5.34 us
    all_to_all x1, starting transfers between devices, on_device(): lax.all_to_all(packed, 'patch', split_axis=0, concat_axis=0, tiled=True)  5.32 us
    all_to_all x1, starting transfers between devices, on_device(): lax.all_to_all(tendency, 'grp', split_axis=0, concat_axis=0, tiled=True)  4.24 us
    convert_element_type x1, local copies, waits for them, and re-layouts, on_device(): tendency = jnp.einsum('bch,hvgl->gbvlc', hidden, w_split, preferred_eleme...  3.97 us
  transfers between devices with their start and end apart: 3, of which 1 were waited for; matrix products, arithmetic and copies ran while one was open for 18% of the time, Pallas kernels for 13%

profile of v7, /device:TPU:0, one launch (start us, length us, event | category | flops | bytes accessed | tf_op | source)
XLA Modules:
  0.0 152.8 jit_solution(17930287932135799532)
XLA Ops:
  0.6 1.6 %copy.66.surf_ref = bf16[4,1,8192]{2,1,0:T(2,128)(2,1)} copy(bf16[4,1,8192]{2,0,1:T(4,128)(2,1)} %bitcast.170) | data formatting | bytes 131072 | tf_op jit(solution)/shard_map/reshape | solution.py:144
  2.2 8.2 %shard_map.113 = (bf16[9,16,384]{2,1,0:T(8,128)(2,1)}, bf16[64,9,16,128]{3,2,1,0:T(8,128)(2,1)}) custom-call(f32[9,15,8192]{2,1,0:T(8,128)} %refs_0_.1, bf16[4,1,8192]{2,1,0:T(2,128)(2,1)} %copy.66.surf_ref), custom_call_target="tpu_custom_call" | custom-call | bytes 5529600 | tf_op jit(solution)/shard_map/pallas_call | solution.py:145
  10.4 5.3 %all-to-all-start = ((bf16[4,16,144,128]{3,2,1,0:T(8,128)(2,1)}), bf16[4,16,144,128]{3,2,1,0:T(8,128)(2,1)S(1)}, u32[]{:S(2)}, u32[]{:S(2)}) async-start(bf16[4,16,144,128]{3,2,1,0:T(8,128)(2,1)} %bitcast.156), calls=%async_computation | async-start | bytes 4718592 | tf_op jit(solution)/shard_map/all_to_all | solution.py:231
  26.7 16.3 %all-gather = bf16[72,16,384]{2,1,0:T(8,128)(2,1)S(1)} all-gather(bf16[9,16,384]{2,1,0:T(8,128)(2,1)} %get-tuple-element.22), channel_id=2, replica_groups=mesh['grp'=4,'patch'=8] {'patch'}, dimensions={0}, use_global_device_ids=true | all-gather | bytes 995328 | tf_op jit(solution)/shard_map/all_gather | solution.py:169
  42.9 0.8 select_bitcast_fusion.11
  44.3 1.4 and_reduce_fusion
  45.7 2.0 %broadcast_select_fusion = bf16[4,4,1,256]{3,2,0,1:T(2,128)(2,1)S(1)} fusion(pred[]{:T(512)} %and_reduce_fusion, bf16[4,4,1,256]{3,1,0,2:T(4,128)(2,1)S(1)} %reshape.161, s32[]{:T(128)} %bitcast.55, s32[]{:T(128)} %bitcast.56, bf16[4,9,15,256]{3,2,0,1:T(8,128)(2,1)S(1)} %bitcast.154), kind=kLoop, calls=%fused_computation.46 | loop fusion | flops 4096 | bytes 292873 | tf_op jit(solution)/shard_map/select.1
  47.8 1.4 reduce_window_sum.11
  49.2 1.4 scatter.4
  50.6 0.7 copy.89
  51.4 1.0 reshape.463
  52.4 0.8 slice.259
  53.2 0.8 slice.260
  55.0 0.7 maximum_convert_fusion.refs_3_
  55.7 10.1 %shard_map.114 = (f32[9,15,8192]{2,1,0:T(8,128)}, bf16[9,16,384]{2,1,0:T(8,128)(2,1)}) custom-call(f32[9,15,8192]{2,1,0:T(8,128)} %refs_0_.1, f32[15,8192]{1,0:T(8,128)} %refs_1_.5, f32[15,8192]{1,0:T(8,128)} %refs_2_.5, f32[9,15,384]{2,1,0:T(8,128)} %maximum_convert_fusion.refs_3_), custom_call_target="tpu_custom_call" | custom-call | flops 22118400 | bytes 9830400 | tf_op jit(solution)/shard_map/pallas_call | solution.py:100
  65.8 16.6 %all-gather.1 = bf16[72,16,384]{2,1,0:T(8,128)(2,1)S(1)} all-gather(bf16[9,16,384]{2,1,0:T(8,128)(2,1)} %get-tuple-element.24), channel_id=3, replica_groups=mesh['grp'=4,'patch'=8] {'patch'}, dimensions={0}, use_global_device_ids=true | all-gather | bytes 995328 | tf_op jit(solution)/shard_map/all_gather | solution.py:169
  82.4 0.7 select_bitcast_fusion.7
  83.8 0.7 multiply_add_fusion
  84.5 3.8 %multiply_convert_fusion.2 = bf16[16,128,256]{2,1,0:T(8,128)(2,1)} fusion(f32[256]{0:T(256)S(1)} %bitcast.174, bf16[4,16,144,128]{3,2,1,0:T(8,128)(2,1)S(1)} %all-to-all-done, bf16[4,144,256,1]{2,1,3,0:T(8,128)(2,1)} %bitcast.166, f32[256]{0:T(256)S(1)} %bitcast.175, bf16[3,256,256]{2,1,0:T(8,128)(2,1)} %param.20), kind=kOutput, calls=%fused_computation.4 | convolution fusion | flops 878706688 | bytes 3835904 | tf_op jit(solution)/shard_map/...h,hj->...j/dot_general | solution.py:191
  88.4 3.0 %multiply_convert_fusion.1 = bf16[16,128,256]{2,1,0:T(8,128)(2,1)} fusion(bf16[16,128,256]{2,1,0:T(8,128)(2,1)} %multiply_convert_fusion.2, f32[256]{0:T(256)S(1)} %bitcast.173, bf16[3,256,256]{2,1,0:T(8,128)(2,1)} %param.20), kind=kOutput, calls=%fused_computation.3 | convolution fusion | flops 271581184 | bytes 2229248 | tf_op jit(solution)/shard_map/...h,hj->...j/dot_general | solution.py:191
  91.3 2.4 %convert_bitcast_fusion = bf16[4,16,9,15,128]{4,3,0,2,1:T(8,128)(2,1)S(1)} fusion(bf16[256,9,4,15,1]{0,3,2,1,4:T(8,128)(2,1)S(1)} %reshape.463, bf16[16,128,256]{2,1,0:T(8,128)(2,1)} %multiply_convert_fusion.1, f32[256]{0:T(256)S(1)} %bitcast.172, bf16[3,256,256]{2,1,0:T(8,128)(2,1)} %param.20), kind=kOutput, calls=%fused_computation | convolution fusion | flops 838918144 | bytes 3668992 | tf_op jit(solution)/shard_map/bch,hvgl->gbvlc/dot_general | solution.py:237
  93.8 0.7 fusion.15
  94.6 5.3 %all-to-all-start.2 = ((f32[8,4,128]{2,1,0:T(4,128)}), f32[8,4,128]{2,1,0:T(4,128)S(1)}, u32[]{:S(2)}, u32[]{:S(2)}) async-start(f32[8,4,128]{2,1,0:T(4,128)} %bitcast.77), calls=%async_computation.2 | async-start | bytes 32768 | tf_op jit(solution)/shard_map/all_to_all | solution.py:244
  100.0 0.8 slice.268
  101.2 4.0 %copy.91 = bf16[4,16,9,15,128]{4,1,3,2,0:T(8,128)(2,1)} copy(bf16[4,16,9,15,128]{4,3,0,2,1:T(8,128)(2,1)S(1)} %convert_bitcast_fusion) | data formatting | bytes 4423680 | tf_op jit(solution)/shard_map/convert_element_type | solution.py:239
  105.6 4.2 %all-to-all-start.1 = ((bf16[4,16,9,15,128]{4,1,3,2,0:T(8,128)(2,1)}), bf16[4,16,9,15,128]{4,1,3,2,0:T(8,128)(2,1)S(1)}, u32[]{:S(2)}, u32[]{:S(2)}) async-start(bf16[4,16,9,15,128]{4,1,3,2,0:T(8,128)(2,1)} %copy.91), calls=%async_computation.1 | async-start | bytes 4423680 | tf_op jit(solution)/shard_map/all_to_all | solution.py:247
  110.3 0.7 maximum_convert_fusion.1.refs_3_
  111.1 10.1 %shard_map.115 = (f32[9,15,8192]{2,1,0:T(8,128)}, bf16[9,16,384]{2,1,0:T(8,128)(2,1)}) custom-call(f32[9,15,8192]{2,1,0:T(8,128)} %get-tuple-element.23.refs_0_, f32[15,8192]{1,0:T(8,128)} %refs_1_.5, f32[15,8192]{1,0:T(8,128)} %refs_2_.5, f32[9,15,384]{2,1,0:T(8,128)} %maximum_convert_fusion.1.refs_3_), custom_call_target="tpu_custom_call" | custom-call | flops 22118400 | bytes 9830400 | tf_op jit(solution)/shard_map/pallas_call | solution.py:100
  121.2 16.1 %all-gather.2 = bf16[72,16,384]{2,1,0:T(8,128)(2,1)S(1)} all-gather(bf16[9,16,384]{2,1,0:T(8,128)(2,1)} %get-tuple-element.26), channel_id=4, replica_groups=mesh['grp'=4,'patch'=8] {'patch'}, dimensions={0}, use_global_device_ids=true | all-gather | bytes 995328 | tf_op jit(solution)/shard_map/all_gather | solution.py:169
  139.0 0.7 maximum_convert_fusion.2.refs_3_
  139.8 2.0 %copy.92 = bf16[4,16,9,15,128]{4,3,2,1,0:T(8,128)(2,1)} copy(bf16[4,16,9,15,128]{4,1,3,2,0:T(8,128)(2,1)S(1)} %all-to-all-done.1) | data formatting | bytes 4423680 | tf_op jit(solution)/shard_map/all_to_all | solution.py:247
  141.8 10.4 %shard_map.116 = (f32[9,15,8192]{2,1,0:T(8,128)}, bf16[9,16,384]{2,1,0:T(8,128)(2,1)}) custom-call(f32[9,15,8192]{2,1,0:T(8,128)} %get-tuple-element.25.refs_0_, f32[15,8192]{1,0:T(8,128)} %refs_1_.5, f32[15,8192]{1,0:T(8,128)} %refs_2_.5, f32[9,15,384]{2,1,0:T(8,128)} %maximum_convert_fusion.2.refs_3_, bf16[64,9,15,128]{3,2,1,0:T(8,128)(2,1)} %bitcast.153), custom_call_target="tpu_custom_call" | custom-call | flops 22118400 | bytes 9830400 | tf_op jit(solution)/shard_map/pallas_call | solution.py:100
  (84 shorter events, 9.4 us)
Async XLA Ops:
  10.4 5.4 %copy-start.4 = (s32[8,4]{0,1:T(4,128)S(1)}, s32[8,4]{0,1:T(4,128)}, u32[]{:S(2)}) copy-start(s32[8,4]{0,1:T(4,128)} %param.23) | copy-start | bytes 388
  10.4 13.5 %copy-start = (bf16[556,256]{1,0:T(8,128)(2,1)S(1)}, bf16[556,256]{1,0:T(8,128)(2,1)}, u32[]{:S(2)}) copy-start(bf16[556,256]{1,0:T(8,128)(2,1)} %param.18) | copy-start | bytes 854020
  10.4 14.7 %copy-start.5 = (s32[512,1]{0,1:T(1,128)S(1)}, s32[512,1]{0,1:T(1,128)}, u32[]{:S(2)}) copy-start(s32[512,1]{0,1:T(1,128)} %param.22) | copy-start | bytes 6148
  10.4 16.2 %slice-start = ((bf16[556,256]{1,0:T(8,128)(2,1)}), bf16[540,256]{1,0:T(8,128)(2,1)S(1)}, s32[]{:S(2)}) async-start(bf16[556,256]{1,0:T(8,128)(2,1)} %param.18), calls=%async_computation.3 | async-start | bytes 557056 | tf_op jit(solution)/shard_map/slice | solution.py:226
  10.4 74.1 %all-to-all-start = ((bf16[4,16,144,128]{3,2,1,0:T(8,128)(2,1)}), bf16[4,16,144,128]{3,2,1,0:T(8,128)(2,1)S(1)}, u32[]{:S(2)}, u32[]{:S(2)}) async-start(bf16[4,16,144,128]{3,2,1,0:T(8,128)(2,1)} %bitcast.156), calls=%async_computation | async-start | bytes 4718592 | tf_op jit(solution)/shard_map/all_to_all | solution.py:231
  25.9 0.8 copy-start.2
  65.8 17.8 %copy-start.1 = (s32[4,16,8]{2,1,0:T(8,128)S(1)}, s32[4,16,8]{2,1,0:T(8,128)}, u32[]{:S(2)}) copy-start(s32[4,16,8]{2,1,0:T(8,128)} %reduce_window_sum.11) | copy-start | bytes 6148
  65.8 18.7 %copy-start.3 = (f32[4,256]{1,0:T(4,128)S(1)}, f32[4,256]{1,0:T(4,128)}, u32[]{:S(2)}) copy-start(f32[4,256]{1,0:T(4,128)} %param.19) | copy-start | bytes 12292
  94.6 11.0 %all-to-all-start.2 = ((f32[8,4,128]{2,1,0:T(4,128)}), f32[8,4,128]{2,1,0:T(4,128)S(1)}, u32[]{:S(2)}, u32[]{:S(2)}) async-start(f32[8,4,128]{2,1,0:T(4,128)} %bitcast.77), calls=%async_computation.2 | async-start | bytes 32768 | tf_op jit(solution)/shard_map/all_to_all | solution.py:244
  105.6 34.2 %all-to-all-start.1 = ((bf16[4,16,9,15,128]{4,1,3,2,0:T(8,128)(2,1)}), bf16[4,16,9,15,128]{4,1,3,2,0:T(8,128)(2,1)S(1)}, u32[]{:S(2)}, u32[]{:S(2)}) async-start(bf16[4,16,9,15,128]{4,1,3,2,0:T(8,128)(2,1)} %copy.91), calls=%async_computation.1 | async-start | bytes 4423680 | tf_op jit(solution)/shard_map/all_to_all | solution.py:247

commit v8 on v7

--- a/solution.py
+++ b/solution.py
@@ -50,7 +50,9 @@
             + KAPPA * (up + down + west + east - 4.0 * cur)
         )
         if with_tend:
-            val = val + PHYS_DT * tend_ref[x, 0].astype(jnp.float32)
+            quarter = rows // tend_ref.shape[0]
+            block = tend_ref[x // quarter, 0, 0:levels, (x % quarter) * PY : (x % quarter + 1) * PY]
+            val = val + PHYS_DT * block.astype(jnp.float32)
         out_ref[0, :, here] = val
         packed = val.astype(jnp.bfloat16)
         stack_ref[x * slot : x * slot + levels, :] = packed
@@ -95,7 +97,7 @@
     ]
     args = [tracer, along_x, along_y, halo]
     if with_tend:
-        in_specs.append(pl.BlockSpec((tend.shape[0], 1, levels, PY), lambda v: (0, v, 0, 0)))
+        in_specs.append(pl.BlockSpec((tend.shape[0], 1) + tend.shape[2:], lambda v: (0, v, 0, 0)))
         args.append(tend)
     return pl.pallas_call(
         functools.partial(stencil_kernel, with_tend=with_tend),
@@ -234,18 +236,23 @@
         + b_hidden[0]
     )
     hidden = hidden_layers(activate(pre_act), b_hidden, w_mid)
-    tendency = jnp.einsum(
-        "bch,hvgl->gbvlc", hidden, w_split, preferred_element_type=jnp.float32
+    w_pad = jnp.pad(w_split, ((0, 0), (0, 0), (0, 0), (0, slot - level_share)))
+    w_rows = w_pad.transpose(2, 1, 3, 0).reshape(groups * VARS * slot, -1)
+    hidden_flat = hidden.reshape(quarter_rows * PY, -1)
+    tendency = lax.dot_general(
+        w_rows, hidden_flat, (((1,), (1,)), ((), ())), preferred_element_type=jnp.float32
     ).astype(jnp.bfloat16)
-    heating = HEAT_WEIGHT * jnp.sum(tendency[:, :, 0].astype(jnp.float32), axis=(0, 2))
+    tendency = tendency.reshape(groups, VARS, slot, quarter_rows * PY)
+    heating = HEAT_WEIGHT * jnp.sum(
+        tendency[:, 0, 0:level_share].astype(jnp.float32), axis=(0, 1)
+    ).reshape(quarter_rows, PY)
     packed = jnp.dot(
         selector_here.astype(jnp.float32), heating, precision=lax.Precision.HIGHEST
     ).reshape(patches, capacity, PY)
     owner_heating = lax.all_to_all(
         packed, "patch", split_axis=0, concat_axis=0, tiled=True
     ).reshape(slot_count, PY)
-    arrived = lax.all_to_all(tendency, "grp", split_axis=0, concat_axis=0, tiled=True)
-    tendency_here = arrived.reshape(PX, VARS, level_share, PY)
+    tendency_here = lax.all_to_all(tendency, "grp", split_axis=0, concat_axis=0, tiled=True)
     advected = state
     for section_index in range(SUBSTEPS):
         halo = exchange_halo(payload, beside_all, patches, level_share)

time: 155 us -> 158 us (1.019)
  waiting for transfers between devices: 0.35 us -> 4.63 us
    all_to_all x1, waiting for transfers between devices: 0.35 us -> 4.62 us  [on_device(): lax.all_to_all(packed, 'patch', split_axis=0, concat_axis=0, tiled=True)]
    convert_element_type x1 -> x0, local copies, waits for them, and re-layouts: 3.97 us -> none  [on_device(): tendency = jnp.einsum('bch,hvgl->gbvlc', hidden, w_split, preferred_eleme...]
    unnamed x14 -> x28, local copies, waits for them, and re-layouts: 1.14 us -> 3.75 us
    all_to_all x1 -> x0, local copies, waits for them, and re-layouts: 2.04 us -> none  [on_device(): lax.all_to_all(tendency, 'grp', split_axis=0, concat_axis=0, tiled=True)]
  transfers between devices with their start and end apart: 3 -> 3, of which waited for: 1 -> 1; matrix products, arithmetic and copies ran while one was open for 18% -> 16% of each run, Pallas kernels for 13% -> 13%
where the time goes in v8:
time: 158 us; the launch traced here: 156 us
  blocking collectives  48.9 us (31%)
  Pallas kernels  38.7 us (24%)
  local copies, waits for them, and re-layouts  19.2 us (12%)
  starting transfers between devices  14.9 us (9%)
  other arithmetic  11.5 us (7%)
  matrix products  9.29 us (6%)
  between operations  8.74 us (6%)
  waiting for transfers between devices  4.63 us (3%)
    all_gather x3, blocking collectives, exchange_halo(): got = lax.all_gather(payload, 'patch', axis=0, tiled=False)  48.9 us
    pallas_call x3, Pallas kernels, stencil(): pl.pallas_call(functools.partial(stencil_kernel, with_tend=with_tend), gr...  30.5 us
    pallas_call x1, Pallas kernels, first_edges(): pl.pallas_call(functools.partial(pack_kernel, n_surf=n_surf), grid=(n_var...  8.16 us
    dot_general x2, matrix products, hidden_layers(): jnp.einsum('...h,hj->...j', hidden, w_mid[layer_index], preferred_element...  6.28 us
    all_to_all x1, starting transfers between devices, on_device(): lax.all_to_all(by_quarter, 'grp', split_axis=0, concat_axis=0, tiled=True)  5.34 us
    all_to_all x1, starting transfers between devices, on_device(): lax.all_to_all(packed, 'patch', split_axis=0, concat_axis=0, tiled=True)  5.31 us
    all_to_all x1, waiting for transfers between devices, on_device(): lax.all_to_all(packed, 'patch', split_axis=0, concat_axis=0, tiled=True)  4.62 us
    all_to_all x1, starting transfers between devices, on_device(): lax.all_to_all(tendency, 'grp', split_axis=0, concat_axis=0, tiled=True)  4.24 us
  transfers between devices with their start and end apart: 3, of which 1 were waited for; matrix products, arithmetic and copies ran while one was open for 16% of the time, Pallas kernels for 13%

profile of v8, /device:TPU:0, one launch (start us, length us, event | category | flops | bytes accessed | tf_op | source)
XLA Modules:
  0.0 155.9 jit_solution(13509831654374405424)
XLA Ops:
  0.6 1.6 %copy.69.surf_ref = bf16[4,1,8192]{2,1,0:T(2,128)(2,1)} copy(bf16[4,1,8192]{2,0,1:T(4,128)(2,1)} %bitcast.170) | data formatting | bytes 131072 | tf_op jit(solution)/shard_map/reshape | solution.py:146
  2.2 8.2 %shard_map.113 = (bf16[9,16,384]{2,1,0:T(8,128)(2,1)}, bf16[64,9,16,128]{3,2,1,0:T(8,128)(2,1)}) custom-call(f32[9,15,8192]{2,1,0:T(8,128)} %refs_0_.1, bf16[4,1,8192]{2,1,0:T(2,128)(2,1)} %copy.69.surf_ref), custom_call_target="tpu_custom_call" | custom-call | bytes 5529600 | tf_op jit(solution)/shard_map/pallas_call | solution.py:147
  10.4 5.3 %all-to-all-start = ((bf16[4,16,144,128]{3,2,1,0:T(8,128)(2,1)}), bf16[4,16,144,128]{3,2,1,0:T(8,128)(2,1)S(1)}, u32[]{:S(2)}, u32[]{:S(2)}) async-start(bf16[4,16,144,128]{3,2,1,0:T(8,128)(2,1)} %bitcast.154), calls=%async_computation | async-start | bytes 4718592 | tf_op jit(solution)/shard_map/all_to_all | solution.py:233
  28.5 0.8 reshape.180
  29.3 16.2 %all-gather = bf16[72,16,384]{2,1,0:T(8,128)(2,1)S(1)} all-gather(bf16[9,16,384]{2,1,0:T(8,128)(2,1)} %get-tuple-element.22), channel_id=2, replica_groups=mesh['grp'=4,'patch'=8] {'patch'}, dimensions={0}, use_global_device_ids=true | all-gather | bytes 995328 | tf_op jit(solution)/shard_map/all_gather | solution.py:171
  45.6 0.8 select_bitcast_fusion.11
  46.9 0.8 and_reduce_fusion
  47.7 2.7 %broadcast_select_fusion = bf16[4,4,1,256]{3,2,0,1:T(2,128)(2,1)S(1)} fusion(pred[]{:T(512)} %and_reduce_fusion, bf16[4,4,1,256]{3,1,0,2:T(4,128)(2,1)} %reshape.184, s32[]{:T(128)} %bitcast.57, s32[]{:T(128)} %bitcast.58, bf16[4,9,15,256]{3,2,0,1:T(8,128)(2,1)S(1)} %bitcast.152), kind=kLoop, calls=%fused_computation.44 | loop fusion | flops 4096 | bytes 292873 | tf_op jit(solution)/shard_map/select.1
  50.4 1.0 pad_bitcast_fusion
  52.7 1.4 scatter.4
  54.1 0.7 copy.93
  54.9 0.8 slice.259
  55.7 0.8 slice.260
  56.7 0.8 copy.74
  58.1 0.7 maximum_convert_fusion.refs_3_
  58.9 10.1 %shard_map.114 = (f32[9,15,8192]{2,1,0:T(8,128)}, bf16[9,16,384]{2,1,0:T(8,128)(2,1)}) custom-call(f32[9,15,8192]{2,1,0:T(8,128)} %refs_0_.1, f32[15,8192]{1,0:T(8,128)} %refs_1_.5, f32[15,8192]{1,0:T(8,128)} %refs_2_.5, f32[9,15,384]{2,1,0:T(8,128)} %maximum_convert_fusion.refs_3_), custom_call_target="tpu_custom_call" | custom-call | flops 22118400 | bytes 9830400 | tf_op jit(solution)/shard_map/pallas_call | solution.py:102
  69.0 16.6 %all-gather.1 = bf16[72,16,384]{2,1,0:T(8,128)(2,1)S(1)} all-gather(bf16[9,16,384]{2,1,0:T(8,128)(2,1)} %get-tuple-element.24), channel_id=3, replica_groups=mesh['grp'=4,'patch'=8] {'patch'}, dimensions={0}, use_global_device_ids=true | all-gather | bytes 995328 | tf_op jit(solution)/shard_map/all_gather | solution.py:171
  85.5 0.7 select_bitcast_fusion.7
  87.5 3.7 %multiply_convert_fusion.2 = bf16[16,128,256]{2,1,0:T(8,128)(2,1)} fusion(f32[256]{0:T(256)S(1)} %bitcast.175, bf16[4,16,144,128]{3,2,1,0:T(8,128)(2,1)S(1)} %all-to-all-done, bf16[4,144,256,1]{2,1,3,0:T(8,128)(2,1)S(1)} %bitcast.166, f32[256]{0:T(256)S(1)} %bitcast.176, bf16[3,256,256]{2,1,0:T(8,128)(2,1)} %param.20), kind=kOutput, calls=%fused_computation.4 | convolution fusion | flops 878706688 | bytes 3835904 | tf_op jit(solution)/shard_map/...h,hj->...j/dot_general | solution.py:193
  91.2 2.6 %multiply_convert_fusion = bf16[16,128,256]{2,1,0:T(8,128)(2,1)S(1)} fusion(f32[256]{0:T(256)S(1)} %bitcast.174, bf16[16,128,256]{2,1,0:T(8,128)(2,1)} %multiply_convert_fusion.2, f32[256]{0:T(256)S(1)} %bitcast.173, bf16[3,256,256]{2,1,0:T(8,128)(2,1)} %param.20), kind=kOutput, calls=%fused_computation.2 | convolution fusion | flops 543162368 | bytes 2361344 | tf_op jit(solution)/shard_map/...h,hj->...j/dot_general | solution.py:193
  93.8 2.3 %convolution_convert_fusion = bf16[576,2048]{1,0:T(8,128)(2,1)} fusion(bf16[576,256]{1,0:T(8,128)(2,1)S(1)} %bitcast.158, bf16[2048,256]{1,0:T(8,128)(2,1)S(1)} %bitcast.162), kind=kOutput, calls=%fused_computation | convolution fusion | flops 605159424 | bytes 3702784 | tf_op jit(solution)/shard_map/dot_general | solution.py:242
  96.0 1.0 convert_reduce_fusion
  97.1 0.8 fusion.11
  97.8 5.3 %all-to-all-start.2 = ((f32[8,4,128]{2,1,0:T(4,128)}), f32[8,4,128]{2,1,0:T(4,128)S(1)}, u32[]{:S(2)}, u32[]{:S(2)}) async-start(f32[8,4,128]{2,1,0:T(4,128)} %fusion.11), calls=%async_computation.2 | async-start | bytes 32768 | tf_op jit(solution)/shard_map/all_to_all | solution.py:252
  103.1 0.8 slice.273
  104.1 4.6 %all-to-all-done.2 = f32[8,4,128]{2,1,0:T(4,128)S(1)} async-done(((f32[8,4,128]{2,1,0:T(4,128)}), f32[8,4,128]{2,1,0:T(4,128)S(1)}, u32[]{:S(2)}, u32[]{:S(2)}) %all-to-all-start.2) | async-done | bytes 16416 | tf_op jit(solution)/shard_map/all_to_all | solution.py:252
  108.8 4.2 %all-to-all-start.1 = ((bf16[4,9,16,2048]{3,2,1,0:T(8,128)(2,1)}), bf16[4,9,16,2048]{3,2,1,0:T(8,128)(2,1)S(1)}, u32[]{:S(2)}, u32[]{:S(2)}) async-start(bf16[4,9,16,2048]{3,2,1,0:T(8,128)(2,1)} %bitcast.74), calls=%async_computation.1 | async-start | bytes 4718592 | tf_op jit(solution)/shard_map/all_to_all | solution.py:255
  114.8 10.1 %shard_map.115 = (f32[9,15,8192]{2,1,0:T(8,128)}, bf16[9,16,384]{2,1,0:T(8,128)(2,1)}) custom-call(f32[9,15,8192]{2,1,0:T(8,128)} %get-tuple-element.23.refs_0_, f32[15,8192]{1,0:T(8,128)} %refs_1_.5, f32[15,8192]{1,0:T(8,128)} %refs_2_.5, f32[9,15,384]{2,1,0:T(8,128)} %maximum_convert_fusion.1.refs_3_), custom_call_target="tpu_custom_call" | custom-call | flops 22118400 | bytes 9830400 | tf_op jit(solution)/shard_map/pallas_call | solution.py:102
  124.9 16.1 %all-gather.2 = bf16[72,16,384]{2,1,0:T(8,128)(2,1)S(1)} all-gather(bf16[9,16,384]{2,1,0:T(8,128)(2,1)} %get-tuple-element.26), channel_id=4, replica_groups=mesh['grp'=4,'patch'=8] {'patch'}, dimensions={0}, use_global_device_ids=true | all-gather | bytes 995328 | tf_op jit(solution)/shard_map/all_gather | solution.py:171
  142.8 0.7 maximum_convert_fusion.2.refs_3_
  143.5 1.4 copy-done
  145.0 10.3 %shard_map.116 = (f32[9,15,8192]{2,1,0:T(8,128)}, bf16[9,16,384]{2,1,0:T(8,128)(2,1)}) custom-call(f32[9,15,8192]{2,1,0:T(8,128)} %get-tuple-element.25.refs_0_, f32[15,8192]{1,0:T(8,128)} %refs_1_.5, f32[15,8192]{1,0:T(8,128)} %refs_2_.5, f32[9,15,384]{2,1,0:T(8,128)} %maximum_convert_fusion.2.refs_3_, bf16[4,9,16,2048]{3,2,1,0:T(8,128)(2,1)} %copy-done), custom_call_target="tpu_custom_call" | custom-call | flops 22118400 | bytes 9830400 | tf_op jit(solution)/shard_map/pallas_call | solution.py:102
  (99 shorter events, 13.2 us)
Async XLA Ops:
  10.4 5.4 %copy-start.10 = (s32[8,4]{0,1:T(4,128)S(1)}, s32[8,4]{0,1:T(4,128)}, u32[]{:S(2)}) copy-start(s32[8,4]{0,1:T(4,128)} %param.23) | copy-start | bytes 388
  10.4 13.7 %copy-start.1 = (bf16[556,256]{1,0:T(8,128)(2,1)S(1)}, bf16[556,256]{1,0:T(8,128)(2,1)}, u32[]{:S(2)}) copy-start(bf16[556,256]{1,0:T(8,128)(2,1)} %param.18) | copy-start | bytes 854020
  10.4 15.4 %copy-start.11 = (s32[512,1]{0,1:T(1,128)S(1)}, s32[512,1]{0,1:T(1,128)}, u32[]{:S(2)}) copy-start(s32[512,1]{0,1:T(1,128)} %param.22) | copy-start | bytes 6148
  10.4 18.0 %slice-start = ((bf16[556,256]{1,0:T(8,128)(2,1)}), bf16[540,256]{1,0:T(8,128)(2,1)S(1)}, s32[]{:S(2)}) async-start(bf16[556,256]{1,0:T(8,128)(2,1)} %param.18), calls=%async_computation.3 | async-start | bytes 557056 | tf_op jit(solution)/shard_map/slice | solution.py:228
  10.4 18.1 %copy-start.3 = (bf16[256,540]{0,1:T(8,128)(2,1)S(1)}, bf16[256,540]{0,1:T(8,128)(2,1)}, u32[]{:S(2)}) copy-start(bf16[256,540]{0,1:T(8,128)(2,1)} %param.21) | copy-start | bytes 829444
  10.4 77.1 %all-to-all-start = ((bf16[4,16,144,128]{3,2,1,0:T(8,128)(2,1)}), bf16[4,16,144,128]{3,2,1,0:T(8,128)(2,1)S(1)}, u32[]{:S(2)}, u32[]{:S(2)}) async-start(bf16[4,16,144,128]{3,2,1,0:T(8,128)(2,1)} %bitcast.154), calls=%async_computation | async-start | bytes 4718592 | tf_op jit(solution)/shard_map/all_to_all | solution.py:233
  26.6 0.6 copy-start.6
  27.2 0.6 copy-start.7
  28.4 18.5 %copy-start.12 = (s32[4]{0:T(128)S(1)}, s32[4]{0:T(128)}, u32[]{:S(2)}) copy-start(s32[4]{0:T(128)} %constant.98.clone.1) | copy-start | bytes 52
  46.4 5.7 %copy-start.4 = (s32[4,16,8]{2,1,0:T(8,128)S(1)}, s32[4,16,8]{2,1,0:T(8,128)}, u32[]{:S(2)}) copy-start(s32[4,16,8]{2,1,0:T(8,128)} %fusion.8) | copy-start | bytes 6148
  68.9 17.6 %copy-start.5 = (s32[4,16,8]{2,1,0:T(8,128)S(1)}, s32[4,16,8]{2,1,0:T(8,128)}, u32[]{:S(2)}) copy-start(s32[4,16,8]{2,1,0:T(8,128)} %reduce_window_sum.11) | copy-start | bytes 6148
  68.9 17.6 %copy-start.8 = (s32[4,16]{1,0:T(4,128)S(1)}, s32[4,16]{1,0:T(4,128)}, u32[]{:S(2)}) copy-start(s32[4,16]{1,0:T(4,128)} %copy-done.7) | copy-start | bytes 772
  69.0 18.5 %copy-start.9 = (f32[4,256]{1,0:T(4,128)S(1)}, f32[4,256]{1,0:T(4,128)}, u32[]{:S(2)}) copy-start(f32[4,256]{1,0:T(4,128)} %param.19) | copy-start | bytes 12292
  69.0 18.5 %copy-start.2 = (bf16[4,9,16,256]{3,2,1,0:T(8,128)(2,1)S(1)}, bf16[4,9,16,256]{3,2,1,0:T(8,128)(2,1)}, u32[]{:S(2)}) copy-start(bf16[4,9,16,256]{3,2,1,0:T(8,128)(2,1)} %copy.93) | copy-start | bytes 884740
  97.8 11.0 %all-to-all-start.2 = ((f32[8,4,128]{2,1,0:T(4,128)}), f32[8,4,128]{2,1,0:T(4,128)S(1)}, u32[]{:S(2)}, u32[]{:S(2)}) async-start(f32[8,4,128]{2,1,0:T(4,128)} %fusion.11), calls=%async_computation.2 | async-start | bytes 32768 | tf_op jit(solution)/shard_map/all_to_all | solution.py:252
  108.8 34.8 %all-to-all-start.1 = ((bf16[4,9,16,2048]{3,2,1,0:T(8,128)(2,1)}), bf16[4,9,16,2048]{3,2,1,0:T(8,128)(2,1)S(1)}, u32[]{:S(2)}, u32[]{:S(2)}) async-start(bf16[4,9,16,2048]{3,2,1,0:T(8,128)(2,1)} %bitcast.74), calls=%async_computation.1 | async-start | bytes 4718592 | tf_op jit(solution)/shard_map/all_to_all | solution.py:255
  143.5 1.4 copy-start

commit v9 on v8

--- a/solution.py
+++ b/solution.py
@@ -214,8 +214,6 @@
     slot_count = patches * capacity
     slot = 16
     beside_all = jnp.take(neighbours, patch_here, axis=0)
-    payload, feat = first_edges(state, surface)
-    by_quarter = feat.reshape(groups, quarter_rows, VARS * slot, PY)
     owners_all = owner_map.reshape(patches, groups, quarter_rows)
     owners_here = jnp.take(owners_all, patch_here, axis=0)
     matches = (owners_here[..., None] == jnp.arange(patches, dtype=jnp.int32)).astype(jnp.int32)
@@ -230,14 +228,17 @@
     surf_part = w_in[VARS * LEV :].reshape(groups, surf_share, -1)
     w_local = state_part.at[:, :surf_share, level_share, :].set(surf_part).reshape(groups, VARS * slot, -1)
     w_split = w_out.reshape(-1, VARS, groups, level_share)
+    w_pad = jnp.pad(w_split, ((0, 0), (0, 0), (0, 0), (0, slot - level_share)))
+    w_rows = w_pad.transpose(2, 1, 3, 0).reshape(groups * VARS * slot, -1)
+    w_local, w_rows, state_in = lax.optimization_barrier((w_local, w_rows, state))
+    payload, feat = first_edges(state_in, surface)
+    by_quarter = feat.reshape(groups, quarter_rows, VARS * slot, PY)
     regrouped = lax.all_to_all(by_quarter, "grp", split_axis=0, concat_axis=0, tiled=True)
     pre_act = (
         jnp.einsum("gbfc,gfh->bch", regrouped, w_local, preferred_element_type=jnp.float32)
         + b_hidden[0]
     )
     hidden = hidden_layers(activate(pre_act), b_hidden, w_mid)
-    w_pad = jnp.pad(w_split, ((0, 0), (0, 0), (0, 0), (0, slot - level_share)))
-    w_rows = w_pad.transpose(2, 1, 3, 0).reshape(groups * VARS * slot, -1)
     hidden_flat = hidden.reshape(quarter_rows * PY, -1)
     tendency = lax.dot_general(
         w_rows, hidden_flat, (((1,), (1,)), ((), ())), preferred_element_type=jnp.float32

time: 158 us -> 154 us (0.975)
  local copies, waits for them, and re-layouts: 19.2 us -> 17 us
    unnamed x28 -> x14, local copies, waits for them, and re-layouts: 3.75 us -> 2.58 us
  transfers between devices with their start and end apart: 3 -> 3, of which waited for: 1 -> 1; matrix products, arithmetic and copies ran while one was open for 16% -> 10% of each run, Pallas kernels for 13% -> 13%
where the time goes in v9:
time: 154 us; the launch traced here: 153 us
  blocking collectives  48.9 us (32%)
  Pallas kernels  38.7 us (25%)
  local copies, waits for them, and re-layouts  17 us (11%)
  starting transfers between devices  14.9 us (10%)
  other arithmetic  10.7 us (7%)
  matrix products  9.29 us (6%)
  between operations  8.48 us (6%)
  waiting for transfers between devices  4.63 us (3%)
    all_gather x3, blocking collectives, exchange_halo(): got = lax.all_gather(payload, 'patch', axis=0, tiled=False)  48.9 us
    pallas_call x3, Pallas kernels, stencil(): pl.pallas_call(functools.partial(stencil_kernel, with_tend=with_tend), gr...  30.5 us
    pallas_call x1, Pallas kernels, first_edges(): pl.pallas_call(functools.partial(pack_kernel, n_surf=n_surf), grid=(n_var...  8.18 us
    dot_general x2, matrix products, hidden_layers(): jnp.einsum('...h,hj->...j', hidden, w_mid[layer_index], preferred_element...  6.28 us
    all_to_all x1, starting transfers between devices, on_device(): lax.all_to_all(by_quarter, 'grp', split_axis=0, concat_axis=0, tiled=True)  5.33 us
    all_to_all x1, starting transfers between devices, on_device(): lax.all_to_all(packed, 'patch', split_axis=0, concat_axis=0, tiled=True)  5.31 us
    all_to_all x1, waiting for transfers between devices, on_device(): lax.all_to_all(packed, 'patch', split_axis=0, concat_axis=0, tiled=True)  4.62 us
    all_to_all x1, starting transfers between devices, on_device(): lax.all_to_all(tendency, 'grp', split_axis=0, concat_axis=0, tiled=True)  4.24 us
  transfers between devices with their start and end apart: 3, of which 1 were waited for; matrix products, arithmetic and copies ran while one was open for 10% of the time, Pallas kernels for 13%

profile of v9, /device:TPU:0, one launch (start us, length us, event | category | flops | bytes accessed | tf_op | source)
XLA Modules:
  0.0 152.6 jit_solution(6468072475726125805)
XLA Ops:
  0.6 0.8 slice.177
  1.4 1.0 slice.176
  3.0 1.6 %copy.72.surf_ref = bf16[4,1,8192]{2,1,0:T(2,128)(2,1)} copy(bf16[4,1,8192]{2,0,1:T(4,128)(2,1)} %bitcast.171) | data formatting | bytes 131072 | tf_op jit(solution)/shard_map/reshape | solution.py:146
  4.7 1.4 and_reduce_fusion
  6.1 1.9 %broadcast_select_fusion = bf16[4,4,1,256]{3,2,0,1:T(2,128)(2,1)S(1)} fusion(pred[]{:T(512)} %and_reduce_fusion, bf16[4,4,1,256]{3,1,0,2:T(4,128)(2,1)S(1)} %reshape.165, s32[]{:T(128)} %bitcast.2, s32[]{:T(128)} %bitcast.3, bf16[4,9,15,256]{3,2,0,1:T(8,128)(2,1)S(1)} %bitcast.154), kind=kLoop, calls=%fused_computation.45 | loop fusion | flops 4096 | bytes 292873 | tf_op jit(solution)/shard_map/select.1
  8.0 1.3 scatter.4
  9.3 0.7 copy.70
  10.2 8.2 %shard_map.113 = (bf16[9,16,384]{2,1,0:T(8,128)(2,1)}, bf16[64,9,16,128]{3,2,1,0:T(8,128)(2,1)}) custom-call(f32[9,15,8192]{2,1,0:T(8,128)} %refs_0_.1, bf16[4,1,8192]{2,1,0:T(2,128)(2,1)} %copy.72.surf_ref), custom_call_target="tpu_custom_call" | custom-call | bytes 5529600 | tf_op jit(solution)/shard_map/pallas_call | solution.py:147
  18.4 5.3 %all-to-all-start = ((bf16[4,16,144,128]{3,2,1,0:T(8,128)(2,1)}), bf16[4,16,144,128]{3,2,1,0:T(8,128)(2,1)S(1)}, u32[]{:S(2)}, u32[]{:S(2)}) async-start(bf16[4,16,144,128]{3,2,1,0:T(8,128)(2,1)} %bitcast.155), calls=%async_computation | async-start | bytes 4718592 | tf_op jit(solution)/shard_map/all_to_all | solution.py:236
  33.7 16.2 %all-gather = bf16[72,16,384]{2,1,0:T(8,128)(2,1)S(1)} all-gather(bf16[9,16,384]{2,1,0:T(8,128)(2,1)} %get-tuple-element.26), channel_id=2, replica_groups=mesh['grp'=4,'patch'=8] {'patch'}, dimensions={0}, use_global_device_ids=true | all-gather | bytes 995328 | tf_op jit(solution)/shard_map/all_gather | solution.py:171
  49.9 0.7 select_bitcast_fusion.11
  51.2 0.8 fusion.10
  52.1 0.8 slice.259
  52.9 0.8 slice.260
  55.4 10.1 %shard_map.114 = (f32[9,15,8192]{2,1,0:T(8,128)}, bf16[9,16,384]{2,1,0:T(8,128)(2,1)}) custom-call(f32[9,15,8192]{2,1,0:T(8,128)} %refs_0_.1, f32[15,8192]{1,0:T(8,128)} %refs_1_.5, f32[15,8192]{1,0:T(8,128)} %refs_2_.5, f32[9,15,384]{2,1,0:T(8,128)} %maximum_convert_fusion.refs_3_), custom_call_target="tpu_custom_call" | custom-call | flops 22118400 | bytes 9830400 | tf_op jit(solution)/shard_map/pallas_call | solution.py:102
  65.5 16.6 %all-gather.1 = bf16[72,16,384]{2,1,0:T(8,128)(2,1)S(1)} all-gather(bf16[9,16,384]{2,1,0:T(8,128)(2,1)} %get-tuple-element.28), channel_id=3, replica_groups=mesh['grp'=4,'patch'=8] {'patch'}, dimensions={0}, use_global_device_ids=true | all-gather | bytes 995328 | tf_op jit(solution)/shard_map/all_gather | solution.py:171
  83.3 0.9 fusion.23
  84.2 3.7 %multiply_convert_fusion.2 = bf16[16,128,256]{2,1,0:T(8,128)(2,1)} fusion(f32[256]{0:T(256)S(1)} %bitcast.176, bf16[4,16,144,128]{3,2,1,0:T(8,128)(2,1)S(1)} %all-to-all-done, f32[256]{0:T(256)S(1)} %bitcast.177, bf16[4,144,256]{2,1,0:T(8,128)(2,1)S(1)} %bitcast.167, bf16[3,256,256]{2,1,0:T(8,128)(2,1)} %param.20), kind=kOutput, calls=%fused_computation.4 | convolution fusion | flops 878706688 | bytes 3835904 | tf_op jit(solution)/shard_map/...h,hj->...j/dot_general | solution.py:193
  87.9 2.6 %multiply_convert_fusion = bf16[16,128,256]{2,1,0:T(8,128)(2,1)S(1)} fusion(f32[256]{0:T(256)S(1)} %bitcast.175, bf16[16,128,256]{2,1,0:T(8,128)(2,1)} %multiply_convert_fusion.2, f32[256]{0:T(256)S(1)} %bitcast.174, bf16[3,256,256]{2,1,0:T(8,128)(2,1)} %param.20), kind=kOutput, calls=%fused_computation.2 | convolution fusion | flops 543162368 | bytes 2361344 | tf_op jit(solution)/shard_map/...h,hj->...j/dot_general | solution.py:193
  90.4 2.3 %convolution_convert_fusion = bf16[576,2048]{1,0:T(8,128)(2,1)} fusion(bf16[576,256]{1,0:T(8,128)(2,1)S(1)} %bitcast.159, bf16[2048,256]{1,0:T(8,128)(2,1)S(1)} %bitcast.163), kind=kOutput, calls=%fused_computation | convolution fusion | flops 605159424 | bytes 3702784 | tf_op jit(solution)/shard_map/dot_general | solution.py:243
  92.7 1.0 convert_reduce_fusion
  93.7 0.8 fusion.13
  94.5 5.3 %all-to-all-start.2 = ((f32[8,4,128]{2,1,0:T(4,128)}), f32[8,4,128]{2,1,0:T(4,128)S(1)}, u32[]{:S(2)}, u32[]{:S(2)}) async-start(f32[8,4,128]{2,1,0:T(4,128)} %fusion.13), calls=%async_computation.2 | async-start | bytes 32768 | tf_op jit(solution)/shard_map/all_to_all | solution.py:253
  99.8 0.8 slice.273
  100.8 4.6 %all-to-all-done.2 = f32[8,4,128]{2,1,0:T(4,128)S(1)} async-done(((f32[8,4,128]{2,1,0:T(4,128)}), f32[8,4,128]{2,1,0:T(4,128)S(1)}, u32[]{:S(2)}, u32[]{:S(2)}) %all-to-all-start.2) | async-done | bytes 16416 | tf_op jit(solution)/shard_map/all_to_all | solution.py:253
  105.4 4.2 %all-to-all-start.1 = ((bf16[4,9,16,2048]{3,2,1,0:T(8,128)(2,1)}), bf16[4,9,16,2048]{3,2,1,0:T(8,128)(2,1)S(1)}, u32[]{:S(2)}, u32[]{:S(2)}) async-start(bf16[4,9,16,2048]{3,2,1,0:T(8,128)(2,1)} %bitcast.74), calls=%async_computation.1 | async-start | bytes 4718592 | tf_op jit(solution)/shard_map/all_to_all | solution.py:256
  110.8 0.7 maximum_convert_fusion.1.refs_3_
  111.5 10.1 %shard_map.115 = (f32[9,15,8192]{2,1,0:T(8,128)}, bf16[9,16,384]{2,1,0:T(8,128)(2,1)}) custom-call(f32[9,15,8192]{2,1,0:T(8,128)} %get-tuple-element.27.refs_0_, f32[15,8192]{1,0:T(8,128)} %refs_1_.5, f32[15,8192]{1,0:T(8,128)} %refs_2_.5, f32[9,15,384]{2,1,0:T(8,128)} %maximum_convert_fusion.1.refs_3_), custom_call_target="tpu_custom_call" | custom-call | flops 22118400 | bytes 9830400 | tf_op jit(solution)/shard_map/pallas_call | solution.py:102
  121.6 16.1 %all-gather.2 = bf16[72,16,384]{2,1,0:T(8,128)(2,1)S(1)} all-gather(bf16[9,16,384]{2,1,0:T(8,128)(2,1)} %get-tuple-element.30), channel_id=4, replica_groups=mesh['grp'=4,'patch'=8] {'patch'}, dimensions={0}, use_global_device_ids=true | all-gather | bytes 995328 | tf_op jit(solution)/shard_map/all_gather | solution.py:171
  139.5 0.7 maximum_convert_fusion.2.refs_3_
  140.2 1.4 copy-done
  141.6 10.3 %shard_map.116 = (f32[9,15,8192]{2,1,0:T(8,128)}, bf16[9,16,384]{2,1,0:T(8,128)(2,1)}) custom-call(f32[9,15,8192]{2,1,0:T(8,128)} %get-tuple-element.29.refs_0_, f32[15,8192]{1,0:T(8,128)} %refs_1_.5, f32[15,8192]{1,0:T(8,128)} %refs_2_.5, f32[9,15,384]{2,1,0:T(8,128)} %maximum_convert_fusion.2.refs_3_, bf16[4,9,16,2048]{3,2,1,0:T(8,128)(2,1)} %copy-done), custom_call_target="tpu_custom_call" | custom-call | flops 22118400 | bytes 9830400 | tf_op jit(solution)/shard_map/pallas_call | solution.py:102
  (84 shorter events, 10.4 us)
Async XLA Ops:
  0.6 9.4 %copy-start.2 = (bf16[256,540]{0,1:T(8,128)(2,1)S(1)}, bf16[256,540]{0,1:T(8,128)(2,1)}, u32[]{:S(2)}) copy-start(bf16[256,540]{0,1:T(8,128)(2,1)} %param.21) | copy-start | bytes 829444
  18.4 5.3 %copy-start.4 = (s32[8,4]{0,1:T(4,128)S(1)}, s32[8,4]{0,1:T(4,128)}, u32[]{:S(2)}) copy-start(s32[8,4]{0,1:T(4,128)} %param.23) | copy-start | bytes 388
  18.4 14.0 %copy-start.5 = (s32[512,1]{0,1:T(1,128)S(1)}, s32[512,1]{0,1:T(1,128)}, u32[]{:S(2)}) copy-start(s32[512,1]{0,1:T(1,128)} %param.22) | copy-start | bytes 6148
  18.4 65.7 %all-to-all-start = ((bf16[4,16,144,128]{3,2,1,0:T(8,128)(2,1)}), bf16[4,16,144,128]{3,2,1,0:T(8,128)(2,1)S(1)}, u32[]{:S(2)}, u32[]{:S(2)}) async-start(bf16[4,16,144,128]{3,2,1,0:T(8,128)(2,1)} %bitcast.155), calls=%async_computation | async-start | bytes 4718592 | tf_op jit(solution)/shard_map/all_to_all | solution.py:236
  65.5 17.5 %copy-start.3 = (s32[4,16]{1,0:T(4,128)S(1)}, s32[4,16]{1,0:T(4,128)}, u32[]{:S(2)}) copy-start(s32[4,16]{1,0:T(4,128)} %fusion.19) | copy-start | bytes 772
  65.5 18.7 %copy-start.1 = (bf16[4,9,16,256]{3,2,1,0:T(8,128)(2,1)S(1)}, bf16[4,9,16,256]{3,2,1,0:T(8,128)(2,1)}, u32[]{:S(2)}) copy-start(bf16[4,9,16,256]{3,2,1,0:T(8,128)(2,1)} %copy.70) | copy-start | bytes 884740
  94.5 11.0 %all-to-all-start.2 = ((f32[8,4,128]{2,1,0:T(4,128)}), f32[8,4,128]{2,1,0:T(4,128)S(1)}, u32[]{:S(2)}, u32[]{:S(2)}) async-start(f32[8,4,128]{2,1,0:T(4,128)} %fusion.13), calls=%async_computation.2 | async-start | bytes 32768 | tf_op jit(solution)/shard_map/all_to_all | solution.py:253
  105.4 34.8 %all-to-all-start.1 = ((bf16[4,9,16,2048]{3,2,1,0:T(8,128)(2,1)}), bf16[4,9,16,2048]{3,2,1,0:T(8,128)(2,1)S(1)}, u32[]{:S(2)}, u32[]{:S(2)}) async-start(bf16[4,9,16,2048]{3,2,1,0:T(8,128)(2,1)} %bitcast.74), calls=%async_computation.1 | async-start | bytes 4718592 | tf_op jit(solution)/shard_map/all_to_all | solution.py:256
  140.2 1.4 copy-start

commit v10 on v9

--- a/solution.py
+++ b/solution.py
@@ -230,7 +230,9 @@
     w_split = w_out.reshape(-1, VARS, groups, level_share)
     w_pad = jnp.pad(w_split, ((0, 0), (0, 0), (0, 0), (0, slot - level_share)))
     w_rows = w_pad.transpose(2, 1, 3, 0).reshape(groups * VARS * slot, -1)
-    w_local, w_rows, state_in = lax.optimization_barrier((w_local, w_rows, state))
+    w_local, w_rows, selector_here, beside_all, state_in = lax.optimization_barrier(
+        (w_local, w_rows, selector_here, beside_all, state)
+    )
     payload, feat = first_edges(state_in, surface)
     by_quarter = feat.reshape(groups, quarter_rows, VARS * slot, PY)
     regrouped = lax.all_to_all(by_quarter, "grp", split_axis=0, concat_axis=0, tiled=True)

time: 154 us -> 155 us (level)
  transfers between devices with their start and end apart: 3 -> 3, of which waited for: 1 -> 1; matrix products, arithmetic and copies ran while one was open for 10% -> 8% of each run, Pallas kernels for 13% -> 13%
where the time goes in v10:
time: 155 us; the launch traced here: 153 us
  blocking collectives  48.9 us (32%)
  Pallas kernels  38.8 us (25%)
  local copies, waits for them, and re-layouts  17 us (11%)
  starting transfers between devices  14.7 us (9%)
  other arithmetic  10.9 us (7%)
  matrix products  9.28 us (6%)
  between operations  8.93 us (6%)
  waiting for transfers between devices  4.63 us (3%)
    all_gather x3, blocking collectives, exchange_halo(): got = lax.all_gather(payload, 'patch', axis=0, tiled=False)  48.9 us
    pallas_call x3, Pallas kernels, stencil(): pl.pallas_call(functools.partial(stencil_kernel, with_tend=with_tend), gr...  30.5 us
    pallas_call x1, Pallas kernels, first_edges(): pl.pallas_call(functools.partial(pack_kernel, n_surf=n_surf), grid=(n_var...  8.25 us
    dot_general x2, matrix products, hidden_layers(): jnp.einsum('...h,hj->...j', hidden, w_mid[layer_index], preferred_element...  6.29 us
    all_to_all x1, starting transfers between devices, on_device(): lax.all_to_all(packed, 'patch', split_axis=0, concat_axis=0, tiled=True)  5.32 us
    all_to_all x1, starting transfers between devices, on_device(): lax.all_to_all(by_quarter, 'grp', split_axis=0, concat_axis=0, tiled=True)  5.19 us
    all_to_all x1, waiting for transfers between devices, on_device(): lax.all_to_all(packed, 'patch', split_axis=0, concat_axis=0, tiled=True)  4.62 us
    all_to_all x1, starting transfers between devices, on_device(): lax.all_to_all(tendency, 'grp', split_axis=0, concat_axis=0, tiled=True)  4.23 us
  transfers between devices with their start and end apart: 3, of which 1 were waited for; matrix products, arithmetic and copies ran while one was open for 8% of the time, Pallas kernels for 13%

profile of v10, /device:TPU:0, one launch (start us, length us, event | category | flops | bytes accessed | tf_op | source)
XLA Modules:
  0.0 153.3 jit_solution(7548696310765655997)
XLA Ops:
  0.7 0.8 slice.177
  1.4 1.0 slice.176
  3.6 1.3 reduce.14
  5.0 0.9 fusion.21
  6.3 1.6 %copy.72.surf_ref = bf16[4,1,8192]{2,1,0:T(2,128)(2,1)} copy(bf16[4,1,8192]{2,0,1:T(4,128)(2,1)} %bitcast.173) | data formatting | bytes 131072 | tf_op jit(solution)/shard_map/reshape | solution.py:146
  8.0 1.4 and_reduce_fusion
  9.4 1.9 %broadcast_select_fusion = bf16[4,4,1,256]{3,2,0,1:T(2,128)(2,1)S(1)} fusion(pred[]{:T(512)} %and_reduce_fusion, bf16[4,4,1,256]{3,1,0,2:T(4,128)(2,1)S(1)} %reshape.157, s32[]{:T(128)} %bitcast.1, s32[]{:T(128)} %bitcast.2, bf16[4,9,15,256]{3,2,0,1:T(8,128)(2,1)S(1)} %bitcast.156), kind=kLoop, calls=%fused_computation.45 | loop fusion | flops 4096 | bytes 292873 | tf_op jit(solution)/shard_map/select.1
  11.3 1.3 scatter.4
  12.6 0.7 copy.70
  13.5 8.3 %shard_map.113 = (bf16[9,16,384]{2,1,0:T(8,128)(2,1)}, bf16[64,9,16,128]{3,2,1,0:T(8,128)(2,1)}) custom-call(f32[9,15,8192]{2,1,0:T(8,128)} %refs_0_.1, bf16[4,1,8192]{2,1,0:T(2,128)(2,1)} %copy.72.surf_ref), custom_call_target="tpu_custom_call" | custom-call | bytes 5529600 | tf_op jit(solution)/shard_map/pallas_call | solution.py:147
  21.8 5.2 %all-to-all-start = ((bf16[4,16,144,128]{3,2,1,0:T(8,128)(2,1)}), bf16[4,16,144,128]{3,2,1,0:T(8,128)(2,1)S(1)}, u32[]{:S(2)}, u32[]{:S(2)}) async-start(bf16[4,16,144,128]{3,2,1,0:T(8,128)(2,1)} %bitcast.157), calls=%async_computation | async-start | bytes 4718592 | tf_op jit(solution)/shard_map/all_to_all | solution.py:238
  27.0 16.2 %all-gather = bf16[72,16,384]{2,1,0:T(8,128)(2,1)S(1)} all-gather(bf16[9,16,384]{2,1,0:T(8,128)(2,1)} %get-tuple-element.28), channel_id=2, replica_groups=mesh['grp'=4,'patch'=8] {'patch'}, dimensions={0}, use_global_device_ids=true | all-gather | bytes 995328 | tf_op jit(solution)/shard_map/all_gather | solution.py:171
  51.8 0.8 select_bitcast_fusion.11
  52.9 0.8 slice.255
  53.6 0.8 slice.257
  54.4 0.8 slice.256
  57.2 10.1 %shard_map.114 = (f32[9,15,8192]{2,1,0:T(8,128)}, bf16[9,16,384]{2,1,0:T(8,128)(2,1)}) custom-call(f32[9,15,8192]{2,1,0:T(8,128)} %refs_0_.1, f32[15,8192]{1,0:T(8,128)} %refs_1_.5, f32[15,8192]{1,0:T(8,128)} %refs_2_.5, f32[9,15,384]{2,1,0:T(8,128)} %maximum_convert_fusion.refs_3_), custom_call_target="tpu_custom_call" | custom-call | flops 22118400 | bytes 9830400 | tf_op jit(solution)/shard_map/pallas_call | solution.py:102
  67.3 16.6 %all-gather.1 = bf16[72,16,384]{2,1,0:T(8,128)(2,1)S(1)} all-gather(bf16[9,16,384]{2,1,0:T(8,128)(2,1)} %get-tuple-element.31), channel_id=3, replica_groups=mesh['grp'=4,'patch'=8] {'patch'}, dimensions={0}, use_global_device_ids=true | all-gather | bytes 995328 | tf_op jit(solution)/shard_map/all_gather | solution.py:171
  84.8 3.7 %multiply_convert_fusion.2 = bf16[16,128,256]{2,1,0:T(8,128)(2,1)} fusion(f32[256]{0:T(256)S(1)} %bitcast.178, bf16[4,16,144,128]{3,2,1,0:T(8,128)(2,1)S(1)} %all-to-all-done, f32[256]{0:T(256)S(1)} %bitcast.179, bf16[4,144,256]{2,1,0:T(8,128)(2,1)S(1)} %bitcast.169, bf16[3,256,256]{2,1,0:T(8,128)(2,1)} %param.20), kind=kOutput, calls=%fused_computation.4 | convolution fusion | flops 878706688 | bytes 3835904 | tf_op jit(solution)/shard_map/...h,hj->...j/dot_general | solution.py:193
  88.6 2.6 %multiply_convert_fusion = bf16[16,128,256]{2,1,0:T(8,128)(2,1)S(1)} fusion(f32[256]{0:T(256)S(1)} %bitcast.177, bf16[16,128,256]{2,1,0:T(8,128)(2,1)} %multiply_convert_fusion.2, f32[256]{0:T(256)S(1)} %bitcast.176, bf16[3,256,256]{2,1,0:T(8,128)(2,1)} %param.20), kind=kOutput, calls=%fused_computation.2 | convolution fusion | flops 543162368 | bytes 2361344 | tf_op jit(solution)/shard_map/...h,hj->...j/dot_general | solution.py:193
  91.1 2.2 %convolution_convert_fusion = bf16[576,2048]{1,0:T(8,128)(2,1)} fusion(bf16[576,256]{1,0:T(8,128)(2,1)S(1)} %bitcast.161, bf16[2048,256]{1,0:T(8,128)(2,1)S(1)} %bitcast.165), kind=kOutput, calls=%fused_computation | convolution fusion | flops 605159424 | bytes 3702784 | tf_op jit(solution)/shard_map/dot_general | solution.py:245
  93.4 1.0 convert_reduce_fusion
  94.4 0.8 fusion.14
  95.1 5.3 %all-to-all-start.2 = ((f32[8,4,128]{2,1,0:T(4,128)}), f32[8,4,128]{2,1,0:T(4,128)S(1)}, u32[]{:S(2)}, u32[]{:S(2)}) async-start(f32[8,4,128]{2,1,0:T(4,128)} %fusion.14), calls=%async_computation.2 | async-start | bytes 32768 | tf_op jit(solution)/shard_map/all_to_all | solution.py:255
  100.5 0.8 slice.269
  101.5 4.6 %all-to-all-done.2 = f32[8,4,128]{2,1,0:T(4,128)S(1)} async-done(((f32[8,4,128]{2,1,0:T(4,128)}), f32[8,4,128]{2,1,0:T(4,128)S(1)}, u32[]{:S(2)}, u32[]{:S(2)}) %all-to-all-start.2) | async-done | bytes 16416 | tf_op jit(solution)/shard_map/all_to_all | solution.py:255
  106.1 4.2 %all-to-all-start.1 = ((bf16[4,9,16,2048]{3,2,1,0:T(8,128)(2,1)}), bf16[4,9,16,2048]{3,2,1,0:T(8,128)(2,1)S(1)}, u32[]{:S(2)}, u32[]{:S(2)}) async-start(bf16[4,9,16,2048]{3,2,1,0:T(8,128)(2,1)} %bitcast.76), calls=%async_computation.1 | async-start | bytes 4718592 | tf_op jit(solution)/shard_map/all_to_all | solution.py:258
  111.5 0.7 maximum_convert_fusion.1.refs_3_
  112.2 10.1 %shard_map.115 = (f32[9,15,8192]{2,1,0:T(8,128)}, bf16[9,16,384]{2,1,0:T(8,128)(2,1)}) custom-call(f32[9,15,8192]{2,1,0:T(8,128)} %get-tuple-element.30.refs_0_, f32[15,8192]{1,0:T(8,128)} %refs_1_.5, f32[15,8192]{1,0:T(8,128)} %refs_2_.5, f32[9,15,384]{2,1,0:T(8,128)} %maximum_convert_fusion.1.refs_3_), custom_call_target="tpu_custom_call" | custom-call | flops 22118400 | bytes 9830400 | tf_op jit(solution)/shard_map/pallas_call | solution.py:102
  122.3 16.1 %all-gather.2 = bf16[72,16,384]{2,1,0:T(8,128)(2,1)S(1)} all-gather(bf16[9,16,384]{2,1,0:T(8,128)(2,1)} %get-tuple-element.33), channel_id=4, replica_groups=mesh['grp'=4,'patch'=8] {'patch'}, dimensions={0}, use_global_device_ids=true | all-gather | bytes 995328 | tf_op jit(solution)/shard_map/all_gather | solution.py:171
  140.9 1.4 copy-done
  142.3 10.3 %shard_map.116 = (f32[9,15,8192]{2,1,0:T(8,128)}, bf16[9,16,384]{2,1,0:T(8,128)(2,1)}) custom-call(f32[9,15,8192]{2,1,0:T(8,128)} %get-tuple-element.32.refs_0_, f32[15,8192]{1,0:T(8,128)} %refs_1_.5, f32[15,8192]{1,0:T(8,128)} %refs_2_.5, f32[9,15,384]{2,1,0:T(8,128)} %maximum_convert_fusion.2.refs_3_, bf16[4,9,16,2048]{3,2,1,0:T(8,128)(2,1)} %copy-done), custom_call_target="tpu_custom_call" | custom-call | flops 22118400 | bytes 9830400 | tf_op jit(solution)/shard_map/pallas_call | solution.py:102
  (80 shorter events, 10.1 us)
Async XLA Ops:
  0.6 12.7 %copy-start.2 = (bf16[256,540]{0,1:T(8,128)(2,1)S(1)}, bf16[256,540]{0,1:T(8,128)(2,1)}, u32[]{:S(2)}) copy-start(bf16[256,540]{0,1:T(8,128)(2,1)} %param.21) | copy-start | bytes 829444
  21.8 63.0 %all-to-all-start = ((bf16[4,16,144,128]{3,2,1,0:T(8,128)(2,1)}), bf16[4,16,144,128]{3,2,1,0:T(8,128)(2,1)S(1)}, u32[]{:S(2)}, u32[]{:S(2)}) async-start(bf16[4,16,144,128]{3,2,1,0:T(8,128)(2,1)} %bitcast.157), calls=%async_computation | async-start | bytes 4718592 | tf_op jit(solution)/shard_map/all_to_all | solution.py:238
  67.3 17.5 %copy-start.3 = (f32[4,256]{1,0:T(4,128)S(1)}, f32[4,256]{1,0:T(4,128)}, u32[]{:S(2)}) copy-start(f32[4,256]{1,0:T(4,128)} %param.19) | copy-start | bytes 12292
  67.3 17.6 %copy-start.1 = (bf16[4,9,16,256]{3,2,1,0:T(8,128)(2,1)S(1)}, bf16[4,9,16,256]{3,2,1,0:T(8,128)(2,1)}, u32[]{:S(2)}) copy-start(bf16[4,9,16,256]{3,2,1,0:T(8,128)(2,1)} %copy.70) | copy-start | bytes 884740
  95.1 11.0 %all-to-all-start.2 = ((f32[8,4,128]{2,1,0:T(4,128)}), f32[8,4,128]{2,1,0:T(4,128)S(1)}, u32[]{:S(2)}, u32[]{:S(2)}) async-start(f32[8,4,128]{2,1,0:T(4,128)} %fusion.14), calls=%async_computation.2 | async-start | bytes 32768 | tf_op jit(solution)/shard_map/all_to_all | solution.py:255
  106.1 34.8 %all-to-all-start.1 = ((bf16[4,9,16,2048]{3,2,1,0:T(8,128)(2,1)}), bf16[4,9,16,2048]{3,2,1,0:T(8,128)(2,1)S(1)}, u32[]{:S(2)}, u32[]{:S(2)}) async-start(bf16[4,9,16,2048]{3,2,1,0:T(8,128)(2,1)} %bitcast.76), calls=%async_computation.1 | async-start | bytes 4718592 | tf_op jit(solution)/shard_map/all_to_all | solution.py:258
  140.9 1.4 copy-start

commit v11 on v10

--- a/solution.py
+++ b/solution.py
@@ -215,18 +215,18 @@
     slot = 16
     beside_all = jnp.take(neighbours, patch_here, axis=0)
     owners_all = owner_map.reshape(patches, groups, quarter_rows)
-    owners_here = jnp.take(owners_all, patch_here, axis=0)
-    matches = (owners_here[..., None] == jnp.arange(patches, dtype=jnp.int32)).astype(jnp.int32)
-    slot_rank = jnp.sum((jnp.cumsum(matches, axis=1) - matches) * matches, axis=2)
+    owners_here = jnp.take(jnp.take(owners_all, patch_here, axis=0), group_here, axis=0)
+    matches = (owners_here[:, None] == jnp.arange(patches, dtype=jnp.int32)).astype(jnp.int32)
+    slot_rank = jnp.sum((jnp.cumsum(matches, axis=0) - matches) * matches, axis=1)
     slot_index = owners_here * capacity + slot_rank
-    selector = (
-        slot_index[:, None, :] == jnp.arange(slot_count, dtype=jnp.int32)[None, :, None]
+    selector_here = (
+        slot_index[None, :] == jnp.arange(slot_count, dtype=jnp.int32)[:, None]
     ).astype(jnp.bfloat16)
-    selector_here = jnp.take(selector, group_here, axis=0)
     state_part = w_in[: VARS * LEV].reshape(VARS, groups, level_share, -1).transpose(1, 0, 2, 3)
-    state_part = jnp.pad(state_part, ((0, 0), (0, 0), (0, slot - level_share), (0, 0)))
-    surf_part = w_in[VARS * LEV :].reshape(groups, surf_share, -1)
-    w_local = state_part.at[:, :surf_share, level_share, :].set(surf_part).reshape(groups, VARS * slot, -1)
+    surf_part = w_in[VARS * LEV :].reshape(groups, surf_share, 1, -1)
+    surf_part = jnp.pad(surf_part, ((0, 0), (0, VARS - surf_share), (0, 0), (0, 0)))
+    pad_part = jnp.zeros(state_part.shape[:2] + (slot - level_share - 1, state_part.shape[3]), w_in.dtype)
+    w_local = jnp.concatenate([state_part, surf_part, pad_part], axis=2).reshape(groups, VARS * slot, -1)
     w_split = w_out.reshape(-1, VARS, groups, level_share)
     w_pad = jnp.pad(w_split, ((0, 0), (0, 0), (0, 0), (0, slot - level_share)))
     w_rows = w_pad.transpose(2, 1, 3, 0).reshape(groups * VARS * slot, -1)
@@ -246,6 +246,7 @@
         w_rows, hidden_flat, (((1,), (1,)), ((), ())), preferred_element_type=jnp.float32
     ).astype(jnp.bfloat16)
     tendency = tendency.reshape(groups, VARS, slot, quarter_rows * PY)
+    tendency_here = lax.all_to_all(tendency, "grp", split_axis=0, concat_axis=0, tiled=True)
     heating = HEAT_WEIGHT * jnp.sum(
         tendency[:, 0, 0:level_share].astype(jnp.float32), axis=(0, 1)
     ).reshape(quarter_rows, PY)
@@ -255,7 +256,6 @@
     owner_heating = lax.all_to_all(
         packed, "patch", split_axis=0, concat_axis=0, tiled=True
     ).reshape(slot_count, PY)
-    tendency_here = lax.all_to_all(tendency, "grp", split_axis=0, concat_axis=0, tiled=True)
     advected = state
     for section_index in range(SUBSTEPS):
         halo = exchange_halo(payload, beside_all, patches, level_share)

time: 155 us -> 150 us (0.968)
  other arithmetic: 10.9 us -> 7.63 us
  local copies, waits for them, and re-layouts: 17 us -> 15.1 us
    another operation x4 -> x1, other arithmetic: 3.35 us -> 0.04 us  [on_device(): jnp.cumsum(matches, axis=0) - matches]
    scatter x2 -> x0, local copies, waits for them, and re-layouts: 2.04 us -> none  [on_device(): state_part.at[:, :surf_share, level_share, :].set(surf_part)]
  transfers between devices with their start and end apart: 3 -> 3, of which waited for: 1 -> 1; matrix products, arithmetic and copies ran while one was open for 8% -> 8% of each run, Pallas kernels for 13% -> 14%
where the time goes in v11:
time: 150 us; the launch traced here: 148 us
  blocking collectives  48.9 us (33%)
  Pallas kernels  38.8 us (26%)
  local copies, waits for them, and re-layouts  15.1 us (10%)
  starting transfers between devices  14.7 us (10%)
  matrix products  9.28 us (6%)
  between operations  9.04 us (6%)
  other arithmetic  7.63 us (5%)
  waiting for transfers between devices  4.63 us (3%)
    all_gather x3, blocking collectives, exchange_halo(): got = lax.all_gather(payload, 'patch', axis=0, tiled=False)  48.9 us
    pallas_call x3, Pallas kernels, stencil(): pl.pallas_call(functools.partial(stencil_kernel, with_tend=with_tend), gr...  30.5 us
    pallas_call x1, Pallas kernels, first_edges(): pl.pallas_call(functools.partial(pack_kernel, n_surf=n_surf), grid=(n_var...  8.21 us
    dot_general x2, matrix products, hidden_layers(): jnp.einsum('...h,hj->...j', hidden, w_mid[layer_index], preferred_element...  6.28 us
    all_to_all x1, starting transfers between devices, on_device(): lax.all_to_all(packed, 'patch', split_axis=0, concat_axis=0, tiled=True)  5.32 us
    all_to_all x1, starting transfers between devices, on_device(): lax.all_to_all(by_quarter, 'grp', split_axis=0, concat_axis=0, tiled=True)  5.19 us
    all_to_all x1, waiting for transfers between devices, on_device(): lax.all_to_all(packed, 'patch', split_axis=0, concat_axis=0, tiled=True)  4.62 us
    all_to_all x1, starting transfers between devices, on_device(): lax.all_to_all(tendency, 'grp', split_axis=0, concat_axis=0, tiled=True)  4.23 us
  transfers between devices with their start and end apart: 3, of which 1 were waited for; matrix products, arithmetic and copies ran while one was open for 8% of the time, Pallas kernels for 14%

profile of v11, /device:TPU:0, one launch (start us, length us, event | category | flops | bytes accessed | tf_op | source)
XLA Modules:
  0.0 148.1 jit_solution(17624169137496648557)
XLA Ops:
  0.6 0.8 slice.143
  1.4 1.0 slice.142
  2.9 1.3 reduce.6
  4.4 0.9 fusion.20
  5.6 1.6 %copy.72.surf_ref = bf16[4,1,8192]{2,1,0:T(2,128)(2,1)} copy(bf16[4,1,8192]{2,0,1:T(4,128)(2,1)} %bitcast.168) | data formatting | bytes 131072 | tf_op jit(solution)/shard_map/reshape | solution.py:146
  7.4 0.7 copy.70
  8.3 8.2 %shard_map.113 = (bf16[9,16,384]{2,1,0:T(8,128)(2,1)}, bf16[64,9,16,128]{3,2,1,0:T(8,128)(2,1)}) custom-call(f32[9,15,8192]{2,1,0:T(8,128)} %refs_0_.1, bf16[4,1,8192]{2,1,0:T(2,128)(2,1)} %copy.72.surf_ref), custom_call_target="tpu_custom_call" | custom-call | bytes 5529600 | tf_op jit(solution)/shard_map/pallas_call | solution.py:147
  16.5 5.2 %all-to-all-start = ((bf16[4,16,144,128]{3,2,1,0:T(8,128)(2,1)}), bf16[4,16,144,128]{3,2,1,0:T(8,128)(2,1)S(1)}, u32[]{:S(2)}, u32[]{:S(2)}) async-start(bf16[4,16,144,128]{3,2,1,0:T(8,128)(2,1)} %bitcast.151), calls=%async_computation | async-start | bytes 4718592 | tf_op jit(solution)/shard_map/all_to_all | solution.py:238
  21.7 16.2 %all-gather = bf16[72,16,384]{2,1,0:T(8,128)(2,1)S(1)} all-gather(bf16[9,16,384]{2,1,0:T(8,128)(2,1)} %get-tuple-element.16), channel_id=2, replica_groups=mesh['grp'=4,'patch'=8] {'patch'}, dimensions={0}, use_global_device_ids=true | all-gather | bytes 995328 | tf_op jit(solution)/shard_map/all_gather | solution.py:171
  46.6 0.7 select_bitcast_fusion.11
  47.7 0.8 slice.217
  48.4 0.8 slice.219
  49.2 0.8 slice.218
  51.2 0.7 maximum_convert_fusion.refs_3_
  52.0 10.1 %shard_map.114 = (f32[9,15,8192]{2,1,0:T(8,128)}, bf16[9,16,384]{2,1,0:T(8,128)(2,1)}) custom-call(f32[9,15,8192]{2,1,0:T(8,128)} %refs_0_.1, f32[15,8192]{1,0:T(8,128)} %refs_1_.5, f32[15,8192]{1,0:T(8,128)} %refs_2_.5, f32[9,15,384]{2,1,0:T(8,128)} %maximum_convert_fusion.refs_3_), custom_call_target="tpu_custom_call" | custom-call | flops 22118400 | bytes 9830400 | tf_op jit(solution)/shard_map/pallas_call | solution.py:102
  62.0 16.6 %all-gather.1 = bf16[72,16,384]{2,1,0:T(8,128)(2,1)S(1)} all-gather(bf16[9,16,384]{2,1,0:T(8,128)(2,1)} %get-tuple-element.19), channel_id=3, replica_groups=mesh['grp'=4,'patch'=8] {'patch'}, dimensions={0}, use_global_device_ids=true | all-gather | bytes 995328 | tf_op jit(solution)/shard_map/all_gather | solution.py:171
  78.6 0.7 select_bitcast_fusion.7
  79.6 3.7 %multiply_convert_fusion.2 = bf16[16,128,256]{2,1,0:T(8,128)(2,1)} fusion(f32[256]{0:T(256)S(1)} %bitcast.173, bf16[4,16,144,128]{3,2,1,0:T(8,128)(2,1)S(1)} %all-to-all-done, f32[256]{0:T(256)S(1)} %bitcast.174, bf16[4,144,256]{2,1,0:T(8,128)(2,1)S(1)} %bitcast.164, bf16[3,256,256]{2,1,0:T(8,128)(2,1)} %param.18), kind=kOutput, calls=%fused_computation.4 | convolution fusion | flops 878706688 | bytes 3835904 | tf_op jit(solution)/shard_map/...h,hj->...j/dot_general | solution.py:193
  83.3 2.6 %multiply_convert_fusion = bf16[16,128,256]{2,1,0:T(8,128)(2,1)S(1)} fusion(f32[256]{0:T(256)S(1)} %bitcast.172, bf16[16,128,256]{2,1,0:T(8,128)(2,1)} %multiply_convert_fusion.2, f32[256]{0:T(256)S(1)} %bitcast.171, bf16[3,256,256]{2,1,0:T(8,128)(2,1)} %param.18), kind=kOutput, calls=%fused_computation.2 | convolution fusion | flops 543162368 | bytes 2361344 | tf_op jit(solution)/shard_map/...h,hj->...j/dot_general | solution.py:193
  85.9 2.3 %convolution_convert_fusion = bf16[576,2048]{1,0:T(8,128)(2,1)} fusion(bf16[576,256]{1,0:T(8,128)(2,1)S(1)} %bitcast.155, bf16[2048,256]{1,0:T(8,128)(2,1)S(1)} %bitcast.160), kind=kOutput, calls=%fused_computation | convolution fusion | flops 605159424 | bytes 3702784 | tf_op jit(solution)/shard_map/dot_general | solution.py:245
  88.2 1.0 convert_reduce_fusion
  89.2 0.8 fusion.13
  89.9 5.3 %all-to-all-start.2 = ((f32[8,4,128]{2,1,0:T(4,128)}), f32[8,4,128]{2,1,0:T(4,128)S(1)}, u32[]{:S(2)}, u32[]{:S(2)}) async-start(f32[8,4,128]{2,1,0:T(4,128)} %fusion.13), calls=%async_computation.2 | async-start | bytes 32768 | tf_op jit(solution)/shard_map/all_to_all | solution.py:256
  95.3 0.8 slice.231
  96.3 4.6 %all-to-all-done.2 = f32[8,4,128]{2,1,0:T(4,128)S(1)} async-done(((f32[8,4,128]{2,1,0:T(4,128)}), f32[8,4,128]{2,1,0:T(4,128)S(1)}, u32[]{:S(2)}, u32[]{:S(2)}) %all-to-all-start.2) | async-done | bytes 16416 | tf_op jit(solution)/shard_map/all_to_all | solution.py:256
  100.9 4.2 %all-to-all-start.1 = ((bf16[4,9,16,2048]{3,2,1,0:T(8,128)(2,1)}), bf16[4,9,16,2048]{3,2,1,0:T(8,128)(2,1)S(1)}, u32[]{:S(2)}, u32[]{:S(2)}) async-start(bf16[4,9,16,2048]{3,2,1,0:T(8,128)(2,1)} %bitcast.73), calls=%async_computation.1 | async-start | bytes 4718592 | tf_op jit(solution)/shard_map/all_to_all | solution.py:249
  106.3 0.7 maximum_convert_fusion.1.refs_3_
  107.0 10.1 %shard_map.115 = (f32[9,15,8192]{2,1,0:T(8,128)}, bf16[9,16,384]{2,1,0:T(8,128)(2,1)}) custom-call(f32[9,15,8192]{2,1,0:T(8,128)} %get-tuple-element.18.refs_0_, f32[15,8192]{1,0:T(8,128)} %refs_1_.5, f32[15,8192]{1,0:T(8,128)} %refs_2_.5, f32[9,15,384]{2,1,0:T(8,128)} %maximum_convert_fusion.1.refs_3_), custom_call_target="tpu_custom_call" | custom-call | flops 22118400 | bytes 9830400 | tf_op jit(solution)/shard_map/pallas_call | solution.py:102
  117.1 16.1 %all-gather.2 = bf16[72,16,384]{2,1,0:T(8,128)(2,1)S(1)} all-gather(bf16[9,16,384]{2,1,0:T(8,128)(2,1)} %get-tuple-element.21), channel_id=4, replica_groups=mesh['grp'=4,'patch'=8] {'patch'}, dimensions={0}, use_global_device_ids=true | all-gather | bytes 995328 | tf_op jit(solution)/shard_map/all_gather | solution.py:171
  135.0 0.7 maximum_convert_fusion.2.refs_3_
  135.7 1.4 copy-done
  137.1 10.3 %shard_map.116 = (f32[9,15,8192]{2,1,0:T(8,128)}, bf16[9,16,384]{2,1,0:T(8,128)(2,1)}) custom-call(f32[9,15,8192]{2,1,0:T(8,128)} %get-tuple-element.20.refs_0_, f32[15,8192]{1,0:T(8,128)} %refs_1_.5, f32[15,8192]{1,0:T(8,128)} %refs_2_.5, f32[9,15,384]{2,1,0:T(8,128)} %maximum_convert_fusion.2.refs_3_, bf16[4,9,16,2048]{3,2,1,0:T(8,128)(2,1)} %copy-done), custom_call_target="tpu_custom_call" | custom-call | flops 22118400 | bytes 9830400 | tf_op jit(solution)/shard_map/pallas_call | solution.py:102
  (76 shorter events, 7.3 us)
Async XLA Ops:
  0.6 7.5 %copy-start.2 = (bf16[256,540]{0,1:T(8,128)(2,1)S(1)}, bf16[256,540]{0,1:T(8,128)(2,1)}, u32[]{:S(2)}) copy-start(bf16[256,540]{0,1:T(8,128)(2,1)} %param.19) | copy-start | bytes 829444
  16.5 63.1 %all-to-all-start = ((bf16[4,16,144,128]{3,2,1,0:T(8,128)(2,1)}), bf16[4,16,144,128]{3,2,1,0:T(8,128)(2,1)S(1)}, u32[]{:S(2)}, u32[]{:S(2)}) async-start(bf16[4,16,144,128]{3,2,1,0:T(8,128)(2,1)} %bitcast.151), calls=%async_computation | async-start | bytes 4718592 | tf_op jit(solution)/shard_map/all_to_all | solution.py:238
  62.0 17.5 %copy-start.3 = (f32[4,256]{1,0:T(4,128)S(1)}, f32[4,256]{1,0:T(4,128)}, u32[]{:S(2)}) copy-start(f32[4,256]{1,0:T(4,128)} %param.17) | copy-start | bytes 12292
  62.0 17.6 %copy-start.1 = (bf16[4,9,16,256]{3,2,1,0:T(8,128)(2,1)S(1)}, bf16[4,9,16,256]{3,2,1,0:T(8,128)(2,1)}, u32[]{:S(2)}) copy-start(bf16[4,9,16,256]{3,2,1,0:T(8,128)(2,1)} %copy.70) | copy-start | bytes 884740
  89.9 11.0 %all-to-all-start.2 = ((f32[8,4,128]{2,1,0:T(4,128)}), f32[8,4,128]{2,1,0:T(4,128)S(1)}, u32[]{:S(2)}, u32[]{:S(2)}) async-start(f32[8,4,128]{2,1,0:T(4,128)} %fusion.13), calls=%async_computation.2 | async-start | bytes 32768 | tf_op jit(solution)/shard_map/all_to_all | solution.py:256
  100.9 34.8 %all-to-all-start.1 = ((bf16[4,9,16,2048]{3,2,1,0:T(8,128)(2,1)}), bf16[4,9,16,2048]{3,2,1,0:T(8,128)(2,1)S(1)}, u32[]{:S(2)}, u32[]{:S(2)}) async-start(bf16[4,9,16,2048]{3,2,1,0:T(8,128)(2,1)} %bitcast.73), calls=%async_computation.1 | async-start | bytes 4718592 | tf_op jit(solution)/shard_map/all_to_all | solution.py:249
  135.7 1.4 copy-start

commit v12 on v11

--- a/solution.py
+++ b/solution.py
@@ -164,23 +164,43 @@
     )(tracer, surf_rows)
 
 
-def exchange_halo(payload, beside_all, patches, levels):
-    n_vars, slot, _ = payload.shape
+def exchange_halo(payload, beside_all, patches, levels, n_vars):
+    slot = payload.shape[1]
     rows = PX
     chunk_rows = PY // slot
     got = lax.all_gather(payload, "patch", axis=0, tiled=False)
-    north = jnp.take(got, beside_all[0], axis=0)[:, 0:levels, PY : 2 * PY]
-    south = jnp.take(got, beside_all[1], axis=0)[:, 0:levels, 0:PY]
+    north = jnp.take(got, beside_all[0], axis=0)[0:n_vars, 0:levels, PY : 2 * PY]
+    south = jnp.take(got, beside_all[1], axis=0)[0:n_vars, 0:levels, 0:PY]
 
     def column(patch, which):
-        cols = jnp.take(got, patch, axis=0)[..., 2 * PY : 3 * PY]
+        cols = jnp.take(got, patch, axis=0)[0:n_vars, :, 2 * PY : 3 * PY]
         cols = cols.reshape(n_vars, rows // chunk_rows, 2, chunk_rows, slot)[:, :, which]
         return cols.transpose(0, 3, 1, 2).reshape(n_vars, slot, rows)[:, 0:levels]
 
     west = column(beside_all[2], 1)
     east = column(beside_all[3], 0)
     sides = jnp.stack([west, jnp.roll(east, -1, axis=-1)], axis=-1).reshape(west.shape[:-1] + (2 * rows,))
-    return jnp.concatenate([north, south, sides], axis=-1).astype(jnp.float32)
+    halo = jnp.concatenate([north, south, sides], axis=-1).astype(jnp.float32)
+    return halo, got[:, n_vars:]
+
+
+def split_pieces(values, block_shape):
+    flat = values.reshape(-1)
+    high = flat.astype(jnp.bfloat16)
+    rest = flat - high.astype(jnp.float32)
+    middle = rest.astype(jnp.bfloat16)
+    low = (rest - middle.astype(jnp.float32)).astype(jnp.bfloat16)
+    pieces = jnp.concatenate([high, middle, low])
+    block = block_shape[0] * block_shape[1]
+    count = -(-pieces.size // block)
+    pieces = jnp.pad(pieces, (0, count * block - pieces.size))
+    return pieces.reshape((count,) + block_shape)
+
+
+def join_pieces(blocks, size):
+    flat = blocks.reshape(blocks.shape[0], -1)[:, : 3 * size].astype(jnp.float32)
+    flat = flat.reshape(blocks.shape[0], 3, size)
+    return (flat[:, 0] + flat[:, 1]) + flat[:, 2]
 
 
 def activate(pre_act):
@@ -253,13 +273,16 @@
     packed = jnp.dot(
         selector_here.astype(jnp.float32), heating, precision=lax.Precision.HIGHEST
     ).reshape(patches, capacity, PY)
-    owner_heating = lax.all_to_all(
-        packed, "patch", split_axis=0, concat_axis=0, tiled=True
-    ).reshape(slot_count, PY)
+    heat_blocks = split_pieces(packed, (slot, 3 * PY))
     advected = state
     for section_index in range(SUBSTEPS):
-        halo = exchange_halo(payload, beside_all, patches, level_share)
         last = section_index == SUBSTEPS - 1
+        if last:
+            payload = jnp.concatenate([payload, heat_blocks], axis=0)
+        halo, extra = exchange_halo(payload, beside_all, patches, level_share, VARS)
+        if last:
+            heat_all = join_pieces(extra, packed.size).reshape((patches,) + packed.shape)
+            owner_heating = jnp.take(heat_all, patch_here, axis=1).reshape(slot_count, PY)
         advected, payload = stencil(
             advected, courant_x, courant_y, halo, tendency_here if last else None
         )

time: 150 us -> 161 us (1.073)
  waiting for transfers between devices: 4.63 us -> 21.1 us
  blocking collectives: 48.9 us -> 32.7 us
  between operations: 9.04 us -> 22.1 us
  starting transfers between devices: 14.7 us -> 9.4 us
  other arithmetic: 7.63 us -> 11.2 us
  matrix products: 9.28 us -> 7.65 us
    all_gather x0 -> x1, waiting for transfers between devices: none -> 20.4 us  [exchange_halo(): got = lax.all_gather(payload, 'patch', axis=0, tiled=False)]
    all_gather x3 -> x2, blocking collectives: 48.9 us -> 32.7 us  [exchange_halo(): got = lax.all_gather(payload, 'patch', axis=0, tiled=False)]
    all_to_all x1 -> x0, starting transfers between devices: 5.32 us -> none  [on_device(): lax.all_to_all(packed, 'patch', split_axis=0, concat_axis=0, tiled=True)]
    all_to_all x1 -> x0, waiting for transfers between devices: 4.62 us -> none  [on_device(): lax.all_to_all(packed, 'patch', split_axis=0, concat_axis=0, tiled=True)]
    select_n x3 -> x4, other arithmetic: 1.51 us -> 3.25 us  [the longest x3 2.63 us: exchange_halo(): north = jnp.take(got, beside_all[0], axis=0)[0:n_vars, 0:levels, PY:2 * PY]]
  transfers between devices with their start and end apart: 3 -> 3, of which waited for: 1 -> 2; matrix products, arithmetic and copies ran while one was open for 8% -> 10% of each run, Pallas kernels for 14% -> 13%
where the time goes in v12:
time: 161 us; the launch traced here: 159 us
  Pallas kernels  38.8 us (24%)
  blocking collectives  32.7 us (20%)
  between operations  22.1 us (14%)
  waiting for transfers between devices  21.1 us (13%)
  local copies, waits for them, and re-layouts  16.1 us (10%)
  other arithmetic  11.2 us (7%)
  starting transfers between devices  9.4 us (6%)
  matrix products  7.65 us (5%)
    all_gather x2, blocking collectives, exchange_halo(): got = lax.all_gather(payload, 'patch', axis=0, tiled=False)  32.7 us
    pallas_call x3, Pallas kernels, stencil(): pl.pallas_call(functools.partial(stencil_kernel, with_tend=with_tend), gr...  30.6 us
    all_gather x1, waiting for transfers between devices, exchange_halo(): got = lax.all_gather(payload, 'patch', axis=0, tiled=False)  20.4 us
    pallas_call x1, Pallas kernels, first_edges(): pl.pallas_call(functools.partial(pack_kernel, n_surf=n_surf), grid=(n_var...  8.22 us
    dot_general x2, matrix products, hidden_layers(): jnp.einsum('...h,hj->...j', hidden, w_mid[layer_index], preferred_element...  5.3 us
    all_to_all x1, starting transfers between devices, on_device(): lax.all_to_all(by_quarter, 'grp', split_axis=0, concat_axis=0, tiled=True)  5.19 us
    all_to_all x1, starting transfers between devices, on_device(): lax.all_to_all(tendency, 'grp', split_axis=0, concat_axis=0, tiled=True)  4.21 us
  transfers between devices with their start and end apart: 3, of which 2 were waited for; matrix products, arithmetic and copies ran while one was open for 10% of the time, Pallas kernels for 13%

profile of v12, /device:TPU:0, one launch (start us, length us, event | category | flops | bytes accessed | tf_op | source)
XLA Modules:
  0.0 159.2 jit_solution(11307434912447681595)
XLA Ops:
  7.2 0.8 slice.155
  7.9 1.0 slice.154
  9.5 1.3 reduce.6
  10.9 0.9 fusion.20
  12.1 1.6 %copy.69.surf_ref = bf16[4,1,8192]{2,1,0:T(2,128)(2,1)} copy(bf16[4,1,8192]{2,0,1:T(4,128)(2,1)} %bitcast.174) | data formatting | bytes 131072 | tf_op jit(solution)/shard_map/reshape | solution.py:146
  13.9 0.7 copy.67
  14.8 8.2 %shard_map.113 = (bf16[9,16,384]{2,1,0:T(8,128)(2,1)}, bf16[64,9,16,128]{3,2,1,0:T(8,128)(2,1)}) custom-call(f32[9,15,8192]{2,1,0:T(8,128)} %refs_0_.1, bf16[4,1,8192]{2,1,0:T(2,128)(2,1)} %copy.69.surf_ref), custom_call_target="tpu_custom_call" | custom-call | bytes 5529600 | tf_op jit(solution)/shard_map/pallas_call | solution.py:147
  23.0 5.2 %all-to-all-start = ((bf16[4,16,144,128]{3,2,1,0:T(8,128)(2,1)}), bf16[4,16,144,128]{3,2,1,0:T(8,128)(2,1)S(1)}, u32[]{:S(2)}, u32[]{:S(2)}) async-start(bf16[4,16,144,128]{3,2,1,0:T(8,128)(2,1)} %bitcast.155), calls=%async_computation | async-start | bytes 4718592 | tf_op jit(solution)/shard_map/all_to_all | solution.py:258
  36.5 16.3 %all-gather = bf16[72,16,384]{2,1,0:T(8,128)(2,1)S(1)} all-gather(bf16[9,16,384]{2,1,0:T(8,128)(2,1)} %get-tuple-element.17), channel_id=2, replica_groups=mesh['grp'=4,'patch'=8] {'patch'}, dimensions={0}, use_global_device_ids=true | all-gather | bytes 995328 | tf_op jit(solution)/shard_map/all_gather | solution.py:171
  52.8 0.7 select_bitcast_fusion.11
  53.9 0.8 slice.255
  54.6 0.8 slice.257
  55.4 0.8 slice.256
  57.4 0.7 maximum_convert_fusion.refs_3_
  58.2 10.1 %shard_map.114 = (f32[9,15,8192]{2,1,0:T(8,128)}, bf16[9,16,384]{2,1,0:T(8,128)(2,1)}) custom-call(f32[9,15,8192]{2,1,0:T(8,128)} %refs_0_.1, f32[15,8192]{1,0:T(8,128)} %refs_1_.5, f32[15,8192]{1,0:T(8,128)} %refs_2_.5, f32[9,15,384]{2,1,0:T(8,128)} %maximum_convert_fusion.refs_3_), custom_call_target="tpu_custom_call" | custom-call | flops 22118400 | bytes 9830400 | tf_op jit(solution)/shard_map/pallas_call | solution.py:102
  68.2 16.5 %all-gather.1 = bf16[72,16,384]{2,1,0:T(8,128)(2,1)S(1)} all-gather(bf16[9,16,384]{2,1,0:T(8,128)(2,1)} %get-tuple-element.20), channel_id=3, replica_groups=mesh['grp'=4,'patch'=8] {'patch'}, dimensions={0}, use_global_device_ids=true | all-gather | bytes 995328 | tf_op jit(solution)/shard_map/all_gather | solution.py:171
  84.7 0.7 select_bitcast_fusion.7
  85.8 0.8 slice.264
  87.8 0.7 maximum_convert_fusion.1.refs_3_
  88.5 10.2 %shard_map.115 = (f32[9,15,8192]{2,1,0:T(8,128)}, bf16[9,16,384]{2,1,0:T(8,128)(2,1)}) custom-call(f32[9,15,8192]{2,1,0:T(8,128)} %get-tuple-element.19.refs_0_, f32[15,8192]{1,0:T(8,128)} %refs_1_.5, f32[15,8192]{1,0:T(8,128)} %refs_2_.5, f32[9,15,384]{2,1,0:T(8,128)} %maximum_convert_fusion.1.refs_3_), custom_call_target="tpu_custom_call" | custom-call | flops 22118400 | bytes 9830400 | tf_op jit(solution)/shard_map/pallas_call | solution.py:102
  98.8 2.8 %multiply_convert_fusion.2 = bf16[16,128,256]{2,1,0:T(8,128)(2,1)} fusion(f32[256]{0:T(256)S(1)} %bitcast.178, bf16[4,16,144,128]{3,2,1,0:T(8,128)(2,1)S(1)} %all-to-all-done, f32[256]{0:T(256)S(1)} %bitcast.179, bf16[4,144,256]{2,1,0:T(8,128)(2,1)S(1)} %bitcast.169, bf16[3,256,256]{2,1,0:T(8,128)(2,1)S(1)} %copy-done.5), kind=kOutput, calls=%fused_computation.4 | convolution fusion | flops 878706688 | bytes 3835904 | tf_op jit(solution)/shard_map/...h,hj->...j/dot_general | solution.py:213
  101.6 2.5 %multiply_convert_fusion = bf16[16,128,256]{2,1,0:T(8,128)(2,1)S(1)} fusion(f32[256]{0:T(256)S(1)} %bitcast.177, bf16[16,128,256]{2,1,0:T(8,128)(2,1)} %multiply_convert_fusion.2, f32[256]{0:T(256)S(1)} %bitcast.176, bf16[3,256,256]{2,1,0:T(8,128)(2,1)S(1)} %copy-done.5), kind=kOutput, calls=%fused_computation.2 | convolution fusion | flops 543162368 | bytes 2361344 | tf_op jit(solution)/shard_map/...h,hj->...j/dot_general | solution.py:213
  104.1 2.2 %convolution_convert_fusion = bf16[576,2048]{1,0:T(8,128)(2,1)} fusion(bf16[576,256]{1,0:T(8,128)(2,1)S(1)} %bitcast.158, bf16[2048,256]{1,0:T(8,128)(2,1)S(1)} %bitcast.163), kind=kOutput, calls=%fused_computation | convolution fusion | flops 605159424 | bytes 3702784 | tf_op jit(solution)/shard_map/dot_general | solution.py:265
  106.3 1.0 convert_reduce_fusion
  108.2 4.2 %all-to-all-start.1 = ((bf16[4,9,16,2048]{3,2,1,0:T(8,128)(2,1)}), bf16[4,9,16,2048]{3,2,1,0:T(8,128)(2,1)S(1)}, u32[]{:S(2)}, u32[]{:S(2)}) async-start(bf16[4,9,16,2048]{3,2,1,0:T(8,128)(2,1)} %bitcast.57), calls=%async_computation.1 | async-start | bytes 4718592 | tf_op jit(solution)/shard_map/all_to_all | solution.py:269
  112.4 20.4 %all-gather.5.cloned.1.call-done = bf16[88,16,384]{2,1,0:T(8,128)(2,1)} async-done(((bf16[11,16,384]{2,1,0:T(8,128)(2,1)}), bf16[88,16,384]{2,1,0:T(8,128)(2,1)}) %all-gather.5.cloned.1.call-update) | async-done | bytes 1081360 | tf_op jit(solution)/shard_map/all_gather | solution.py:171
  132.9 1.2 select_bitcast_fusion.3
  134.4 1.0 slice_convert_fusion
  136.5 1.0 copy.86
  139.2 0.7 maximum_convert_fusion.2.refs_3_
  140.6 1.4 copy-done
  142.0 10.3 %shard_map.116 = (f32[9,15,8192]{2,1,0:T(8,128)}, bf16[9,16,384]{2,1,0:T(8,128)(2,1)}) custom-call(f32[9,15,8192]{2,1,0:T(8,128)} %get-tuple-element.21.refs_0_, f32[15,8192]{1,0:T(8,128)} %refs_1_.5, f32[15,8192]{1,0:T(8,128)} %refs_2_.5, f32[9,15,384]{2,1,0:T(8,128)} %maximum_convert_fusion.2.refs_3_, bf16[4,9,16,2048]{3,2,1,0:T(8,128)(2,1)} %copy-done), custom_call_target="tpu_custom_call" | custom-call | flops 22118400 | bytes 9830400 | tf_op jit(solution)/shard_map/pallas_call | solution.py:102
  (86 shorter events, 9.6 us)
Async XLA Ops:
  7.2 7.5 %copy-start.2 = (bf16[256,540]{0,1:T(8,128)(2,1)S(1)}, bf16[256,540]{0,1:T(8,128)(2,1)}, u32[]{:S(2)}) copy-start(bf16[256,540]{0,1:T(8,128)(2,1)} %param.21) | copy-start | bytes 829444
  23.0 75.7 %all-to-all-start = ((bf16[4,16,144,128]{3,2,1,0:T(8,128)(2,1)}), bf16[4,16,144,128]{3,2,1,0:T(8,128)(2,1)S(1)}, u32[]{:S(2)}, u32[]{:S(2)}) async-start(bf16[4,16,144,128]{3,2,1,0:T(8,128)(2,1)} %bitcast.155), calls=%async_computation | async-start | bytes 4718592 | tf_op jit(solution)/shard_map/all_to_all | solution.py:258
  28.2 104.6 %all-gather.5.cloned.1.call-start = ((), (), s32[]{:S(2)}) async-start(), calls=%async_computation.2 | async-start | bytes 1216512 | tf_op jit(solution)/shard_map/all_gather | solution.py:171
  88.5 10.2 %copy-start.4 = (f32[4,256]{1,0:T(4,128)S(1)}, f32[4,256]{1,0:T(4,128)}, u32[]{:S(2)}) copy-start(f32[4,256]{1,0:T(4,128)} %param.19) | copy-start | bytes 12292
  88.5 10.2 %copy-start.1 = (bf16[4,9,16,256]{3,2,1,0:T(8,128)(2,1)S(1)}, bf16[4,9,16,256]{3,2,1,0:T(8,128)(2,1)}, u32[]{:S(2)}) copy-start(bf16[4,9,16,256]{3,2,1,0:T(8,128)(2,1)} %copy.67) | copy-start | bytes 884740
  88.5 10.2 %copy-start.5 = (bf16[3,256,256]{2,1,0:T(8,128)(2,1)S(1)}, bf16[3,256,256]{2,1,0:T(8,128)(2,1)}, u32[]{:S(2)}) copy-start(bf16[3,256,256]{2,1,0:T(8,128)(2,1)} %param.20) | copy-start | bytes 1179652
  104.1 3.4 %copy-start.3 = (bf16[9,16,384]{2,1,0:T(8,128)(2,1)S(1)}, bf16[9,16,384]{2,1,0:T(8,128)(2,1)}, u32[]{:S(2)}) copy-start(bf16[9,16,384]{2,1,0:T(8,128)(2,1)} %get-tuple-element.22) | copy-start | bytes 331780
  108.2 32.4 %all-to-all-start.1 = ((bf16[4,9,16,2048]{3,2,1,0:T(8,128)(2,1)}), bf16[4,9,16,2048]{3,2,1,0:T(8,128)(2,1)S(1)}, u32[]{:S(2)}, u32[]{:S(2)}) async-start(bf16[4,9,16,2048]{3,2,1,0:T(8,128)(2,1)} %bitcast.57), calls=%async_computation.1 | async-start | bytes 4718592 | tf_op jit(solution)/shard_map/all_to_all | solution.py:269
  140.6 1.4 copy-start
Sparse Core Ops, SparseCore 0:
  108.3 24.4 all-gather.4

commit v13 on v11

--- a/solution.py
+++ b/solution.py
@@ -5,6 +5,7 @@
 from jax import lax
 from jax.experimental import pallas as pl
 from jax.experimental.pallas import tpu as pltpu
+
 from jax.sharding import PartitionSpec as P
 
 VARS = 9
@@ -164,7 +165,7 @@
     )(tracer, surf_rows)
 
 
-def exchange_halo(payload, beside_all, patches, levels):
+def exchange_halo(payload, beside_all, levels):
     n_vars, slot, _ = payload.shape
     rows = PX
     chunk_rows = PY // slot
@@ -208,7 +209,6 @@
     patch_here = lax.axis_index("patch")
     level_share = LEV // groups
     surf_share = SURF // groups
-    feat_share = VARS * level_share + surf_share
     quarter_rows = PX // groups
     capacity = max(2, 2 * quarter_rows // patches)
     slot_count = patches * capacity
@@ -258,7 +258,7 @@
     ).reshape(slot_count, PY)
     advected = state
     for section_index in range(SUBSTEPS):
-        halo = exchange_halo(payload, beside_all, patches, level_share)
+        halo = exchange_halo(payload, beside_all, level_share)
         last = section_index == SUBSTEPS - 1
         advected, payload = stencil(
             advected, courant_x, courant_y, halo, tendency_here if last else None
@@ -280,6 +280,7 @@
         P(),
         P(),
     )
+
     return jax.shard_map(
         on_device,
         mesh=mesh,

time: 150 us -> 150 us (level)
  no operation moved by 1% of the time
where the time goes in v13:
time: 150 us; the launch traced here: 148 us
  blocking collectives  48.9 us (33%)
  Pallas kernels  38.8 us (26%)
  local copies, waits for them, and re-layouts  15.1 us (10%)
  starting transfers between devices  14.7 us (10%)
  matrix products  9.29 us (6%)
  between operations  9.04 us (6%)
  other arithmetic  7.63 us (5%)
  waiting for transfers between devices  4.63 us (3%)
    all_gather x3, blocking collectives, exchange_halo(): got = lax.all_gather(payload, 'patch', axis=0, tiled=False)  48.9 us
    pallas_call x3, Pallas kernels, stencil(): pl.pallas_call(functools.partial(stencil_kernel, with_tend=with_tend), gr...  30.5 us
    pallas_call x1, Pallas kernels, first_edges(): pl.pallas_call(functools.partial(pack_kernel, n_surf=n_surf), grid=(n_var...  8.21 us
    dot_general x2, matrix products, hidden_layers(): jnp.einsum('...h,hj->...j', hidden, w_mid[layer_index], preferred_element...  6.28 us
    all_to_all x1, starting transfers between devices, on_device(): lax.all_to_all(packed, 'patch', split_axis=0, concat_axis=0, tiled=True)  5.31 us
    all_to_all x1, starting transfers between devices, on_device(): lax.all_to_all(by_quarter, 'grp', split_axis=0, concat_axis=0, tiled=True)  5.19 us
    all_to_all x1, waiting for transfers between devices, on_device(): lax.all_to_all(packed, 'patch', split_axis=0, concat_axis=0, tiled=True)  4.62 us
    all_to_all x1, starting transfers between devices, on_device(): lax.all_to_all(tendency, 'grp', split_axis=0, concat_axis=0, tiled=True)  4.23 us
  transfers between devices with their start and end apart: 3, of which 1 were waited for; matrix products, arithmetic and copies ran while one was open for 8% of the time, Pallas kernels for 14%

profile of v13, /device:TPU:0, one launch (start us, length us, event | category | flops | bytes accessed | tf_op | source)
XLA Modules:
  0.0 148.1 jit_solution(17624169137496648557)
XLA Ops:
  0.6 0.8 slice.143
  1.4 1.0 slice.142
  2.9 1.3 reduce.6
  4.4 0.9 fusion.20
  5.6 1.6 %copy.72.surf_ref = bf16[4,1,8192]{2,1,0:T(2,128)(2,1)} copy(bf16[4,1,8192]{2,0,1:T(4,128)(2,1)} %bitcast.168) | data formatting | bytes 131072 | tf_op jit(solution)/shard_map/reshape | solution.py:147
  7.4 0.7 copy.70
  8.3 8.2 %shard_map.113 = (bf16[9,16,384]{2,1,0:T(8,128)(2,1)}, bf16[64,9,16,128]{3,2,1,0:T(8,128)(2,1)}) custom-call(f32[9,15,8192]{2,1,0:T(8,128)} %refs_0_.1, bf16[4,1,8192]{2,1,0:T(2,128)(2,1)} %copy.72.surf_ref), custom_call_target="tpu_custom_call" | custom-call | bytes 5529600 | tf_op jit(solution)/shard_map/pallas_call | solution.py:148
  16.5 5.2 %all-to-all-start = ((bf16[4,16,144,128]{3,2,1,0:T(8,128)(2,1)}), bf16[4,16,144,128]{3,2,1,0:T(8,128)(2,1)S(1)}, u32[]{:S(2)}, u32[]{:S(2)}) async-start(bf16[4,16,144,128]{3,2,1,0:T(8,128)(2,1)} %bitcast.151), calls=%async_computation | async-start | bytes 4718592 | tf_op jit(solution)/shard_map/all_to_all | solution.py:238
  21.7 16.2 %all-gather = bf16[72,16,384]{2,1,0:T(8,128)(2,1)S(1)} all-gather(bf16[9,16,384]{2,1,0:T(8,128)(2,1)} %get-tuple-element.16), channel_id=2, replica_groups=mesh['grp'=4,'patch'=8] {'patch'}, dimensions={0}, use_global_device_ids=true | all-gather | bytes 995328 | tf_op jit(solution)/shard_map/all_gather | solution.py:172
  46.6 0.7 select_bitcast_fusion.11
  47.7 0.8 slice.217
  48.4 0.8 slice.219
  49.2 0.8 slice.218
  51.2 0.7 maximum_convert_fusion.refs_3_
  52.0 10.1 %shard_map.114 = (f32[9,15,8192]{2,1,0:T(8,128)}, bf16[9,16,384]{2,1,0:T(8,128)(2,1)}) custom-call(f32[9,15,8192]{2,1,0:T(8,128)} %refs_0_.1, f32[15,8192]{1,0:T(8,128)} %refs_1_.5, f32[15,8192]{1,0:T(8,128)} %refs_2_.5, f32[9,15,384]{2,1,0:T(8,128)} %maximum_convert_fusion.refs_3_), custom_call_target="tpu_custom_call" | custom-call | flops 22118400 | bytes 9830400 | tf_op jit(solution)/shard_map/pallas_call | solution.py:103
  62.0 16.6 %all-gather.1 = bf16[72,16,384]{2,1,0:T(8,128)(2,1)S(1)} all-gather(bf16[9,16,384]{2,1,0:T(8,128)(2,1)} %get-tuple-element.19), channel_id=3, replica_groups=mesh['grp'=4,'patch'=8] {'patch'}, dimensions={0}, use_global_device_ids=true | all-gather | bytes 995328 | tf_op jit(solution)/shard_map/all_gather | solution.py:172
  78.6 0.7 select_bitcast_fusion.7
  79.6 3.7 %multiply_convert_fusion.2 = bf16[16,128,256]{2,1,0:T(8,128)(2,1)} fusion(f32[256]{0:T(256)S(1)} %bitcast.173, bf16[4,16,144,128]{3,2,1,0:T(8,128)(2,1)S(1)} %all-to-all-done, f32[256]{0:T(256)S(1)} %bitcast.174, bf16[4,144,256]{2,1,0:T(8,128)(2,1)S(1)} %bitcast.164, bf16[3,256,256]{2,1,0:T(8,128)(2,1)} %param.18), kind=kOutput, calls=%fused_computation.4 | convolution fusion | flops 878706688 | bytes 3835904 | tf_op jit(solution)/shard_map/...h,hj->...j/dot_general | solution.py:194
  83.4 2.6 %multiply_convert_fusion = bf16[16,128,256]{2,1,0:T(8,128)(2,1)S(1)} fusion(f32[256]{0:T(256)S(1)} %bitcast.172, bf16[16,128,256]{2,1,0:T(8,128)(2,1)} %multiply_convert_fusion.2, f32[256]{0:T(256)S(1)} %bitcast.171, bf16[3,256,256]{2,1,0:T(8,128)(2,1)} %param.18), kind=kOutput, calls=%fused_computation.2 | convolution fusion | flops 543162368 | bytes 2361344 | tf_op jit(solution)/shard_map/...h,hj->...j/dot_general | solution.py:194
  85.9 2.3 %convolution_convert_fusion = bf16[576,2048]{1,0:T(8,128)(2,1)} fusion(bf16[576,256]{1,0:T(8,128)(2,1)S(1)} %bitcast.155, bf16[2048,256]{1,0:T(8,128)(2,1)S(1)} %bitcast.160), kind=kOutput, calls=%fused_computation | convolution fusion | flops 605159424 | bytes 3702784 | tf_op jit(solution)/shard_map/dot_general | solution.py:245
  88.2 1.0 convert_reduce_fusion
  89.2 0.8 fusion.13
  89.9 5.3 %all-to-all-start.2 = ((f32[8,4,128]{2,1,0:T(4,128)}), f32[8,4,128]{2,1,0:T(4,128)S(1)}, u32[]{:S(2)}, u32[]{:S(2)}) async-start(f32[8,4,128]{2,1,0:T(4,128)} %fusion.13), calls=%async_computation.2 | async-start | bytes 32768 | tf_op jit(solution)/shard_map/all_to_all | solution.py:256
  95.3 0.8 slice.231
  96.3 4.6 %all-to-all-done.2 = f32[8,4,128]{2,1,0:T(4,128)S(1)} async-done(((f32[8,4,128]{2,1,0:T(4,128)}), f32[8,4,128]{2,1,0:T(4,128)S(1)}, u32[]{:S(2)}, u32[]{:S(2)}) %all-to-all-start.2) | async-done | bytes 16416 | tf_op jit(solution)/shard_map/all_to_all | solution.py:256
  100.9 4.2 %all-to-all-start.1 = ((bf16[4,9,16,2048]{3,2,1,0:T(8,128)(2,1)}), bf16[4,9,16,2048]{3,2,1,0:T(8,128)(2,1)S(1)}, u32[]{:S(2)}, u32[]{:S(2)}) async-start(bf16[4,9,16,2048]{3,2,1,0:T(8,128)(2,1)} %bitcast.73), calls=%async_computation.1 | async-start | bytes 4718592 | tf_op jit(solution)/shard_map/all_to_all | solution.py:249
  106.3 0.7 maximum_convert_fusion.1.refs_3_
  107.0 10.1 %shard_map.115 = (f32[9,15,8192]{2,1,0:T(8,128)}, bf16[9,16,384]{2,1,0:T(8,128)(2,1)}) custom-call(f32[9,15,8192]{2,1,0:T(8,128)} %get-tuple-element.18.refs_0_, f32[15,8192]{1,0:T(8,128)} %refs_1_.5, f32[15,8192]{1,0:T(8,128)} %refs_2_.5, f32[9,15,384]{2,1,0:T(8,128)} %maximum_convert_fusion.1.refs_3_), custom_call_target="tpu_custom_call" | custom-call | flops 22118400 | bytes 9830400 | tf_op jit(solution)/shard_map/pallas_call | solution.py:103
  117.1 16.1 %all-gather.2 = bf16[72,16,384]{2,1,0:T(8,128)(2,1)S(1)} all-gather(bf16[9,16,384]{2,1,0:T(8,128)(2,1)} %get-tuple-element.21), channel_id=4, replica_groups=mesh['grp'=4,'patch'=8] {'patch'}, dimensions={0}, use_global_device_ids=true | all-gather | bytes 995328 | tf_op jit(solution)/shard_map/all_gather | solution.py:172
  135.0 0.7 maximum_convert_fusion.2.refs_3_
  135.7 1.4 copy-done
  137.1 10.3 %shard_map.116 = (f32[9,15,8192]{2,1,0:T(8,128)}, bf16[9,16,384]{2,1,0:T(8,128)(2,1)}) custom-call(f32[9,15,8192]{2,1,0:T(8,128)} %get-tuple-element.20.refs_0_, f32[15,8192]{1,0:T(8,128)} %refs_1_.5, f32[15,8192]{1,0:T(8,128)} %refs_2_.5, f32[9,15,384]{2,1,0:T(8,128)} %maximum_convert_fusion.2.refs_3_, bf16[4,9,16,2048]{3,2,1,0:T(8,128)(2,1)} %copy-done), custom_call_target="tpu_custom_call" | custom-call | flops 22118400 | bytes 9830400 | tf_op jit(solution)/shard_map/pallas_call | solution.py:103
  (76 shorter events, 7.3 us)
Async XLA Ops:
  0.6 7.5 %copy-start.2 = (bf16[256,540]{0,1:T(8,128)(2,1)S(1)}, bf16[256,540]{0,1:T(8,128)(2,1)}, u32[]{:S(2)}) copy-start(bf16[256,540]{0,1:T(8,128)(2,1)} %param.19) | copy-start | bytes 829444
  16.5 63.1 %all-to-all-start = ((bf16[4,16,144,128]{3,2,1,0:T(8,128)(2,1)}), bf16[4,16,144,128]{3,2,1,0:T(8,128)(2,1)S(1)}, u32[]{:S(2)}, u32[]{:S(2)}) async-start(bf16[4,16,144,128]{3,2,1,0:T(8,128)(2,1)} %bitcast.151), calls=%async_computation | async-start | bytes 4718592 | tf_op jit(solution)/shard_map/all_to_all | solution.py:238
  62.0 17.5 %copy-start.3 = (f32[4,256]{1,0:T(4,128)S(1)}, f32[4,256]{1,0:T(4,128)}, u32[]{:S(2)}) copy-start(f32[4,256]{1,0:T(4,128)} %param.17) | copy-start | bytes 12292
  62.0 17.6 %copy-start.1 = (bf16[4,9,16,256]{3,2,1,0:T(8,128)(2,1)S(1)}, bf16[4,9,16,256]{3,2,1,0:T(8,128)(2,1)}, u32[]{:S(2)}) copy-start(bf16[4,9,16,256]{3,2,1,0:T(8,128)(2,1)} %copy.70) | copy-start | bytes 884740
  89.9 11.0 %all-to-all-start.2 = ((f32[8,4,128]{2,1,0:T(4,128)}), f32[8,4,128]{2,1,0:T(4,128)S(1)}, u32[]{:S(2)}, u32[]{:S(2)}) async-start(f32[8,4,128]{2,1,0:T(4,128)} %fusion.13), calls=%async_computation.2 | async-start | bytes 32768 | tf_op jit(solution)/shard_map/all_to_all | solution.py:256
  100.9 34.8 %all-to-all-start.1 = ((bf16[4,9,16,2048]{3,2,1,0:T(8,128)(2,1)}), bf16[4,9,16,2048]{3,2,1,0:T(8,128)(2,1)S(1)}, u32[]{:S(2)}, u32[]{:S(2)}) async-start(bf16[4,9,16,2048]{3,2,1,0:T(8,128)(2,1)} %bitcast.73), calls=%async_computation.1 | async-start | bytes 4718592 | tf_op jit(solution)/shard_map/all_to_all | solution.py:249
  135.7 1.4 copy-start

commit v14 on v11

--- a/solution.py
+++ b/solution.py
@@ -28,9 +28,9 @@
     rows = st_ref.shape[2] // PY
     slot = stack_ref.shape[0] // rows
     levels = st_ref.shape[1]
-    north = rows_ref[0, :, 0:PY]
-    south = rows_ref[0, :, PY : 2 * PY]
-    sides = rows_ref[0, :, 2 * PY : 3 * PY]
+    north = rows_ref[0, :, 0:PY].astype(jnp.float32)
+    south = rows_ref[0, :, PY : 2 * PY].astype(jnp.float32)
+    sides = rows_ref[0, :, 2 * PY : 3 * PY].astype(jnp.float32)
     lane = lax.broadcasted_iota(jnp.int32, north.shape, 1)
     stack_ref[...] = jnp.zeros(stack_ref.shape, stack_ref.dtype)
     for x in range(rows):
@@ -180,7 +180,7 @@
     west = column(beside_all[2], 1)
     east = column(beside_all[3], 0)
     sides = jnp.stack([west, jnp.roll(east, -1, axis=-1)], axis=-1).reshape(west.shape[:-1] + (2 * rows,))
-    return jnp.concatenate([north, south, sides], axis=-1).astype(jnp.float32)
+    return jnp.concatenate([north, south, sides], axis=-1)
 
 
 def activate(pre_act):

time: 150 us -> 149 us (level)
    convert_element_type x3 -> x0, other arithmetic: 2.14 us -> none  [exchange_halo(): return jnp.concatenate([north, south, sides], axis=-1).astype(jnp.float32)]
    concatenate x0 -> x3, other arithmetic: none -> 2.02 us  [exchange_halo(): return jnp.concatenate([north, south, sides], axis=-1)]
  transfers between devices with their start and end apart: 3 -> 3, of which waited for: 1 -> 1; matrix products, arithmetic and copies ran while one was open for 8% -> 8% of each run, Pallas kernels for 14% -> 13%
where the time goes in v14:
time: 149 us; the launch traced here: 147 us
  blocking collectives  48.9 us (33%)
  Pallas kernels  38.2 us (26%)
  local copies, waits for them, and re-layouts  15.1 us (10%)
  starting transfers between devices  14.7 us (10%)
  matrix products  9.29 us (6%)
  between operations  9.04 us (6%)
  other arithmetic  7.5 us (5%)
  waiting for transfers between devices  4.63 us (3%)
    all_gather x3, blocking collectives, exchange_halo(): got = lax.all_gather(payload, 'patch', axis=0, tiled=False)  48.9 us
    pallas_call x3, Pallas kernels, stencil(): pl.pallas_call(functools.partial(stencil_kernel, with_tend=with_tend), gr...  30 us
    pallas_call x1, Pallas kernels, first_edges(): pl.pallas_call(functools.partial(pack_kernel, n_surf=n_surf), grid=(n_var...  8.21 us
    dot_general x2, matrix products, hidden_layers(): jnp.einsum('...h,hj->...j', hidden, w_mid[layer_index], preferred_element...  6.28 us
    all_to_all x1, starting transfers between devices, on_device(): lax.all_to_all(packed, 'patch', split_axis=0, concat_axis=0, tiled=True)  5.31 us
    all_to_all x1, starting transfers between devices, on_device(): lax.all_to_all(by_quarter, 'grp', split_axis=0, concat_axis=0, tiled=True)  5.19 us
    all_to_all x1, waiting for transfers between devices, on_device(): lax.all_to_all(packed, 'patch', split_axis=0, concat_axis=0, tiled=True)  4.62 us
    all_to_all x1, starting transfers between devices, on_device(): lax.all_to_all(tendency, 'grp', split_axis=0, concat_axis=0, tiled=True)  4.23 us
  transfers between devices with their start and end apart: 3, of which 1 were waited for; matrix products, arithmetic and copies ran while one was open for 8% of the time, Pallas kernels for 13%

profile of v14, /device:TPU:0, one launch (start us, length us, event | category | flops | bytes accessed | tf_op | source)
XLA Modules:
  0.0 147.4 jit_solution(7130074880650475407)
XLA Ops:
  0.6 0.8 slice.143
  1.4 1.0 slice.142
  2.9 1.3 reduce.6
  4.4 0.9 fusion.20
  5.6 1.6 %copy.72.surf_ref = bf16[4,1,8192]{2,1,0:T(2,128)(2,1)} copy(bf16[4,1,8192]{2,0,1:T(4,128)(2,1)} %bitcast.168) | data formatting | bytes 131072 | tf_op jit(solution)/shard_map/reshape | solution.py:146
  7.4 0.7 copy.70
  8.3 8.2 %shard_map.113 = (bf16[9,16,384]{2,1,0:T(8,128)(2,1)}, bf16[64,9,16,128]{3,2,1,0:T(8,128)(2,1)}) custom-call(f32[9,15,8192]{2,1,0:T(8,128)} %refs_0_.1, bf16[4,1,8192]{2,1,0:T(2,128)(2,1)} %copy.72.surf_ref), custom_call_target="tpu_custom_call" | custom-call | bytes 5529600 | tf_op jit(solution)/shard_map/pallas_call | solution.py:147
  16.5 5.2 %all-to-all-start = ((bf16[4,16,144,128]{3,2,1,0:T(8,128)(2,1)}), bf16[4,16,144,128]{3,2,1,0:T(8,128)(2,1)S(1)}, u32[]{:S(2)}, u32[]{:S(2)}) async-start(bf16[4,16,144,128]{3,2,1,0:T(8,128)(2,1)} %bitcast.151), calls=%async_computation | async-start | bytes 4718592 | tf_op jit(solution)/shard_map/all_to_all | solution.py:238
  21.7 16.2 %all-gather = bf16[72,16,384]{2,1,0:T(8,128)(2,1)S(1)} all-gather(bf16[9,16,384]{2,1,0:T(8,128)(2,1)} %get-tuple-element.16), channel_id=2, replica_groups=mesh['grp'=4,'patch'=8] {'patch'}, dimensions={0}, use_global_device_ids=true | all-gather | bytes 995328 | tf_op jit(solution)/shard_map/all_gather | solution.py:171
  46.6 0.7 select_bitcast_fusion.11
  47.7 0.8 slice.217
  48.4 0.8 slice.219
  49.2 0.8 slice.218
  51.2 0.7 pad_maximum_fusion.refs_3_
  51.9 9.8 %shard_map.114 = (f32[9,15,8192]{2,1,0:T(8,128)}, bf16[9,16,384]{2,1,0:T(8,128)(2,1)}) custom-call(f32[9,15,8192]{2,1,0:T(8,128)} %refs_0_.1, f32[15,8192]{1,0:T(8,128)} %refs_1_.5, f32[15,8192]{1,0:T(8,128)} %refs_2_.5, bf16[9,15,384]{2,1,0:T(8,128)(2,1)} %pad_maximum_fusion.refs_3_), custom_call_target="tpu_custom_call" | custom-call | flops 22118400 | bytes 9830400 | tf_op jit(solution)/shard_map/pallas_call | solution.py:102
  61.8 16.6 %all-gather.1 = bf16[72,16,384]{2,1,0:T(8,128)(2,1)S(1)} all-gather(bf16[9,16,384]{2,1,0:T(8,128)(2,1)} %get-tuple-element.19), channel_id=3, replica_groups=mesh['grp'=4,'patch'=8] {'patch'}, dimensions={0}, use_global_device_ids=true | all-gather | bytes 995328 | tf_op jit(solution)/shard_map/all_gather | solution.py:171
  78.3 0.7 select_bitcast_fusion.7
  79.3 3.7 %multiply_convert_fusion.2 = bf16[16,128,256]{2,1,0:T(8,128)(2,1)} fusion(f32[256]{0:T(256)S(1)} %bitcast.173, bf16[4,16,144,128]{3,2,1,0:T(8,128)(2,1)S(1)} %all-to-all-done, f32[256]{0:T(256)S(1)} %bitcast.174, bf16[4,144,256]{2,1,0:T(8,128)(2,1)S(1)} %bitcast.164, bf16[3,256,256]{2,1,0:T(8,128)(2,1)} %param.18), kind=kOutput, calls=%fused_computation.4 | convolution fusion | flops 878706688 | bytes 3835904 | tf_op jit(solution)/shard_map/...h,hj->...j/dot_general | solution.py:193
  83.1 2.6 %multiply_convert_fusion = bf16[16,128,256]{2,1,0:T(8,128)(2,1)S(1)} fusion(f32[256]{0:T(256)S(1)} %bitcast.172, bf16[16,128,256]{2,1,0:T(8,128)(2,1)} %multiply_convert_fusion.2, f32[256]{0:T(256)S(1)} %bitcast.171, bf16[3,256,256]{2,1,0:T(8,128)(2,1)} %param.18), kind=kOutput, calls=%fused_computation.2 | convolution fusion | flops 543162368 | bytes 2361344 | tf_op jit(solution)/shard_map/...h,hj->...j/dot_general | solution.py:193
  85.6 2.3 %convolution_convert_fusion = bf16[576,2048]{1,0:T(8,128)(2,1)} fusion(bf16[576,256]{1,0:T(8,128)(2,1)S(1)} %bitcast.155, bf16[2048,256]{1,0:T(8,128)(2,1)S(1)} %bitcast.160), kind=kOutput, calls=%fused_computation | convolution fusion | flops 605159424 | bytes 3702784 | tf_op jit(solution)/shard_map/dot_general | solution.py:245
  87.9 1.0 convert_reduce_fusion
  88.9 0.8 fusion.13
  89.6 5.3 %all-to-all-start.2 = ((f32[8,4,128]{2,1,0:T(4,128)}), f32[8,4,128]{2,1,0:T(4,128)S(1)}, u32[]{:S(2)}, u32[]{:S(2)}) async-start(f32[8,4,128]{2,1,0:T(4,128)} %fusion.13), calls=%async_computation.2 | async-start | bytes 32768 | tf_op jit(solution)/shard_map/all_to_all | solution.py:256
  95.0 0.8 slice.231
  96.0 4.6 %all-to-all-done.2 = f32[8,4,128]{2,1,0:T(4,128)S(1)} async-done(((f32[8,4,128]{2,1,0:T(4,128)}), f32[8,4,128]{2,1,0:T(4,128)S(1)}, u32[]{:S(2)}, u32[]{:S(2)}) %all-to-all-start.2) | async-done | bytes 16416 | tf_op jit(solution)/shard_map/all_to_all | solution.py:256
  100.6 4.2 %all-to-all-start.1 = ((bf16[4,9,16,2048]{3,2,1,0:T(8,128)(2,1)}), bf16[4,9,16,2048]{3,2,1,0:T(8,128)(2,1)S(1)}, u32[]{:S(2)}, u32[]{:S(2)}) async-start(bf16[4,9,16,2048]{3,2,1,0:T(8,128)(2,1)} %bitcast.73), calls=%async_computation.1 | async-start | bytes 4718592 | tf_op jit(solution)/shard_map/all_to_all | solution.py:249
  106.0 0.7 pad_maximum_fusion.1.refs_3_
  106.7 9.9 %shard_map.115 = (f32[9,15,8192]{2,1,0:T(8,128)}, bf16[9,16,384]{2,1,0:T(8,128)(2,1)}) custom-call(f32[9,15,8192]{2,1,0:T(8,128)} %get-tuple-element.18.refs_0_, f32[15,8192]{1,0:T(8,128)} %refs_1_.5, f32[15,8192]{1,0:T(8,128)} %refs_2_.5, bf16[9,15,384]{2,1,0:T(8,128)(2,1)} %pad_maximum_fusion.1.refs_3_), custom_call_target="tpu_custom_call" | custom-call | flops 22118400 | bytes 9830400 | tf_op jit(solution)/shard_map/pallas_call | solution.py:102
  116.5 16.1 %all-gather.2 = bf16[72,16,384]{2,1,0:T(8,128)(2,1)S(1)} all-gather(bf16[9,16,384]{2,1,0:T(8,128)(2,1)} %get-tuple-element.21), channel_id=4, replica_groups=mesh['grp'=4,'patch'=8] {'patch'}, dimensions={0}, use_global_device_ids=true | all-gather | bytes 995328 | tf_op jit(solution)/shard_map/all_gather | solution.py:171
  134.4 0.7 pad_maximum_fusion.2.refs_3_
  135.1 1.4 copy-done
  136.5 10.3 %shard_map.116 = (f32[9,15,8192]{2,1,0:T(8,128)}, bf16[9,16,384]{2,1,0:T(8,128)(2,1)}) custom-call(f32[9,15,8192]{2,1,0:T(8,128)} %get-tuple-element.20.refs_0_, f32[15,8192]{1,0:T(8,128)} %refs_1_.5, f32[15,8192]{1,0:T(8,128)} %refs_2_.5, bf16[9,15,384]{2,1,0:T(8,128)(2,1)} %pad_maximum_fusion.2.refs_3_, bf16[4,9,16,2048]{3,2,1,0:T(8,128)(2,1)} %copy-done), custom_call_target="tpu_custom_call" | custom-call | flops 22118400 | bytes 9830400 | tf_op jit(solution)/shard_map/pallas_call | solution.py:102
  (76 shorter events, 7.3 us)
Async XLA Ops:
  0.6 7.5 %copy-start.2 = (bf16[256,540]{0,1:T(8,128)(2,1)S(1)}, bf16[256,540]{0,1:T(8,128)(2,1)}, u32[]{:S(2)}) copy-start(bf16[256,540]{0,1:T(8,128)(2,1)} %param.19) | copy-start | bytes 829444
  16.5 62.8 %all-to-all-start = ((bf16[4,16,144,128]{3,2,1,0:T(8,128)(2,1)}), bf16[4,16,144,128]{3,2,1,0:T(8,128)(2,1)S(1)}, u32[]{:S(2)}, u32[]{:S(2)}) async-start(bf16[4,16,144,128]{3,2,1,0:T(8,128)(2,1)} %bitcast.151), calls=%async_computation | async-start | bytes 4718592 | tf_op jit(solution)/shard_map/all_to_all | solution.py:238
  61.8 17.5 %copy-start.3 = (f32[4,256]{1,0:T(4,128)S(1)}, f32[4,256]{1,0:T(4,128)}, u32[]{:S(2)}) copy-start(f32[4,256]{1,0:T(4,128)} %param.17) | copy-start | bytes 12292
  61.8 17.6 %copy-start.1 = (bf16[4,9,16,256]{3,2,1,0:T(8,128)(2,1)S(1)}, bf16[4,9,16,256]{3,2,1,0:T(8,128)(2,1)}, u32[]{:S(2)}) copy-start(bf16[4,9,16,256]{3,2,1,0:T(8,128)(2,1)} %copy.70) | copy-start | bytes 884740
  89.6 11.0 %all-to-all-start.2 = ((f32[8,4,128]{2,1,0:T(4,128)}), f32[8,4,128]{2,1,0:T(4,128)S(1)}, u32[]{:S(2)}, u32[]{:S(2)}) async-start(f32[8,4,128]{2,1,0:T(4,128)} %fusion.13), calls=%async_computation.2 | async-start | bytes 32768 | tf_op jit(solution)/shard_map/all_to_all | solution.py:256
  100.6 34.4 %all-to-all-start.1 = ((bf16[4,9,16,2048]{3,2,1,0:T(8,128)(2,1)}), bf16[4,9,16,2048]{3,2,1,0:T(8,128)(2,1)S(1)}, u32[]{:S(2)}, u32[]{:S(2)}) async-start(bf16[4,9,16,2048]{3,2,1,0:T(8,128)(2,1)} %bitcast.73), calls=%async_computation.1 | async-start | bytes 4718592 | tf_op jit(solution)/shard_map/all_to_all | solution.py:249
  135.0 1.4 copy-start

commit v15 on v14

--- a/solution.py
+++ b/solution.py
@@ -122,15 +122,16 @@
     rows = st_ref.shape[2] // PY
     slot = stack_ref.shape[0] // rows
     levels = st_ref.shape[1]
-    keep_surface = pl.program_id(0) < n_surf
     stack_ref[...] = jnp.zeros(stack_ref.shape, stack_ref.dtype)
     for x in range(rows):
         here = slice(x * PY, (x + 1) * PY)
         packed = st_ref[0, :, here].astype(jnp.bfloat16)
         stack_ref[x * slot : x * slot + levels, :] = packed
         feat_ref[x, 0, 0:levels, :] = packed
-        surf_row = surf_ref[0, :, here]
-        feat_ref[x, 0, levels : levels + 1, :] = jnp.where(keep_surface, surf_row, jnp.zeros_like(surf_row))
+        surf_all = surf_ref[:, here].astype(jnp.float32)
+        pick = lax.broadcasted_iota(jnp.int32, surf_all.shape, 0) == pl.program_id(0)
+        surf_row = jnp.sum(jnp.where(pick, surf_all, 0.0), axis=0, keepdims=True)
+        feat_ref[x, 0, levels : levels + 1, :] = surf_row.astype(feat_ref.dtype)
         if x == 0:
             pay_ref[0, 0:levels, 0:PY] = packed
         if x == rows - 1:
@@ -143,13 +144,12 @@
     n_surf = surface.shape[0]
     rows = width // PY
     slot = 16
-    surf_rows = surface.reshape(n_surf, 1, width)
     return pl.pallas_call(
         functools.partial(pack_kernel, n_surf=n_surf),
         grid=(n_vars,),
         in_specs=[
             pl.BlockSpec((1, levels, width), lambda v: (v, 0, 0)),
-            pl.BlockSpec((1, 1, width), lambda v: (jnp.minimum(v, n_surf - 1), 0, 0)),
+            pl.BlockSpec((n_surf, width), lambda v: (0, 0)),
         ],
         out_specs=[
             pl.BlockSpec((1, slot, 3 * PY), lambda v: (v, 0, 0)),
@@ -161,7 +161,7 @@
         ],
         scratch_shapes=[pltpu.VMEM((rows * slot, PY), jnp.bfloat16)],
         cost_estimate=pl.CostEstimate(flops=0, transcendentals=0, bytes_accessed=5 * tracer.size),
-    )(tracer, surf_rows)
+    )(tracer, surface)
 
 
 def exchange_halo(payload, beside_all, patches, levels):

time: 149 us -> 147 us (0.987)
  local copies, waits for them, and re-layouts: 15.1 us -> 13.5 us
    reshape x1 -> x0, local copies, waits for them, and re-layouts: 1.6 us -> none  [first_edges(): surf_rows = surface.reshape(n_surf, 1, width)]
  transfers between devices with their start and end apart: 3 -> 3, of which waited for: 1 -> 1; matrix products, arithmetic and copies ran while one was open for 8% -> 8% of each run, Pallas kernels for 13% -> 14%
where the time goes in v15:
time: 147 us; the launch traced here: 146 us
  blocking collectives  48.9 us (33%)
  Pallas kernels  38.2 us (26%)
  starting transfers between devices  14.7 us (10%)
  local copies, waits for them, and re-layouts  13.5 us (9%)
  matrix products  9.29 us (6%)
  between operations  9.05 us (6%)
  other arithmetic  7.5 us (5%)
  waiting for transfers between devices  4.63 us (3%)
    all_gather x3, blocking collectives, exchange_halo(): got = lax.all_gather(payload, 'patch', axis=0, tiled=False)  48.9 us
    pallas_call x3, Pallas kernels, stencil(): pl.pallas_call(functools.partial(stencil_kernel, with_tend=with_tend), gr...  30 us
    pallas_call x1, Pallas kernels, first_edges(): pl.pallas_call(functools.partial(pack_kernel, n_surf=n_surf), grid=(n_var...  8.15 us
    dot_general x2, matrix products, hidden_layers(): jnp.einsum('...h,hj->...j', hidden, w_mid[layer_index], preferred_element...  6.28 us
    all_to_all x1, starting transfers between devices, on_device(): lax.all_to_all(packed, 'patch', split_axis=0, concat_axis=0, tiled=True)  5.31 us
    all_to_all x1, starting transfers between devices, on_device(): lax.all_to_all(by_quarter, 'grp', split_axis=0, concat_axis=0, tiled=True)  5.19 us
    all_to_all x1, waiting for transfers between devices, on_device(): lax.all_to_all(packed, 'patch', split_axis=0, concat_axis=0, tiled=True)  4.62 us
    all_to_all x1, starting transfers between devices, on_device(): lax.all_to_all(tendency, 'grp', split_axis=0, concat_axis=0, tiled=True)  4.23 us
  transfers between devices with their start and end apart: 3, of which 1 were waited for; matrix products, arithmetic and copies ran while one was open for 8% of the time, Pallas kernels for 14%

profile of v15, /device:TPU:0, one launch (start us, length us, event | category | flops | bytes accessed | tf_op | source)
XLA Modules:
  0.0 145.8 jit_solution(8683733191022373870)
XLA Ops:
  0.6 0.8 slice.143
  1.4 1.0 slice.142
  2.9 1.3 reduce.6
  4.4 0.9 fusion.20
  5.8 0.7 copy.68
  6.7 8.2 %shard_map.113 = (bf16[9,16,384]{2,1,0:T(8,128)(2,1)}, bf16[64,9,16,128]{3,2,1,0:T(8,128)(2,1)}) custom-call(f32[9,15,8192]{2,1,0:T(8,128)} %refs_0_.1, bf16[4,8192]{1,0:T(4,128)(2,1)} %surf_ref.1), custom_call_target="tpu_custom_call" | custom-call | bytes 5529600 | tf_op jit(solution)/shard_map/pallas_call | solution.py:147
  14.8 5.2 %all-to-all-start = ((bf16[4,16,144,128]{3,2,1,0:T(8,128)(2,1)}), bf16[4,16,144,128]{3,2,1,0:T(8,128)(2,1)S(1)}, u32[]{:S(2)}, u32[]{:S(2)}) async-start(bf16[4,16,144,128]{3,2,1,0:T(8,128)(2,1)} %bitcast.150), calls=%async_computation | async-start | bytes 4718592 | tf_op jit(solution)/shard_map/all_to_all | solution.py:238
  20.0 16.2 %all-gather = bf16[72,16,384]{2,1,0:T(8,128)(2,1)S(1)} all-gather(bf16[9,16,384]{2,1,0:T(8,128)(2,1)} %get-tuple-element.16), channel_id=2, replica_groups=mesh['grp'=4,'patch'=8] {'patch'}, dimensions={0}, use_global_device_ids=true | all-gather | bytes 995328 | tf_op jit(solution)/shard_map/all_gather | solution.py:171
  36.3 0.7 fusion.26
  44.9 0.7 select_bitcast_fusion.11
  46.0 0.8 slice.217
  46.8 0.8 slice.219
  47.6 0.8 slice.218
  49.6 0.7 pad_maximum_fusion.refs_3_
  50.3 9.8 %shard_map.114 = (f32[9,15,8192]{2,1,0:T(8,128)}, bf16[9,16,384]{2,1,0:T(8,128)(2,1)}) custom-call(f32[9,15,8192]{2,1,0:T(8,128)} %refs_0_.1, f32[15,8192]{1,0:T(8,128)} %refs_1_.5, f32[15,8192]{1,0:T(8,128)} %refs_2_.5, bf16[9,15,384]{2,1,0:T(8,128)(2,1)} %pad_maximum_fusion.refs_3_), custom_call_target="tpu_custom_call" | custom-call | flops 22118400 | bytes 9830400 | tf_op jit(solution)/shard_map/pallas_call | solution.py:102
  60.1 16.6 %all-gather.1 = bf16[72,16,384]{2,1,0:T(8,128)(2,1)S(1)} all-gather(bf16[9,16,384]{2,1,0:T(8,128)(2,1)} %get-tuple-element.19), channel_id=3, replica_groups=mesh['grp'=4,'patch'=8] {'patch'}, dimensions={0}, use_global_device_ids=true | all-gather | bytes 995328 | tf_op jit(solution)/shard_map/all_gather | solution.py:171
  76.7 0.7 select_bitcast_fusion.7
  77.7 3.7 %multiply_convert_fusion.2 = bf16[16,128,256]{2,1,0:T(8,128)(2,1)} fusion(f32[256]{0:T(256)S(1)} %bitcast.171, bf16[4,16,144,128]{3,2,1,0:T(8,128)(2,1)S(1)} %all-to-all-done, f32[256]{0:T(256)S(1)} %bitcast.172, bf16[4,144,256]{2,1,0:T(8,128)(2,1)S(1)} %bitcast.163, bf16[3,256,256]{2,1,0:T(8,128)(2,1)} %param.18), kind=kOutput, calls=%fused_computation.4 | convolution fusion | flops 878706688 | bytes 3835904 | tf_op jit(solution)/shard_map/...h,hj->...j/dot_general | solution.py:193
  81.4 2.6 %multiply_convert_fusion = bf16[16,128,256]{2,1,0:T(8,128)(2,1)S(1)} fusion(f32[256]{0:T(256)S(1)} %bitcast.170, bf16[16,128,256]{2,1,0:T(8,128)(2,1)} %multiply_convert_fusion.2, f32[256]{0:T(256)S(1)} %bitcast.169, bf16[3,256,256]{2,1,0:T(8,128)(2,1)} %param.18), kind=kOutput, calls=%fused_computation.2 | convolution fusion | flops 543162368 | bytes 2361344 | tf_op jit(solution)/shard_map/...h,hj->...j/dot_general | solution.py:193
  84.0 2.3 %convolution_convert_fusion = bf16[576,2048]{1,0:T(8,128)(2,1)} fusion(bf16[576,256]{1,0:T(8,128)(2,1)S(1)} %bitcast.154, bf16[2048,256]{1,0:T(8,128)(2,1)S(1)} %bitcast.159), kind=kOutput, calls=%fused_computation | convolution fusion | flops 605159424 | bytes 3702784 | tf_op jit(solution)/shard_map/dot_general | solution.py:245
  86.2 1.0 convert_reduce_fusion
  87.2 0.8 fusion.13
  88.0 5.3 %all-to-all-start.2 = ((f32[8,4,128]{2,1,0:T(4,128)}), f32[8,4,128]{2,1,0:T(4,128)S(1)}, u32[]{:S(2)}, u32[]{:S(2)}) async-start(f32[8,4,128]{2,1,0:T(4,128)} %fusion.13), calls=%async_computation.2 | async-start | bytes 32768 | tf_op jit(solution)/shard_map/all_to_all | solution.py:256
  93.3 0.8 slice.231
  94.3 4.6 %all-to-all-done.2 = f32[8,4,128]{2,1,0:T(4,128)S(1)} async-done(((f32[8,4,128]{2,1,0:T(4,128)}), f32[8,4,128]{2,1,0:T(4,128)S(1)}, u32[]{:S(2)}, u32[]{:S(2)}) %all-to-all-start.2) | async-done | bytes 16416 | tf_op jit(solution)/shard_map/all_to_all | solution.py:256
  99.0 4.2 %all-to-all-start.1 = ((bf16[4,9,16,2048]{3,2,1,0:T(8,128)(2,1)}), bf16[4,9,16,2048]{3,2,1,0:T(8,128)(2,1)S(1)}, u32[]{:S(2)}, u32[]{:S(2)}) async-start(bf16[4,9,16,2048]{3,2,1,0:T(8,128)(2,1)} %bitcast.72), calls=%async_computation.1 | async-start | bytes 4718592 | tf_op jit(solution)/shard_map/all_to_all | solution.py:249
  104.3 0.7 pad_maximum_fusion.1.refs_3_
  105.0 9.9 %shard_map.115 = (f32[9,15,8192]{2,1,0:T(8,128)}, bf16[9,16,384]{2,1,0:T(8,128)(2,1)}) custom-call(f32[9,15,8192]{2,1,0:T(8,128)} %get-tuple-element.18.refs_0_, f32[15,8192]{1,0:T(8,128)} %refs_1_.5, f32[15,8192]{1,0:T(8,128)} %refs_2_.5, bf16[9,15,384]{2,1,0:T(8,128)(2,1)} %pad_maximum_fusion.1.refs_3_), custom_call_target="tpu_custom_call" | custom-call | flops 22118400 | bytes 9830400 | tf_op jit(solution)/shard_map/pallas_call | solution.py:102
  114.9 16.1 %all-gather.2 = bf16[72,16,384]{2,1,0:T(8,128)(2,1)S(1)} all-gather(bf16[9,16,384]{2,1,0:T(8,128)(2,1)} %get-tuple-element.21), channel_id=4, replica_groups=mesh['grp'=4,'patch'=8] {'patch'}, dimensions={0}, use_global_device_ids=true | all-gather | bytes 995328 | tf_op jit(solution)/shard_map/all_gather | solution.py:171
  132.7 0.7 pad_maximum_fusion.2.refs_3_
  133.4 1.4 copy-done
  134.8 10.3 %shard_map.116 = (f32[9,15,8192]{2,1,0:T(8,128)}, bf16[9,16,384]{2,1,0:T(8,128)(2,1)}) custom-call(f32[9,15,8192]{2,1,0:T(8,128)} %get-tuple-element.20.refs_0_, f32[15,8192]{1,0:T(8,128)} %refs_1_.5, f32[15,8192]{1,0:T(8,128)} %refs_2_.5, bf16[9,15,384]{2,1,0:T(8,128)(2,1)} %pad_maximum_fusion.2.refs_3_, bf16[4,9,16,2048]{3,2,1,0:T(8,128)(2,1)} %copy-done), custom_call_target="tpu_custom_call" | custom-call | flops 22118400 | bytes 9830400 | tf_op jit(solution)/shard_map/pallas_call | solution.py:102
  (75 shorter events, 6.6 us)
Async XLA Ops:
  0.6 5.9 %copy-start.2 = (bf16[256,540]{0,1:T(8,128)(2,1)S(1)}, bf16[256,540]{0,1:T(8,128)(2,1)}, u32[]{:S(2)}) copy-start(bf16[256,540]{0,1:T(8,128)(2,1)} %param.19) | copy-start | bytes 829444
  14.8 62.8 %all-to-all-start = ((bf16[4,16,144,128]{3,2,1,0:T(8,128)(2,1)}), bf16[4,16,144,128]{3,2,1,0:T(8,128)(2,1)S(1)}, u32[]{:S(2)}, u32[]{:S(2)}) async-start(bf16[4,16,144,128]{3,2,1,0:T(8,128)(2,1)} %bitcast.150), calls=%async_computation | async-start | bytes 4718592 | tf_op jit(solution)/shard_map/all_to_all | solution.py:238
  60.1 17.5 %copy-start.3 = (f32[4,256]{1,0:T(4,128)S(1)}, f32[4,256]{1,0:T(4,128)}, u32[]{:S(2)}) copy-start(f32[4,256]{1,0:T(4,128)} %param.17) | copy-start | bytes 12292
  60.1 17.6 %copy-start.1 = (bf16[4,9,16,256]{3,2,1,0:T(8,128)(2,1)S(1)}, bf16[4,9,16,256]{3,2,1,0:T(8,128)(2,1)}, u32[]{:S(2)}) copy-start(bf16[4,9,16,256]{3,2,1,0:T(8,128)(2,1)} %copy.68) | copy-start | bytes 884740
  88.0 11.0 %all-to-all-start.2 = ((f32[8,4,128]{2,1,0:T(4,128)}), f32[8,4,128]{2,1,0:T(4,128)S(1)}, u32[]{:S(2)}, u32[]{:S(2)}) async-start(f32[8,4,128]{2,1,0:T(4,128)} %fusion.13), calls=%async_computation.2 | async-start | bytes 32768 | tf_op jit(solution)/shard_map/all_to_all | solution.py:256
  99.0 34.4 %all-to-all-start.1 = ((bf16[4,9,16,2048]{3,2,1,0:T(8,128)(2,1)}), bf16[4,9,16,2048]{3,2,1,0:T(8,128)(2,1)S(1)}, u32[]{:S(2)}, u32[]{:S(2)}) async-start(bf16[4,9,16,2048]{3,2,1,0:T(8,128)(2,1)} %bitcast.72), calls=%async_computation.1 | async-start | bytes 4718592 | tf_op jit(solution)/shard_map/all_to_all | solution.py:249
  133.4 1.4 copy-start

commit v16 on v15

--- a/solution.py
+++ b/solution.py
@@ -1,6 +1,7 @@
 import functools
 
 import jax
+import numpy as np
 import jax.numpy as jnp
 from jax import lax
 from jax.experimental import pallas as pl
@@ -222,11 +223,14 @@
     selector_here = (
         slot_index[None, :] == jnp.arange(slot_count, dtype=jnp.int32)[:, None]
     ).astype(jnp.bfloat16)
-    state_part = w_in[: VARS * LEV].reshape(VARS, groups, level_share, -1).transpose(1, 0, 2, 3)
-    surf_part = w_in[VARS * LEV :].reshape(groups, surf_share, 1, -1)
-    surf_part = jnp.pad(surf_part, ((0, 0), (0, VARS - surf_share), (0, 0), (0, 0)))
-    pad_part = jnp.zeros(state_part.shape[:2] + (slot - level_share - 1, state_part.shape[3]), w_in.dtype)
-    w_local = jnp.concatenate([state_part, surf_part, pad_part], axis=2).reshape(groups, VARS * slot, -1)
+    order = np.full((groups, VARS, slot), w_in.shape[0], np.int32)
+    for q in range(groups):
+        for v in range(VARS):
+            order[q, v, :level_share] = v * LEV + q * level_share + np.arange(level_share)
+            if v < surf_share:
+                order[q, v, level_share] = VARS * LEV + q * surf_share + v
+    w_padded = jnp.concatenate([w_in, jnp.zeros((1, w_in.shape[1]), w_in.dtype)], axis=0)
+    w_local = jnp.take(w_padded, jnp.asarray(order.reshape(-1)), axis=0).reshape(groups, VARS * slot, -1)
     w_split = w_out.reshape(-1, VARS, groups, level_share)
     w_pad = jnp.pad(w_split, ((0, 0), (0, 0), (0, 0), (0, slot - level_share)))
     w_rows = w_pad.transpose(2, 1, 3, 0).reshape(groups * VARS * slot, -1)

time: 147 us -> 151 us (1.027)
  local copies, waits for them, and re-layouts: 13.5 us -> 16 us
    gather x0 -> x1, local copies, waits for them, and re-layouts: none -> 3.23 us  [on_device(): jnp.take(w_padded, jnp.asarray(order.reshape(-1)), axis=0)]
    slice x2 -> x0, local copies, waits for them, and re-layouts: 1.73 us -> none  [the longest x1 0.97 us: on_device(): w_in[:VARS * LEV].reshape(VARS, groups, level_share, -1)]
  transfers between devices with their start and end apart: 3 -> 3, of which waited for: 1 -> 1; matrix products, arithmetic and copies ran while one was open for 8% -> 8% of each run, Pallas kernels for 14% -> 13%
where the time goes in v16:
time: 151 us; the launch traced here: 149 us
  blocking collectives  48.9 us (32%)
  Pallas kernels  38.1 us (25%)
  local copies, waits for them, and re-layouts  16 us (11%)
  starting transfers between devices  14.7 us (10%)
  matrix products  9.29 us (6%)
  between operations  8.87 us (6%)
  other arithmetic  8.15 us (5%)
  waiting for transfers between devices  4.63 us (3%)
    all_gather x3, blocking collectives, exchange_halo(): got = lax.all_gather(payload, 'patch', axis=0, tiled=False)  48.9 us
    pallas_call x3, Pallas kernels, stencil(): pl.pallas_call(functools.partial(stencil_kernel, with_tend=with_tend), gr...  30 us
    pallas_call x1, Pallas kernels, first_edges(): pl.pallas_call(functools.partial(pack_kernel, n_surf=n_surf), grid=(n_var...  8.12 us
    dot_general x2, matrix products, hidden_layers(): jnp.einsum('...h,hj->...j', hidden, w_mid[layer_index], preferred_element...  6.28 us
    all_to_all x1, starting transfers between devices, on_device(): lax.all_to_all(packed, 'patch', split_axis=0, concat_axis=0, tiled=True)  5.32 us
    all_to_all x1, starting transfers between devices, on_device(): lax.all_to_all(by_quarter, 'grp', split_axis=0, concat_axis=0, tiled=True)  5.19 us
    all_to_all x1, waiting for transfers between devices, on_device(): lax.all_to_all(packed, 'patch', split_axis=0, concat_axis=0, tiled=True)  4.62 us
    all_to_all x1, starting transfers between devices, on_device(): lax.all_to_all(tendency, 'grp', split_axis=0, concat_axis=0, tiled=True)  4.23 us
  transfers between devices with their start and end apart: 3, of which 1 were waited for; matrix products, arithmetic and copies ran while one was open for 8% of the time, Pallas kernels for 13%

profile of v16, /device:TPU:0, one launch (start us, length us, event | category | flops | bytes accessed | tf_op | source)
XLA Modules:
  0.0 148.8 jit_solution(11003606867958939264)
XLA Ops:
  0.6 0.7 pad_clamp_fusion
  1.8 1.3 reduce.6
  3.3 0.9 fusion.17
  4.5 1.1 reshape.110
  5.6 1.0 concatenate.22
  6.6 3.2 %gather_fusion = bf16[576,256]{1,0:T(8,128)(2,1)} fusion(bf16[557,256]{1,0:T(8,128)(2,1)S(1)} %concatenate.22, s32[1024]{0:T(1024)S(1)} %pad_clamp_fusion), kind=kCustom, calls=%fused_computation | custom fusion | bytes 592128 | tf_op jit(solution)/shard_map/jit(_take)/gather | solution.py:233
  9.8 8.1 %shard_map.122 = (bf16[9,16,384]{2,1,0:T(8,128)(2,1)}, bf16[64,9,16,128]{3,2,1,0:T(8,128)(2,1)}) custom-call(f32[9,15,8192]{2,1,0:T(8,128)} %refs_0_.1, bf16[4,8192]{1,0:T(4,128)(2,1)} %surf_ref.1), custom_call_target="tpu_custom_call" | custom-call | bytes 5529600 | tf_op jit(solution)/shard_map/pallas_call | solution.py:148
  18.0 5.2 %all-to-all-start = ((bf16[4,16,144,128]{3,2,1,0:T(8,128)(2,1)}), bf16[4,16,144,128]{3,2,1,0:T(8,128)(2,1)S(1)}, u32[]{:S(2)}, u32[]{:S(2)}) async-start(bf16[4,16,144,128]{3,2,1,0:T(8,128)(2,1)} %bitcast.149), calls=%async_computation | async-start | bytes 4718592 | tf_op jit(solution)/shard_map/all_to_all | solution.py:242
  23.2 16.2 %all-gather = bf16[72,16,384]{2,1,0:T(8,128)(2,1)S(1)} all-gather(bf16[9,16,384]{2,1,0:T(8,128)(2,1)} %get-tuple-element.16), channel_id=2, replica_groups=mesh['grp'=4,'patch'=8] {'patch'}, dimensions={0}, use_global_device_ids=true | all-gather | bytes 995328 | tf_op jit(solution)/shard_map/all_gather | solution.py:172
  47.9 0.7 select_bitcast_fusion.11
  49.0 0.8 slice.211
  49.8 0.8 slice.213
  50.6 0.8 slice.212
  52.6 0.7 pad_maximum_fusion.refs_3_
  53.3 9.8 %shard_map.123 = (f32[9,15,8192]{2,1,0:T(8,128)}, bf16[9,16,384]{2,1,0:T(8,128)(2,1)}) custom-call(f32[9,15,8192]{2,1,0:T(8,128)} %refs_0_.1, f32[15,8192]{1,0:T(8,128)} %refs_1_.5, f32[15,8192]{1,0:T(8,128)} %refs_2_.5, bf16[9,15,384]{2,1,0:T(8,128)(2,1)} %pad_maximum_fusion.refs_3_), custom_call_target="tpu_custom_call" | custom-call | flops 22118400 | bytes 9830400 | tf_op jit(solution)/shard_map/pallas_call | solution.py:103
  63.1 16.6 %all-gather.1 = bf16[72,16,384]{2,1,0:T(8,128)(2,1)S(1)} all-gather(bf16[9,16,384]{2,1,0:T(8,128)(2,1)} %get-tuple-element.19), channel_id=3, replica_groups=mesh['grp'=4,'patch'=8] {'patch'}, dimensions={0}, use_global_device_ids=true | all-gather | bytes 995328 | tf_op jit(solution)/shard_map/all_gather | solution.py:172
  79.7 0.7 select_bitcast_fusion.7
  80.7 3.7 %multiply_convert_fusion.2 = bf16[16,128,256]{2,1,0:T(8,128)(2,1)} fusion(f32[256]{0:T(256)S(1)} %bitcast.169, bf16[4,16,144,128]{3,2,1,0:T(8,128)(2,1)S(1)} %all-to-all-done, f32[256]{0:T(256)S(1)} %bitcast.170, bf16[4,144,256]{2,1,0:T(8,128)(2,1)S(1)} %bitcast.161, bf16[3,256,256]{2,1,0:T(8,128)(2,1)} %param.19), kind=kOutput, calls=%fused_computation.5 | convolution fusion | flops 878706688 | bytes 3835904 | tf_op jit(solution)/shard_map/...h,hj->...j/dot_general | solution.py:194
  84.4 2.6 %multiply_convert_fusion = bf16[16,128,256]{2,1,0:T(8,128)(2,1)S(1)} fusion(f32[256]{0:T(256)S(1)} %bitcast.168, bf16[16,128,256]{2,1,0:T(8,128)(2,1)} %multiply_convert_fusion.2, f32[256]{0:T(256)S(1)} %bitcast.167, bf16[3,256,256]{2,1,0:T(8,128)(2,1)} %param.19), kind=kOutput, calls=%fused_computation.3 | convolution fusion | flops 543162368 | bytes 2361344 | tf_op jit(solution)/shard_map/...h,hj->...j/dot_general | solution.py:194
  87.0 2.3 %convolution_convert_fusion = bf16[576,2048]{1,0:T(8,128)(2,1)} fusion(bf16[576,256]{1,0:T(8,128)(2,1)S(1)} %bitcast.153, bf16[2048,256]{1,0:T(8,128)(2,1)S(1)} %bitcast.157), kind=kOutput, calls=%fused_computation.1 | convolution fusion | flops 605159424 | bytes 3702784 | tf_op jit(solution)/shard_map/dot_general | solution.py:249
  89.2 1.0 convert_reduce_fusion
  90.3 0.8 fusion.11
  91.0 5.3 %all-to-all-start.2 = ((f32[8,4,128]{2,1,0:T(4,128)}), f32[8,4,128]{2,1,0:T(4,128)S(1)}, u32[]{:S(2)}, u32[]{:S(2)}) async-start(f32[8,4,128]{2,1,0:T(4,128)} %fusion.11), calls=%async_computation.2 | async-start | bytes 32768 | tf_op jit(solution)/shard_map/all_to_all | solution.py:260
  96.4 0.8 slice.225
  97.4 4.6 %all-to-all-done.2 = f32[8,4,128]{2,1,0:T(4,128)S(1)} async-done(((f32[8,4,128]{2,1,0:T(4,128)}), f32[8,4,128]{2,1,0:T(4,128)S(1)}, u32[]{:S(2)}, u32[]{:S(2)}) %all-to-all-start.2) | async-done | bytes 16416 | tf_op jit(solution)/shard_map/all_to_all | solution.py:260
  102.0 4.2 %all-to-all-start.1 = ((bf16[4,9,16,2048]{3,2,1,0:T(8,128)(2,1)}), bf16[4,9,16,2048]{3,2,1,0:T(8,128)(2,1)S(1)}, u32[]{:S(2)}, u32[]{:S(2)}) async-start(bf16[4,9,16,2048]{3,2,1,0:T(8,128)(2,1)} %bitcast.71), calls=%async_computation.1 | async-start | bytes 4718592 | tf_op jit(solution)/shard_map/all_to_all | solution.py:253
  107.3 0.7 pad_maximum_fusion.1.refs_3_
  108.0 9.8 %shard_map.124 = (f32[9,15,8192]{2,1,0:T(8,128)}, bf16[9,16,384]{2,1,0:T(8,128)(2,1)}) custom-call(f32[9,15,8192]{2,1,0:T(8,128)} %get-tuple-element.18.refs_0_, f32[15,8192]{1,0:T(8,128)} %refs_1_.5, f32[15,8192]{1,0:T(8,128)} %refs_2_.5, bf16[9,15,384]{2,1,0:T(8,128)(2,1)} %pad_maximum_fusion.1.refs_3_), custom_call_target="tpu_custom_call" | custom-call | flops 22118400 | bytes 9830400 | tf_op jit(solution)/shard_map/pallas_call | solution.py:103
  117.9 16.1 %all-gather.2 = bf16[72,16,384]{2,1,0:T(8,128)(2,1)S(1)} all-gather(bf16[9,16,384]{2,1,0:T(8,128)(2,1)} %get-tuple-element.21), channel_id=4, replica_groups=mesh['grp'=4,'patch'=8] {'patch'}, dimensions={0}, use_global_device_ids=true | all-gather | bytes 995328 | tf_op jit(solution)/shard_map/all_gather | solution.py:172
  135.7 0.7 pad_maximum_fusion.2.refs_3_
  136.4 1.4 copy-done
  137.8 10.3 %shard_map.125 = (f32[9,15,8192]{2,1,0:T(8,128)}, bf16[9,16,384]{2,1,0:T(8,128)(2,1)}) custom-call(f32[9,15,8192]{2,1,0:T(8,128)} %get-tuple-element.20.refs_0_, f32[15,8192]{1,0:T(8,128)} %refs_1_.5, f32[15,8192]{1,0:T(8,128)} %refs_2_.5, bf16[9,15,384]{2,1,0:T(8,128)(2,1)} %pad_maximum_fusion.2.refs_3_, bf16[4,9,16,2048]{3,2,1,0:T(8,128)(2,1)} %copy-done), custom_call_target="tpu_custom_call" | custom-call | flops 22118400 | bytes 9830400 | tf_op jit(solution)/shard_map/pallas_call | solution.py:103
  (69 shorter events, 7.0 us)
Async XLA Ops:
  18.0 62.7 %all-to-all-start = ((bf16[4,16,144,128]{3,2,1,0:T(8,128)(2,1)}), bf16[4,16,144,128]{3,2,1,0:T(8,128)(2,1)S(1)}, u32[]{:S(2)}, u32[]{:S(2)}) async-start(bf16[4,16,144,128]{3,2,1,0:T(8,128)(2,1)} %bitcast.149), calls=%async_computation | async-start | bytes 4718592 | tf_op jit(solution)/shard_map/all_to_all | solution.py:242
  63.1 17.5 %copy-start.2 = (f32[4,256]{1,0:T(4,128)S(1)}, f32[4,256]{1,0:T(4,128)}, u32[]{:S(2)}) copy-start(f32[4,256]{1,0:T(4,128)} %param.18) | copy-start | bytes 12292
  63.1 17.6 %copy-start.1 = (bf16[576,256]{1,0:T(8,128)(2,1)S(1)}, bf16[576,256]{1,0:T(8,128)(2,1)}, u32[]{:S(2)}) copy-start(bf16[576,256]{1,0:T(8,128)(2,1)} %gather_fusion) | copy-start | bytes 884740
  91.0 11.0 %all-to-all-start.2 = ((f32[8,4,128]{2,1,0:T(4,128)}), f32[8,4,128]{2,1,0:T(4,128)S(1)}, u32[]{:S(2)}, u32[]{:S(2)}) async-start(f32[8,4,128]{2,1,0:T(4,128)} %fusion.11), calls=%async_computation.2 | async-start | bytes 32768 | tf_op jit(solution)/shard_map/all_to_all | solution.py:260
  102.0 34.4 %all-to-all-start.1 = ((bf16[4,9,16,2048]{3,2,1,0:T(8,128)(2,1)}), bf16[4,9,16,2048]{3,2,1,0:T(8,128)(2,1)S(1)}, u32[]{:S(2)}, u32[]{:S(2)}) async-start(bf16[4,9,16,2048]{3,2,1,0:T(8,128)(2,1)} %bitcast.71), calls=%async_computation.1 | async-start | bytes 4718592 | tf_op jit(solution)/shard_map/all_to_all | solution.py:253
  136.4 1.4 copy-start

commit v17 on v15

--- a/solution.py
+++ b/solution.py
@@ -22,15 +22,15 @@
 
 def stencil_kernel(*refs, with_tend):
     if with_tend:
-        st_ref, cx_ref, cy_ref, rows_ref, tend_ref, out_ref, pay_ref, stack_ref = refs
+        st_ref, cx_ref, cy_ref, rows_ref, sides_ref, tend_ref, out_ref, pay_ref, stack_ref = refs
     else:
-        st_ref, cx_ref, cy_ref, rows_ref, out_ref, pay_ref, stack_ref = refs
+        st_ref, cx_ref, cy_ref, rows_ref, sides_ref, out_ref, pay_ref, stack_ref = refs
     rows = st_ref.shape[2] // PY
     slot = stack_ref.shape[0] // rows
     levels = st_ref.shape[1]
     north = rows_ref[0, :, 0:PY].astype(jnp.float32)
     south = rows_ref[0, :, PY : 2 * PY].astype(jnp.float32)
-    sides = rows_ref[0, :, 2 * PY : 3 * PY].astype(jnp.float32)
+    sides = sides_ref[0].astype(jnp.float32)
     lane = lax.broadcasted_iota(jnp.int32, north.shape, 1)
     stack_ref[...] = jnp.zeros(stack_ref.shape, stack_ref.dtype)
     for x in range(rows):
@@ -93,9 +93,10 @@
         pl.BlockSpec((1, levels, width), lambda v: (v, 0, 0)),
         pl.BlockSpec((levels, width), lambda v: (0, 0)),
         pl.BlockSpec((levels, width), lambda v: (0, 0)),
-        pl.BlockSpec((1, levels, 3 * PY), lambda v: (v, 0, 0)),
+        pl.BlockSpec((1, levels, 2 * PY), lambda v: (v, 0, 0)),
+        pl.BlockSpec((1, levels, PY), lambda v: (v, 0, 0)),
     ]
-    args = [tracer, along_x, along_y, halo]
+    args = [tracer, along_x, along_y, halo[0], halo[1]]
     if with_tend:
         in_specs.append(pl.BlockSpec((tend.shape[0], 1) + tend.shape[2:], lambda v: (0, v, 0, 0)))
         args.append(tend)
@@ -180,7 +181,7 @@
     west = column(beside_all[2], 1)
     east = column(beside_all[3], 0)
     sides = jnp.stack([west, jnp.roll(east, -1, axis=-1)], axis=-1).reshape(west.shape[:-1] + (2 * rows,))
-    return jnp.concatenate([north, south, sides], axis=-1)
+    return (jnp.concatenate([north, south], axis=-1), sides)
 
 
 def activate(pre_act):

time: 147 us -> 149 us (1.014)
  local copies, waits for them, and re-layouts: 13.5 us -> 15.3 us
    reshape x3, local copies, waits for them, and re-layouts: 0.52 us -> 2.33 us  [exchange_halo(): jnp.stack([west, jnp.roll(east, -1, axis=-1)], axis=-1)]
  transfers between devices with their start and end apart: 3 -> 3, of which waited for: 1 -> 1; matrix products, arithmetic and copies ran while one was open for 8% -> 9% of each run, Pallas kernels for 14% -> 13%
where the time goes in v17:
time: 149 us; the launch traced here: 148 us
  blocking collectives  48.9 us (33%)
  Pallas kernels  38.4 us (26%)
  local copies, waits for them, and re-layouts  15.3 us (10%)
  starting transfers between devices  14.7 us (10%)
  matrix products  9.29 us (6%)
  between operations  9.04 us (6%)
  other arithmetic  7.41 us (5%)
  waiting for transfers between devices  4.63 us (3%)
    all_gather x3, blocking collectives, exchange_halo(): got = lax.all_gather(payload, 'patch', axis=0, tiled=False)  48.9 us
    pallas_call x3, Pallas kernels, stencil(): pl.pallas_call(functools.partial(stencil_kernel, with_tend=with_tend), gr...  30.2 us
    pallas_call x1, Pallas kernels, first_edges(): pl.pallas_call(functools.partial(pack_kernel, n_surf=n_surf), grid=(n_var...  8.15 us
    dot_general x2, matrix products, hidden_layers(): jnp.einsum('...h,hj->...j', hidden, w_mid[layer_index], preferred_element...  6.28 us
    all_to_all x1, starting transfers between devices, on_device(): lax.all_to_all(packed, 'patch', split_axis=0, concat_axis=0, tiled=True)  5.32 us
    all_to_all x1, starting transfers between devices, on_device(): lax.all_to_all(by_quarter, 'grp', split_axis=0, concat_axis=0, tiled=True)  5.19 us
    all_to_all x1, waiting for transfers between devices, on_device(): lax.all_to_all(packed, 'patch', split_axis=0, concat_axis=0, tiled=True)  4.62 us
    all_to_all x1, starting transfers between devices, on_device(): lax.all_to_all(tendency, 'grp', split_axis=0, concat_axis=0, tiled=True)  4.23 us
  transfers between devices with their start and end apart: 3, of which 1 were waited for; matrix products, arithmetic and copies ran while one was open for 9% of the time, Pallas kernels for 13%

profile of v17, /device:TPU:0, one launch (start us, length us, event | category | flops | bytes accessed | tf_op | source)
XLA Modules:
  0.0 147.7 jit_solution(905447934191559391)
XLA Ops:
  0.6 0.8 slice.143
  1.4 1.0 slice.142
  2.9 1.3 reduce.6
  4.4 0.9 fusion.20
  5.8 0.7 copy.68
  6.7 8.2 %shard_map.113 = (bf16[9,16,384]{2,1,0:T(8,128)(2,1)}, bf16[64,9,16,128]{3,2,1,0:T(8,128)(2,1)}) custom-call(f32[9,15,8192]{2,1,0:T(8,128)} %refs_0_.1, bf16[4,8192]{1,0:T(4,128)(2,1)} %surf_ref.1), custom_call_target="tpu_custom_call" | custom-call | bytes 5529600 | tf_op jit(solution)/shard_map/pallas_call | solution.py:148
  14.8 5.2 %all-to-all-start = ((bf16[4,16,144,128]{3,2,1,0:T(8,128)(2,1)}), bf16[4,16,144,128]{3,2,1,0:T(8,128)(2,1)S(1)}, u32[]{:S(2)}, u32[]{:S(2)}) async-start(bf16[4,16,144,128]{3,2,1,0:T(8,128)(2,1)} %bitcast.150), calls=%async_computation | async-start | bytes 4718592 | tf_op jit(solution)/shard_map/all_to_all | solution.py:239
  20.0 16.2 %all-gather = bf16[72,16,384]{2,1,0:T(8,128)(2,1)S(1)} all-gather(bf16[9,16,384]{2,1,0:T(8,128)(2,1)} %get-tuple-element.16), channel_id=2, replica_groups=mesh['grp'=4,'patch'=8] {'patch'}, dimensions={0}, use_global_device_ids=true | all-gather | bytes 995328 | tf_op jit(solution)/shard_map/all_gather | solution.py:172
  36.3 0.7 fusion.26
  44.9 0.7 select_bitcast_fusion.9
  46.0 0.8 slice.219
  46.8 0.8 slice.218
  47.6 0.8 slice.217
  49.4 0.8 copy.76.refs_4_
  50.8 9.9 %shard_map.114 = (f32[9,15,8192]{2,1,0:T(8,128)}, bf16[9,16,384]{2,1,0:T(8,128)(2,1)}) custom-call(f32[9,15,8192]{2,1,0:T(8,128)} %refs_0_.1, f32[15,8192]{1,0:T(8,128)} %refs_1_.5, f32[15,8192]{1,0:T(8,128)} %refs_2_.5, bf16[9,15,256]{2,1,0:T(8,128)(2,1)} %pad_maximum_fusion.refs_3_, bf16[9,15,128]{2,1,0:T(8,128)(2,1)} %copy.76.refs_4_), custom_call_target="tpu_custom_call" | custom-call | flops 22118400 | bytes 9830400 | tf_op jit(solution)/shard_map/pallas_call | solution.py:103
  60.8 16.6 %all-gather.1 = bf16[72,16,384]{2,1,0:T(8,128)(2,1)S(1)} all-gather(bf16[9,16,384]{2,1,0:T(8,128)(2,1)} %get-tuple-element.19), channel_id=3, replica_groups=mesh['grp'=4,'patch'=8] {'patch'}, dimensions={0}, use_global_device_ids=true | all-gather | bytes 995328 | tf_op jit(solution)/shard_map/all_gather | solution.py:172
  77.3 0.7 select_bitcast_fusion.5
  78.3 3.7 %multiply_convert_fusion.2 = bf16[16,128,256]{2,1,0:T(8,128)(2,1)} fusion(f32[256]{0:T(256)S(1)} %bitcast.171, bf16[4,16,144,128]{3,2,1,0:T(8,128)(2,1)S(1)} %all-to-all-done, f32[256]{0:T(256)S(1)} %bitcast.172, bf16[4,144,256]{2,1,0:T(8,128)(2,1)S(1)} %bitcast.163, bf16[3,256,256]{2,1,0:T(8,128)(2,1)} %param.18), kind=kOutput, calls=%fused_computation.4 | convolution fusion | flops 878706688 | bytes 3835904 | tf_op jit(solution)/shard_map/...h,hj->...j/dot_general | solution.py:194
  82.1 2.6 %multiply_convert_fusion = bf16[16,128,256]{2,1,0:T(8,128)(2,1)S(1)} fusion(f32[256]{0:T(256)S(1)} %bitcast.170, bf16[16,128,256]{2,1,0:T(8,128)(2,1)} %multiply_convert_fusion.2, f32[256]{0:T(256)S(1)} %bitcast.169, bf16[3,256,256]{2,1,0:T(8,128)(2,1)} %param.18), kind=kOutput, calls=%fused_computation.2 | convolution fusion | flops 543162368 | bytes 2361344 | tf_op jit(solution)/shard_map/...h,hj->...j/dot_general | solution.py:194
  84.6 2.3 %convolution_convert_fusion = bf16[576,2048]{1,0:T(8,128)(2,1)} fusion(bf16[576,256]{1,0:T(8,128)(2,1)S(1)} %bitcast.154, bf16[2048,256]{1,0:T(8,128)(2,1)S(1)} %bitcast.159), kind=kOutput, calls=%fused_computation | convolution fusion | flops 605159424 | bytes 3702784 | tf_op jit(solution)/shard_map/dot_general | solution.py:246
  86.9 1.0 convert_reduce_fusion
  87.9 0.8 fusion.13
  88.6 5.3 %all-to-all-start.2 = ((f32[8,4,128]{2,1,0:T(4,128)}), f32[8,4,128]{2,1,0:T(4,128)S(1)}, u32[]{:S(2)}, u32[]{:S(2)}) async-start(f32[8,4,128]{2,1,0:T(4,128)} %fusion.13), calls=%async_computation.2 | async-start | bytes 32768 | tf_op jit(solution)/shard_map/all_to_all | solution.py:257
  94.0 0.8 slice.228
  95.0 4.6 %all-to-all-done.2 = f32[8,4,128]{2,1,0:T(4,128)S(1)} async-done(((f32[8,4,128]{2,1,0:T(4,128)}), f32[8,4,128]{2,1,0:T(4,128)S(1)}, u32[]{:S(2)}, u32[]{:S(2)}) %all-to-all-start.2) | async-done | bytes 16416 | tf_op jit(solution)/shard_map/all_to_all | solution.py:257
  99.6 4.2 %all-to-all-start.1 = ((bf16[4,9,16,2048]{3,2,1,0:T(8,128)(2,1)}), bf16[4,9,16,2048]{3,2,1,0:T(8,128)(2,1)S(1)}, u32[]{:S(2)}, u32[]{:S(2)}) async-start(bf16[4,9,16,2048]{3,2,1,0:T(8,128)(2,1)} %bitcast.72), calls=%async_computation.1 | async-start | bytes 4718592 | tf_op jit(solution)/shard_map/all_to_all | solution.py:250
  104.8 0.8 copy.83.refs_4_
  106.2 9.9 %shard_map.115 = (f32[9,15,8192]{2,1,0:T(8,128)}, bf16[9,16,384]{2,1,0:T(8,128)(2,1)}) custom-call(f32[9,15,8192]{2,1,0:T(8,128)} %get-tuple-element.18.refs_0_, f32[15,8192]{1,0:T(8,128)} %refs_1_.5, f32[15,8192]{1,0:T(8,128)} %refs_2_.5, bf16[9,15,256]{2,1,0:T(8,128)(2,1)} %pad_maximum_fusion.2.refs_3_, bf16[9,15,128]{2,1,0:T(8,128)(2,1)} %copy.83.refs_4_), custom_call_target="tpu_custom_call" | custom-call | flops 22118400 | bytes 9830400 | tf_op jit(solution)/shard_map/pallas_call | solution.py:103
  116.2 16.1 %all-gather.2 = bf16[72,16,384]{2,1,0:T(8,128)(2,1)S(1)} all-gather(bf16[9,16,384]{2,1,0:T(8,128)(2,1)} %get-tuple-element.21), channel_id=4, replica_groups=mesh['grp'=4,'patch'=8] {'patch'}, dimensions={0}, use_global_device_ids=true | all-gather | bytes 995328 | tf_op jit(solution)/shard_map/all_gather | solution.py:172
  133.9 0.8 copy.91.refs_4_
  135.3 1.4 copy-done
  136.7 10.4 %shard_map.116 = (f32[9,15,8192]{2,1,0:T(8,128)}, bf16[9,16,384]{2,1,0:T(8,128)(2,1)}) custom-call(f32[9,15,8192]{2,1,0:T(8,128)} %get-tuple-element.20.refs_0_, f32[15,8192]{1,0:T(8,128)} %refs_1_.5, f32[15,8192]{1,0:T(8,128)} %refs_2_.5, bf16[9,15,256]{2,1,0:T(8,128)(2,1)} %pad_maximum_fusion.4.refs_3_, bf16[9,15,128]{2,1,0:T(8,128)(2,1)} %copy.91.refs_4_, ...), custom_call_target="tpu_custom_call" | custom-call | flops 22118400 | bytes 9830400 | tf_op jit(solution)/shard_map/pallas_call | solution.py:103
  (75 shorter events, 8.0 us)
Async XLA Ops:
  0.6 5.9 %copy-start.2 = (bf16[256,540]{0,1:T(8,128)(2,1)S(1)}, bf16[256,540]{0,1:T(8,128)(2,1)}, u32[]{:S(2)}) copy-start(bf16[256,540]{0,1:T(8,128)(2,1)} %param.19) | copy-start | bytes 829444
  14.8 63.5 %all-to-all-start = ((bf16[4,16,144,128]{3,2,1,0:T(8,128)(2,1)}), bf16[4,16,144,128]{3,2,1,0:T(8,128)(2,1)S(1)}, u32[]{:S(2)}, u32[]{:S(2)}) async-start(bf16[4,16,144,128]{3,2,1,0:T(8,128)(2,1)} %bitcast.150), calls=%async_computation | async-start | bytes 4718592 | tf_op jit(solution)/shard_map/all_to_all | solution.py:239
  60.7 17.5 %copy-start.3 = (f32[4,256]{1,0:T(4,128)S(1)}, f32[4,256]{1,0:T(4,128)}, u32[]{:S(2)}) copy-start(f32[4,256]{1,0:T(4,128)} %param.17) | copy-start | bytes 12292
  60.8 17.6 %copy-start.1 = (bf16[4,9,16,256]{3,2,1,0:T(8,128)(2,1)S(1)}, bf16[4,9,16,256]{3,2,1,0:T(8,128)(2,1)}, u32[]{:S(2)}) copy-start(bf16[4,9,16,256]{3,2,1,0:T(8,128)(2,1)} %copy.68) | copy-start | bytes 884740
  88.6 11.0 %all-to-all-start.2 = ((f32[8,4,128]{2,1,0:T(4,128)}), f32[8,4,128]{2,1,0:T(4,128)S(1)}, u32[]{:S(2)}, u32[]{:S(2)}) async-start(f32[8,4,128]{2,1,0:T(4,128)} %fusion.13), calls=%async_computation.2 | async-start | bytes 32768 | tf_op jit(solution)/shard_map/all_to_all | solution.py:257
  99.6 35.7 %all-to-all-start.1 = ((bf16[4,9,16,2048]{3,2,1,0:T(8,128)(2,1)}), bf16[4,9,16,2048]{3,2,1,0:T(8,128)(2,1)S(1)}, u32[]{:S(2)}, u32[]{:S(2)}) async-start(bf16[4,9,16,2048]{3,2,1,0:T(8,128)(2,1)} %bitcast.72), calls=%async_computation.1 | async-start | bytes 4718592 | tf_op jit(solution)/shard_map/all_to_all | solution.py:250
  135.3 1.4 copy-start
